TPU v7x, 256 devices: a whole 4x4x8 slice. The times are simulated.
256 devices in a mesh: stream: 8 (over y, core), seq: 32 (over x, z).
Axes of the slice: x: 4, y: 4, z: 8, core: 2. Of those that a mesh axis runs over, the one named last changes fastest.
Arguments:
- inner_x: bfloat16 [32768, 4096], P(('stream', 'seq')), parts along dimension 0, may hold values from -6 to 6
- inner_gate: bfloat16 [32768, 4096], P(('stream', 'seq')), parts along dimension 0, may hold values from -6 to 6
- conv_weight: float32 [4, 4096], replicated, may hold values from -3 to 3
- conv_bias: float32 [4096], replicated, may hold values from -3 to 3
- step_low: bfloat16 [32768, 256], P(('stream', 'seq')), parts along dimension 0, may hold values from -5 to 48
- step_proj: bfloat16 [256, 4096], replicated, may hold values from -1 to 2
- step_bias: float32 [4096], replicated, may hold values from -4.5 to -3.5
- decay_log: float32 [16, 4096], replicated, may hold values from -12 to 2
- state_in: float32 [32768, 16], P(('stream', 'seq')), parts along dimension 0, may hold values from -8 to 8
- state_out: float32 [32768, 16], P(('stream', 'seq')), parts along dimension 0, may hold values from -1.5 to 1.5
- skip_gain: float32 [4096], replicated, may hold values from 0.5 to 1.5
- query_heads: bfloat16 [32768, 4096], P(('stream', 'seq')), parts along dimension 0, may hold values from -6 to 6
- key_heads: bfloat16 [32768, 1024], P(('stream', 'seq')), parts along dimension 0, may hold values from -6 to 6
- value_heads: bfloat16 [32768, 1024], P(('stream', 'seq')), parts along dimension 0, may hold values from -6 to 6
Outputs:
- mamba_out: bfloat16 [32768, 4096], P(('stream', 'seq')), parts along dimension 0
- attention_out: bfloat16 [32768, 4096], P(('stream', 'seq')), parts along dimension 0
There are 8 independent parts, one for each index of `stream`. A program takes and returns all parts, laid end to end along the dimension named above; an argument that names none is the same for every part. Nothing has to cross between parts.
All inputs are finite; a program needn't handle non-finite values.
Results may differ from a plain program's by a relative error of at most 0.007.
Values may be sent and summed in bfloat16 or wider, within the bound.
No kernel may reach another device: no remote copies, remote signals or barrier semaphores. Data moves between devices by JAX's collectives and lax.ppermute only.
A program may use at most 128 MiB of HBM per device.

v0:
```python
import math

import jax
import jax.numpy as jnp
from jax import lax
from jax.sharding import PartitionSpec as P

HEAD_DIM = 128


def shifted(block, axis, distance):
    devices = range(lax.axis_size(axis))
    route = [(i - distance, i) for i in devices if i - distance in devices]
    return lax.ppermute(block, axis, route)


def convolve(padded, conv_weight, conv_bias):
    reach = conv_weight.shape[0] - 1
    length = padded.shape[0] - reach
    total = jnp.zeros((length, padded.shape[1]), jnp.float32)
    for index in range(reach + 1):
        total = total + conv_weight[index][None, :] * padded[index : index + length].astype(
            jnp.float32
        )
    return jax.nn.silu(total + conv_bias[None, :])


def attend_by_heads(q_three, k_three, v_three):
    tokens = q_three.shape[0]
    group = q_three.shape[1] // k_three.shape[1]
    k_wide = jnp.repeat(k_three, group, axis=1)
    v_wide = jnp.repeat(v_three, group, axis=1)
    q_all, k_all, v_all = (
        lax.all_to_all(q_three, "seq", split_axis=1, concat_axis=0, tiled=True),
        lax.all_to_all(k_wide, "seq", split_axis=1, concat_axis=0, tiled=True),
        lax.all_to_all(v_wide, "seq", split_axis=1, concat_axis=0, tiled=True),
    )
    length = q_all.shape[0]
    width = math.gcd(length, 512)
    scale = HEAD_DIM ** (-0.5)
    columns = jnp.arange(length)

    def block(index):
        start = index * width
        query_block = lax.dynamic_slice_in_dim(q_all, start, width, 0)
        scores = (
            jnp.einsum("ihd,jhd->hij", query_block, k_all, preferred_element_type=jnp.float32)
            * scale
        )
        rows = start + jnp.arange(width)
        allowed = rows[:, None] >= columns[None, :]
        masked = jnp.where(allowed[None], scores, -1e30)
        peak = jnp.max(masked, axis=-1, keepdims=True)
        expo = jnp.where(allowed[None], jnp.exp(masked - peak), 0.0)
        total = jnp.sum(expo, axis=-1)
        summed = jnp.einsum(
            "hij,jhd->ihd", expo.astype(jnp.bfloat16), v_all, preferred_element_type=jnp.float32
        )
        return (summed / jnp.transpose(total)[:, :, None]).astype(jnp.bfloat16)

    blocks = lax.map(block, jnp.arange(length // width))
    merged = blocks.reshape(length, q_all.shape[1], HEAD_DIM)
    back = lax.all_to_all(merged, "seq", split_axis=0, concat_axis=1, tiled=True)
    return back.reshape(tokens, -1)


def per_device(
    inner_x,
    inner_gate,
    conv_weight,
    conv_bias,
    step_low,
    step_proj,
    step_bias,
    decay_log,
    state_in,
    state_out,
    skip_gain,
    query_heads,
    key_heads,
    value_heads,
):
    reach = conv_weight.shape[0] - 1
    rim = shifted(inner_x[-reach:], "seq", 1)
    conv = convolve(jnp.concatenate([rim, inner_x], 0), conv_weight, conv_bias)
    step = jax.nn.softplus(
        jnp.dot(step_low, step_proj, preferred_element_type=jnp.float32) + step_bias[None, :]
    )
    rate = -jnp.exp(decay_log)

    def carry_only(state, row):
        step_row, conv_row, in_row = row
        state = (
            jnp.exp(step_row[None, :] * rate) * state
            + (step_row * conv_row)[None, :] * in_row[:, None]
        )
        return (state, None)

    def with_read(state, row):
        step_row, conv_row, in_row, out_row = row
        state = (
            jnp.exp(step_row[None, :] * rate) * state
            + (step_row * conv_row)[None, :] * in_row[:, None]
        )
        return (state, jnp.sum(out_row[:, None] * state, axis=0))

    zero_state = jnp.zeros(rate.shape, jnp.float32)
    local_end, unused = lax.scan(carry_only, zero_state, (step, conv, state_in), unroll=8)
    decay_total = jnp.exp(rate * jnp.sum(step, axis=0)[None, :])

    def hop(index, incoming):
        leaving = decay_total * incoming + local_end
        return shifted(leaving, "seq", 1)

    incoming = lax.fori_loop(0, lax.axis_size("seq") - 1, hop, zero_state)
    final, read = lax.scan(with_read, incoming, (step, conv, state_in, state_out), unroll=8)
    mamba_out = (
        (read + skip_gain[None, :] * conv) * jax.nn.silu(inner_gate.astype(jnp.float32))
    ).astype(jnp.bfloat16)
    tokens = query_heads.shape[0]
    q_three = query_heads.reshape(tokens, -1, HEAD_DIM)
    k_three = key_heads.reshape(tokens, -1, HEAD_DIM)
    v_three = value_heads.reshape(tokens, -1, HEAD_DIM)
    attention_out = attend_by_heads(q_three, k_three, v_three)
    return (mamba_out, attention_out)


def solution(mesh):
    in_specs = (
        P(("stream", "seq"), None),
        P(("stream", "seq"), None),
        P(),
        P(),
        P(("stream", "seq"), None),
        P(),
        P(),
        P(),
        P(("stream", "seq"), None),
        P(("stream", "seq"), None),
        P(),
        P(("stream", "seq"), None),
        P(("stream", "seq"), None),
        P(("stream", "seq"), None),
    )
    out_specs = (P(("stream", "seq"), None), P(("stream", "seq"), None))
    return jax.shard_map(
        per_device, mesh=mesh, in_specs=in_specs, out_specs=out_specs, check_vma=False
    )
```

profile of v0, /device:TPU:14, one launch (start us, length us, event | category | flops | bytes accessed | tf_op | source)
XLA Modules:
  0.0 694.2 jit_solution(9020401438548626143)
XLA Ops:
  3.0 11.8 %all-to-all-start.2 = ((bf16[128,32,128]{2,0,1:T(8,128)(2,1)}), bf16[128,32,128]{2,0,1:T(8,128)(2,1)}, u32[]{:S(2)}, u32[]{:S(2)}) async-start(bf16[128,32,128]{2,0,1:T(8,128)(2,1)} %bitcast.58), calls=%async_computation.2 | async-start | bytes 2097152 | tf_op jit(solution)/shard_map/all_to_all | solution.py:36
  24.0 17.9 %all-to-all-done.2 = bf16[128,32,128]{2,0,1:T(8,128)(2,1)} async-done(((bf16[128,32,128]{2,0,1:T(8,128)(2,1)}), bf16[128,32,128]{2,0,1:T(8,128)(2,1)}, u32[]{:S(2)}, u32[]{:S(2)}) %all-to-all-start.2) | async-done | bytes 1048608 | tf_op jit(solution)/shard_map/all_to_all | solution.py:36
  41.9 6.9 all-to-all-start
  49.2 5.2 divide_multiply_fusion
  54.4 20.3 %all-to-all-done = bf16[128,32,128]{0,2,1:T(8,128)(2,1)} async-done(((bf16[128,32,128]{0,2,1:T(8,128)(2,1)}), bf16[128,32,128]{0,2,1:T(8,128)(2,1)}, u32[]{:S(2)}, u32[]{:S(2)}) %all-to-all-start) | async-done | bytes 1048608 | tf_op jit(solution)/shard_map/all_to_all | solution.py:34
  75.9 7.2 %all-to-all-start.1 = ((bf16[128,32,128]{2,0,1:T(8,128)(2,1)}), bf16[128,32,128]{2,0,1:T(8,128)(2,1)}, u32[]{:S(2)}, u32[]{:S(2)}) async-start(bf16[128,32,128]{2,0,1:T(8,128)(2,1)} %bitcast.291), calls=%async_computation.1 | async-start | bytes 2097152 | tf_op jit(solution)/shard_map/all_to_all | solution.py:35
  83.1 47.8 %while.47 = (s32[]{:T(128)}, f32[16,4096]{1,0:T(8,128)S(1)}, f32[16,8,4096]{2,1,0:T(8,128)}, f32[16,4096]{1,0:T(8,128)S(1)}, f32[16,8,4096]{2,1,0:T(8,128)}, /*i...) while((s32[]{:T(128)}, f32[16,4096]{1,0:T(8,128)S(1)}, ...), condition=%wide.region_2.3_spmd.clone, body=%wide.region_1.2_spmd.clone.sunk | while | flops 2195466 | bytes 1968919 | solution.py:108
  133.2 90.4 %while.46 = (s32[]{:T(128)}, bf16[8,512,1,128]{3,1,2,0:T(8,128)(2,1)}, s32[8]{0:T(128)S(1)}, bf16[4096,1,128]{2,0,1:T(8,128)(2,1)}, bf16[4096,1,128]{2,0,1:T(8,1...) while((s32[]{:T(128)}, ...), condition=%wide.region_18.19_spmd.clone, body=%wide.region_15.18_spmd.clone.sunk | while | flops 1107426816 | bytes 27543732 | solution.py:61
  140.3 4.2 fusion.71
  162.9 4.2 fusion.71
  174.2 4.2 fusion.71
  185.5 4.2 fusion.71
  229.6 9.8 %all-to-all-start.3 = ((bf16[32,2,8192]{2,1,0:T(2,128)(2,1)}), bf16[32,2,8192]{2,1,0:T(2,128)(2,1)}, u32[]{:S(2)}, u32[]{:S(2)}) async-start(bf16[32,2,8192]{2,1,0:T(2,128)(2,1)} %reshape.395), calls=%async_computation.3 | async-start | bytes 2097152 | tf_op jit(solution)/shard_map/all_to_all | solution.py:63
  239.4 365.6 %while.44 = (s32[]{:T(128)}, f32[16,4096]{1,0:T(8,128)S(1)}, f32[16,4096]{1,0:T(8,128)S(1)}, f32[16,4096]{1,0:T(8,128)S(1)}, s32[]{:T(128)}) while((s32[]{:T(128)}, f32[16,4096]{1,0:T(8,128)S(1)}, f32[16,4096]{1,0:T(8,128)S(1)}, f32[16,4096]{1,0:T(8,128)S(1)}, s32[]{:T(128)}) %tuple.173), condition=%wide.region_4.5_spmd, body=%wide.region_3.4_spmd.sunk | while | flops 131074 | bytes 2097253 | solution.py:115
  242.9 26.6 %collective-permute-done = f32[16,4096]{1,0:T(8,128)S(1)} collective-permute-done((f32[16,4096]{1,0:T(8,128)S(1)}, f32[16,4096]{1,0:T(8,128)S(1)}, u32[]{:S(2)}, u32[]{:S(2)}) %collective-permute-start) | collective-permute-done | bytes 262176 | tf_op jit(solution)/shard_map/while/body/eval_jaxpr/ppermute | solution.py:14
  271.5 9.2 %collective-permute-done = f32[16,4096]{1,0:T(8,128)S(1)} collective-permute-done((f32[16,4096]{1,0:T(8,128)S(1)}, f32[16,4096]{1,0:T(8,128)S(1)}, u32[]{:S(2)}, u32[]{:S(2)}) %collective-permute-start) | collective-permute-done | bytes 262176 | tf_op jit(solution)/shard_map/while/body/eval_jaxpr/ppermute | solution.py:14
  282.7 8.4 %collective-permute-done = f32[16,4096]{1,0:T(8,128)S(1)} collective-permute-done((f32[16,4096]{1,0:T(8,128)S(1)}, f32[16,4096]{1,0:T(8,128)S(1)}, u32[]{:S(2)}, u32[]{:S(2)}) %collective-permute-start) | collective-permute-done | bytes 262176 | tf_op jit(solution)/shard_map/while/body/eval_jaxpr/ppermute | solution.py:14
  293.1 8.4 %collective-permute-done = f32[16,4096]{1,0:T(8,128)S(1)} collective-permute-done((f32[16,4096]{1,0:T(8,128)S(1)}, f32[16,4096]{1,0:T(8,128)S(1)}, u32[]{:S(2)}, u32[]{:S(2)}) %collective-permute-start) | collective-permute-done | bytes 262176 | tf_op jit(solution)/shard_map/while/body/eval_jaxpr/ppermute | solution.py:14
  303.5 8.4 %collective-permute-done = f32[16,4096]{1,0:T(8,128)S(1)} collective-permute-done((f32[16,4096]{1,0:T(8,128)S(1)}, f32[16,4096]{1,0:T(8,128)S(1)}, u32[]{:S(2)}, u32[]{:S(2)}) %collective-permute-start) | collective-permute-done | bytes 262176 | tf_op jit(solution)/shard_map/while/body/eval_jaxpr/ppermute | solution.py:14
  313.9 8.4 %collective-permute-done = f32[16,4096]{1,0:T(8,128)S(1)} collective-permute-done((f32[16,4096]{1,0:T(8,128)S(1)}, f32[16,4096]{1,0:T(8,128)S(1)}, u32[]{:S(2)}, u32[]{:S(2)}) %collective-permute-start) | collective-permute-done | bytes 262176 | tf_op jit(solution)/shard_map/while/body/eval_jaxpr/ppermute | solution.py:14
  324.4 9.5 %collective-permute-done = f32[16,4096]{1,0:T(8,128)S(1)} collective-permute-done((f32[16,4096]{1,0:T(8,128)S(1)}, f32[16,4096]{1,0:T(8,128)S(1)}, u32[]{:S(2)}, u32[]{:S(2)}) %collective-permute-start) | collective-permute-done | bytes 262176 | tf_op jit(solution)/shard_map/while/body/eval_jaxpr/ppermute | solution.py:14
  335.8 10.6 %collective-permute-done = f32[16,4096]{1,0:T(8,128)S(1)} collective-permute-done((f32[16,4096]{1,0:T(8,128)S(1)}, f32[16,4096]{1,0:T(8,128)S(1)}, u32[]{:S(2)}, u32[]{:S(2)}) %collective-permute-start) | collective-permute-done | bytes 262176 | tf_op jit(solution)/shard_map/while/body/eval_jaxpr/ppermute | solution.py:14
  348.4 10.7 %collective-permute-done = f32[16,4096]{1,0:T(8,128)S(1)} collective-permute-done((f32[16,4096]{1,0:T(8,128)S(1)}, f32[16,4096]{1,0:T(8,128)S(1)}, u32[]{:S(2)}, u32[]{:S(2)}) %collective-permute-start) | collective-permute-done | bytes 262176 | tf_op jit(solution)/shard_map/while/body/eval_jaxpr/ppermute | solution.py:14
  361.1 9.9 %collective-permute-done = f32[16,4096]{1,0:T(8,128)S(1)} collective-permute-done((f32[16,4096]{1,0:T(8,128)S(1)}, f32[16,4096]{1,0:T(8,128)S(1)}, u32[]{:S(2)}, u32[]{:S(2)}) %collective-permute-start) | collective-permute-done | bytes 262176 | tf_op jit(solution)/shard_map/while/body/eval_jaxpr/ppermute | solution.py:14
  373.0 9.0 %collective-permute-done = f32[16,4096]{1,0:T(8,128)S(1)} collective-permute-done((f32[16,4096]{1,0:T(8,128)S(1)}, f32[16,4096]{1,0:T(8,128)S(1)}, u32[]{:S(2)}, u32[]{:S(2)}) %collective-permute-start) | collective-permute-done | bytes 262176 | tf_op jit(solution)/shard_map/while/body/eval_jaxpr/ppermute | solution.py:14
  384.0 8.4 %collective-permute-done = f32[16,4096]{1,0:T(8,128)S(1)} collective-permute-done((f32[16,4096]{1,0:T(8,128)S(1)}, f32[16,4096]{1,0:T(8,128)S(1)}, u32[]{:S(2)}, u32[]{:S(2)}) %collective-permute-start) | collective-permute-done | bytes 262176 | tf_op jit(solution)/shard_map/while/body/eval_jaxpr/ppermute | solution.py:14
  394.4 8.4 %collective-permute-done = f32[16,4096]{1,0:T(8,128)S(1)} collective-permute-done((f32[16,4096]{1,0:T(8,128)S(1)}, f32[16,4096]{1,0:T(8,128)S(1)}, u32[]{:S(2)}, u32[]{:S(2)}) %collective-permute-start) | collective-permute-done | bytes 262176 | tf_op jit(solution)/shard_map/while/body/eval_jaxpr/ppermute | solution.py:14
  404.8 8.4 %collective-permute-done = f32[16,4096]{1,0:T(8,128)S(1)} collective-permute-done((f32[16,4096]{1,0:T(8,128)S(1)}, f32[16,4096]{1,0:T(8,128)S(1)}, u32[]{:S(2)}, u32[]{:S(2)}) %collective-permute-start) | collective-permute-done | bytes 262176 | tf_op jit(solution)/shard_map/while/body/eval_jaxpr/ppermute | solution.py:14
  415.2 8.5 %collective-permute-done = f32[16,4096]{1,0:T(8,128)S(1)} collective-permute-done((f32[16,4096]{1,0:T(8,128)S(1)}, f32[16,4096]{1,0:T(8,128)S(1)}, u32[]{:S(2)}, u32[]{:S(2)}) %collective-permute-start) | collective-permute-done | bytes 262176 | tf_op jit(solution)/shard_map/while/body/eval_jaxpr/ppermute | solution.py:14
  425.7 9.7 %collective-permute-done = f32[16,4096]{1,0:T(8,128)S(1)} collective-permute-done((f32[16,4096]{1,0:T(8,128)S(1)}, f32[16,4096]{1,0:T(8,128)S(1)}, u32[]{:S(2)}, u32[]{:S(2)}) %collective-permute-start) | collective-permute-done | bytes 262176 | tf_op jit(solution)/shard_map/while/body/eval_jaxpr/ppermute | solution.py:14
  437.3 10.8 %collective-permute-done = f32[16,4096]{1,0:T(8,128)S(1)} collective-permute-done((f32[16,4096]{1,0:T(8,128)S(1)}, f32[16,4096]{1,0:T(8,128)S(1)}, u32[]{:S(2)}, u32[]{:S(2)}) %collective-permute-start) | collective-permute-done | bytes 262176 | tf_op jit(solution)/shard_map/while/body/eval_jaxpr/ppermute | solution.py:14
  450.1 10.5 %collective-permute-done = f32[16,4096]{1,0:T(8,128)S(1)} collective-permute-done((f32[16,4096]{1,0:T(8,128)S(1)}, f32[16,4096]{1,0:T(8,128)S(1)}, u32[]{:S(2)}, u32[]{:S(2)}) %collective-permute-start) | collective-permute-done | bytes 262176 | tf_op jit(solution)/shard_map/while/body/eval_jaxpr/ppermute | solution.py:14
  462.6 9.7 %collective-permute-done = f32[16,4096]{1,0:T(8,128)S(1)} collective-permute-done((f32[16,4096]{1,0:T(8,128)S(1)}, f32[16,4096]{1,0:T(8,128)S(1)}, u32[]{:S(2)}, u32[]{:S(2)}) %collective-permute-start) | collective-permute-done | bytes 262176 | tf_op jit(solution)/shard_map/while/body/eval_jaxpr/ppermute | solution.py:14
  474.3 8.8 %collective-permute-done = f32[16,4096]{1,0:T(8,128)S(1)} collective-permute-done((f32[16,4096]{1,0:T(8,128)S(1)}, f32[16,4096]{1,0:T(8,128)S(1)}, u32[]{:S(2)}, u32[]{:S(2)}) %collective-permute-start) | collective-permute-done | bytes 262176 | tf_op jit(solution)/shard_map/while/body/eval_jaxpr/ppermute | solution.py:14
  485.1 8.4 %collective-permute-done = f32[16,4096]{1,0:T(8,128)S(1)} collective-permute-done((f32[16,4096]{1,0:T(8,128)S(1)}, f32[16,4096]{1,0:T(8,128)S(1)}, u32[]{:S(2)}, u32[]{:S(2)}) %collective-permute-start) | collective-permute-done | bytes 262176 | tf_op jit(solution)/shard_map/while/body/eval_jaxpr/ppermute | solution.py:14
  495.5 8.4 %collective-permute-done = f32[16,4096]{1,0:T(8,128)S(1)} collective-permute-done((f32[16,4096]{1,0:T(8,128)S(1)}, f32[16,4096]{1,0:T(8,128)S(1)}, u32[]{:S(2)}, u32[]{:S(2)}) %collective-permute-start) | collective-permute-done | bytes 262176 | tf_op jit(solution)/shard_map/while/body/eval_jaxpr/ppermute | solution.py:14
  505.9 8.4 %collective-permute-done = f32[16,4096]{1,0:T(8,128)S(1)} collective-permute-done((f32[16,4096]{1,0:T(8,128)S(1)}, f32[16,4096]{1,0:T(8,128)S(1)}, u32[]{:S(2)}, u32[]{:S(2)}) %collective-permute-start) | collective-permute-done | bytes 262176 | tf_op jit(solution)/shard_map/while/body/eval_jaxpr/ppermute | solution.py:14
  516.4 8.7 %collective-permute-done = f32[16,4096]{1,0:T(8,128)S(1)} collective-permute-done((f32[16,4096]{1,0:T(8,128)S(1)}, f32[16,4096]{1,0:T(8,128)S(1)}, u32[]{:S(2)}, u32[]{:S(2)}) %collective-permute-start) | collective-permute-done | bytes 262176 | tf_op jit(solution)/shard_map/while/body/eval_jaxpr/ppermute | solution.py:14
  527.0 9.8 %collective-permute-done = f32[16,4096]{1,0:T(8,128)S(1)} collective-permute-done((f32[16,4096]{1,0:T(8,128)S(1)}, f32[16,4096]{1,0:T(8,128)S(1)}, u32[]{:S(2)}, u32[]{:S(2)}) %collective-permute-start) | collective-permute-done | bytes 262176 | tf_op jit(solution)/shard_map/while/body/eval_jaxpr/ppermute | solution.py:14
  538.9 11.0 %collective-permute-done = f32[16,4096]{1,0:T(8,128)S(1)} collective-permute-done((f32[16,4096]{1,0:T(8,128)S(1)}, f32[16,4096]{1,0:T(8,128)S(1)}, u32[]{:S(2)}, u32[]{:S(2)}) %collective-permute-start) | collective-permute-done | bytes 262176 | tf_op jit(solution)/shard_map/while/body/eval_jaxpr/ppermute | solution.py:14
  551.8 10.4 %collective-permute-done = f32[16,4096]{1,0:T(8,128)S(1)} collective-permute-done((f32[16,4096]{1,0:T(8,128)S(1)}, f32[16,4096]{1,0:T(8,128)S(1)}, u32[]{:S(2)}, u32[]{:S(2)}) %collective-permute-start) | collective-permute-done | bytes 262176 | tf_op jit(solution)/shard_map/while/body/eval_jaxpr/ppermute | solution.py:14
  564.2 9.5 %collective-permute-done = f32[16,4096]{1,0:T(8,128)S(1)} collective-permute-done((f32[16,4096]{1,0:T(8,128)S(1)}, f32[16,4096]{1,0:T(8,128)S(1)}, u32[]{:S(2)}, u32[]{:S(2)}) %collective-permute-start) | collective-permute-done | bytes 262176 | tf_op jit(solution)/shard_map/while/body/eval_jaxpr/ppermute | solution.py:14
  575.7 8.4 %collective-permute-done = f32[16,4096]{1,0:T(8,128)S(1)} collective-permute-done((f32[16,4096]{1,0:T(8,128)S(1)}, f32[16,4096]{1,0:T(8,128)S(1)}, u32[]{:S(2)}, u32[]{:S(2)}) %collective-permute-start) | collective-permute-done | bytes 262176 | tf_op jit(solution)/shard_map/while/body/eval_jaxpr/ppermute | solution.py:14
  586.1 8.4 %collective-permute-done = f32[16,4096]{1,0:T(8,128)S(1)} collective-permute-done((f32[16,4096]{1,0:T(8,128)S(1)}, f32[16,4096]{1,0:T(8,128)S(1)}, u32[]{:S(2)}, u32[]{:S(2)}) %collective-permute-start) | collective-permute-done | bytes 262176 | tf_op jit(solution)/shard_map/while/body/eval_jaxpr/ppermute | solution.py:14
  596.6 8.4 %collective-permute-done = f32[16,4096]{1,0:T(8,128)S(1)} collective-permute-done((f32[16,4096]{1,0:T(8,128)S(1)}, f32[16,4096]{1,0:T(8,128)S(1)}, u32[]{:S(2)}, u32[]{:S(2)}) %collective-permute-start) | collective-permute-done | bytes 262176 | tf_op jit(solution)/shard_map/while/body/eval_jaxpr/ppermute | solution.py:14
  605.0 74.0 %while.45 = (s32[]{:T(128)}, f32[16,4096]{1,0:T(8,128)S(1)}, f32[16,8,4096]{2,1,0:T(8,128)}, f32[16,8,4096]{2,1,0:T(8,128)}, f32[16,4096]{1,0:T(8,128)S(1)}, /*i...) while((s32[]{:T(128)}, f32[16,4096]{1,0:T(8,128)S(1)}, ...), condition=%wide.region_14.15_spmd, body=%wide.region_5.14_spmd.sunk | while | flops 4718601 | bytes 4134561 | solution.py:116
  679.0 4.2 fusion.52
  683.2 5.7 reshape.396
  (611 shorter events, 275.6 us)
Async XLA Ops:
  0.6 20.4 %copy-start = (bf16[256,4096]{1,0:T(8,128)(2,1)S(1)}, bf16[256,4096]{1,0:T(8,128)(2,1)}, u32[]{:S(2)}) copy-start(bf16[256,4096]{1,0:T(8,128)(2,1)} %param.27) | copy-start | bytes 6291460
  0.6 19.0 %copy-start.1 = (bf16[128,4096]{1,0:T(8,128)(2,1)S(1)}, bf16[128,4096]{1,0:T(8,128)(2,1)}, u32[]{:S(2)}) copy-start(bf16[128,4096]{1,0:T(8,128)(2,1)} %param.33) | copy-start | bytes 3145732
  3.0 18.0 %copy-start.9 = (bf16[128,256]{1,0:T(8,128)(2,1)S(1)}, bf16[128,256]{1,0:T(8,128)(2,1)}, u32[]{:S(2)}) copy-start(bf16[128,256]{1,0:T(8,128)(2,1)} %param.26) | copy-start | bytes 196612
  3.0 18.0 %copy-start.10 = (f32[4096]{0:T(1024)S(1)}, f32[4096]{0:T(1024)}, u32[]{:S(2)}) copy-start(f32[4096]{0:T(1024)} %param.28) | copy-start | bytes 49156
  3.0 38.9 %all-to-all-start.2 = ((bf16[128,32,128]{2,0,1:T(8,128)(2,1)}), bf16[128,32,128]{2,0,1:T(8,128)(2,1)}, u32[]{:S(2)}, u32[]{:S(2)}) async-start(bf16[128,32,128]{2,0,1:T(8,128)(2,1)} %bitcast.58), calls=%async_computation.2 | async-start | bytes 2097152 | tf_op jit(solution)/shard_map/all_to_all | solution.py:36
  16.3 32.9 %collective-permute-start.1 = (bf16[3,4096]{1,0:T(4,128)(2,1)}, bf16[3,4096]{1,0:T(4,128)(2,1)}, u32[]{:S(2)}, u32[]{:S(2)}) collective-permute-start(bf16[3,4096]{1,0:T(4,128)(2,1)} %slice.249), channel_id=1, source_target_pairs={{0,1},{1,2},{2,3},{3,4},{4,5},{5,6},{6,7},{7,8},{8,9},{9,10},{10,1... | collective-permute-start | bytes 73736 | tf_op jit(solution)/shard_map/ppermute | solution.py:14
  21.0 2.9 copy-start.2
  23.9 24.9 %copy-start.4 = (f32[4,4096]{1,0:T(4,128)S(1)}, f32[4,4096]{1,0:T(4,128)}, u32[]{:S(2)}) copy-start(f32[4,4096]{1,0:T(4,128)} %param.24) | copy-start | bytes 196612
  23.9 25.0 %copy-start.3 = (bf16[128,1024]{1,0:T(8,128)(2,1)S(1)}, bf16[128,1024]{1,0:T(8,128)(2,1)}, u32[]{:S(2)}) copy-start(bf16[128,1024]{1,0:T(8,128)(2,1)} %param.34) | copy-start | bytes 786436
  23.9 25.1 %copy-start.7 = (f32[128,16]{0,1:T(8,128)S(1)}, f32[128,16]{0,1:T(8,128)}, u32[]{:S(2)}) copy-start(f32[128,16]{0,1:T(8,128)} %param.30) | copy-start | bytes 24580
  23.9 25.2 %copy-start.8 = (f32[128,16]{0,1:T(8,128)S(1)}, f32[128,16]{0,1:T(8,128)}, u32[]{:S(2)}) copy-start(f32[128,16]{0,1:T(8,128)} %param.31) | copy-start | bytes 24580
  23.9 25.3 %copy-start.5 = (f32[4096]{0:T(1024)S(1)}, f32[4096]{0:T(1024)}, u32[]{:S(2)}) copy-start(f32[4096]{0:T(1024)} %param.25) | copy-start | bytes 49156
  41.9 32.8 %all-to-all-start = ((bf16[128,32,128]{0,2,1:T(8,128)(2,1)}), bf16[128,32,128]{0,2,1:T(8,128)(2,1)}, u32[]{:S(2)}, u32[]{:S(2)}) async-start(bf16[128,32,128]{0,2,1:T(8,128)(2,1)} %bitcast.292), calls=%async_computation | async-start | bytes 2097152 | tf_op jit(solution)/shard_map/all_to_all | solution.py:34
  75.9 57.3 %all-to-all-start.1 = ((bf16[128,32,128]{2,0,1:T(8,128)(2,1)}), bf16[128,32,128]{2,0,1:T(8,128)(2,1)}, u32[]{:S(2)}, u32[]{:S(2)}) async-start(bf16[128,32,128]{2,0,1:T(8,128)(2,1)} %bitcast.291), calls=%async_computation.1 | async-start | bytes 2097152 | tf_op jit(solution)/shard_map/all_to_all | solution.py:35
  229.6 453.6 %all-to-all-start.3 = ((bf16[32,2,8192]{2,1,0:T(2,128)(2,1)}), bf16[32,2,8192]{2,1,0:T(2,128)(2,1)}, u32[]{:S(2)}, u32[]{:S(2)}) async-start(bf16[32,2,8192]{2,1,0:T(2,128)(2,1)} %reshape.395), calls=%async_computation.3 | async-start | bytes 2097152 | tf_op jit(solution)/shard_map/all_to_all | solution.py:63
  239.5 30.0 %collective-permute-start = (f32[16,4096]{1,0:T(8,128)S(1)}, f32[16,4096]{1,0:T(8,128)S(1)}, u32[]{:S(2)}, u32[]{:S(2)}) collective-permute-start(f32[16,4096]{1,0:T(8,128)S(1)} %multiply_add_fusion.12), channel_id=1, source_target_pairs={{0,1},{1,2},{2,3},{3,4},{4,5},{5,6},{6,7},{7,8},{8,9},{9,10},{10,1... | collective-permute-start | bytes 786440 | tf_op jit(solution)/shard_map/while/body/eval_jaxpr/ppermute | solution.py:14
  269.6 11.1 %collective-permute-start = (f32[16,4096]{1,0:T(8,128)S(1)}, f32[16,4096]{1,0:T(8,128)S(1)}, u32[]{:S(2)}, u32[]{:S(2)}) collective-permute-start(f32[16,4096]{1,0:T(8,128)S(1)} %multiply_add_fusion.12), channel_id=1, source_target_pairs={{0,1},{1,2},{2,3},{3,4},{4,5},{5,6},{6,7},{7,8},{8,9},{9,10},{10,1... | collective-permute-start | bytes 786440 | tf_op jit(solution)/shard_map/while/body/eval_jaxpr/ppermute | solution.py:14
  280.8 10.4 %collective-permute-start = (f32[16,4096]{1,0:T(8,128)S(1)}, f32[16,4096]{1,0:T(8,128)S(1)}, u32[]{:S(2)}, u32[]{:S(2)}) collective-permute-start(f32[16,4096]{1,0:T(8,128)S(1)} %multiply_add_fusion.12), channel_id=1, source_target_pairs={{0,1},{1,2},{2,3},{3,4},{4,5},{5,6},{6,7},{7,8},{8,9},{9,10},{10,1... | collective-permute-start | bytes 786440 | tf_op jit(solution)/shard_map/while/body/eval_jaxpr/ppermute | solution.py:14
  291.2 10.4 %collective-permute-start = (f32[16,4096]{1,0:T(8,128)S(1)}, f32[16,4096]{1,0:T(8,128)S(1)}, u32[]{:S(2)}, u32[]{:S(2)}) collective-permute-start(f32[16,4096]{1,0:T(8,128)S(1)} %multiply_add_fusion.12), channel_id=1, source_target_pairs={{0,1},{1,2},{2,3},{3,4},{4,5},{5,6},{6,7},{7,8},{8,9},{9,10},{10,1... | collective-permute-start | bytes 786440 | tf_op jit(solution)/shard_map/while/body/eval_jaxpr/ppermute | solution.py:14
  301.6 10.4 %collective-permute-start = (f32[16,4096]{1,0:T(8,128)S(1)}, f32[16,4096]{1,0:T(8,128)S(1)}, u32[]{:S(2)}, u32[]{:S(2)}) collective-permute-start(f32[16,4096]{1,0:T(8,128)S(1)} %multiply_add_fusion.12), channel_id=1, source_target_pairs={{0,1},{1,2},{2,3},{3,4},{4,5},{5,6},{6,7},{7,8},{8,9},{9,10},{10,1... | collective-permute-start | bytes 786440 | tf_op jit(solution)/shard_map/while/body/eval_jaxpr/ppermute | solution.py:14
  312.0 10.4 %collective-permute-start = (f32[16,4096]{1,0:T(8,128)S(1)}, f32[16,4096]{1,0:T(8,128)S(1)}, u32[]{:S(2)}, u32[]{:S(2)}) collective-permute-start(f32[16,4096]{1,0:T(8,128)S(1)} %multiply_add_fusion.12), channel_id=1, source_target_pairs={{0,1},{1,2},{2,3},{3,4},{4,5},{5,6},{6,7},{7,8},{8,9},{9,10},{10,1... | collective-permute-start | bytes 786440 | tf_op jit(solution)/shard_map/while/body/eval_jaxpr/ppermute | solution.py:14
  322.4 11.4 %collective-permute-start = (f32[16,4096]{1,0:T(8,128)S(1)}, f32[16,4096]{1,0:T(8,128)S(1)}, u32[]{:S(2)}, u32[]{:S(2)}) collective-permute-start(f32[16,4096]{1,0:T(8,128)S(1)} %multiply_add_fusion.12), channel_id=1, source_target_pairs={{0,1},{1,2},{2,3},{3,4},{4,5},{5,6},{6,7},{7,8},{8,9},{9,10},{10,1... | collective-permute-start | bytes 786440 | tf_op jit(solution)/shard_map/while/body/eval_jaxpr/ppermute | solution.py:14
  333.9 12.6 %collective-permute-start = (f32[16,4096]{1,0:T(8,128)S(1)}, f32[16,4096]{1,0:T(8,128)S(1)}, u32[]{:S(2)}, u32[]{:S(2)}) collective-permute-start(f32[16,4096]{1,0:T(8,128)S(1)} %multiply_add_fusion.12), channel_id=1, source_target_pairs={{0,1},{1,2},{2,3},{3,4},{4,5},{5,6},{6,7},{7,8},{8,9},{9,10},{10,1... | collective-permute-start | bytes 786440 | tf_op jit(solution)/shard_map/while/body/eval_jaxpr/ppermute | solution.py:14
  346.5 12.7 %collective-permute-start = (f32[16,4096]{1,0:T(8,128)S(1)}, f32[16,4096]{1,0:T(8,128)S(1)}, u32[]{:S(2)}, u32[]{:S(2)}) collective-permute-start(f32[16,4096]{1,0:T(8,128)S(1)} %multiply_add_fusion.12), channel_id=1, source_target_pairs={{0,1},{1,2},{2,3},{3,4},{4,5},{5,6},{6,7},{7,8},{8,9},{9,10},{10,1... | collective-permute-start | bytes 786440 | tf_op jit(solution)/shard_map/while/body/eval_jaxpr/ppermute | solution.py:14
  359.2 11.8 %collective-permute-start = (f32[16,4096]{1,0:T(8,128)S(1)}, f32[16,4096]{1,0:T(8,128)S(1)}, u32[]{:S(2)}, u32[]{:S(2)}) collective-permute-start(f32[16,4096]{1,0:T(8,128)S(1)} %multiply_add_fusion.12), channel_id=1, source_target_pairs={{0,1},{1,2},{2,3},{3,4},{4,5},{5,6},{6,7},{7,8},{8,9},{9,10},{10,1... | collective-permute-start | bytes 786440 | tf_op jit(solution)/shard_map/while/body/eval_jaxpr/ppermute | solution.py:14
  371.0 11.0 %collective-permute-start = (f32[16,4096]{1,0:T(8,128)S(1)}, f32[16,4096]{1,0:T(8,128)S(1)}, u32[]{:S(2)}, u32[]{:S(2)}) collective-permute-start(f32[16,4096]{1,0:T(8,128)S(1)} %multiply_add_fusion.12), channel_id=1, source_target_pairs={{0,1},{1,2},{2,3},{3,4},{4,5},{5,6},{6,7},{7,8},{8,9},{9,10},{10,1... | collective-permute-start | bytes 786440 | tf_op jit(solution)/shard_map/while/body/eval_jaxpr/ppermute | solution.py:14
  382.0 10.4 %collective-permute-start = (f32[16,4096]{1,0:T(8,128)S(1)}, f32[16,4096]{1,0:T(8,128)S(1)}, u32[]{:S(2)}, u32[]{:S(2)}) collective-permute-start(f32[16,4096]{1,0:T(8,128)S(1)} %multiply_add_fusion.12), channel_id=1, source_target_pairs={{0,1},{1,2},{2,3},{3,4},{4,5},{5,6},{6,7},{7,8},{8,9},{9,10},{10,1... | collective-permute-start | bytes 786440 | tf_op jit(solution)/shard_map/while/body/eval_jaxpr/ppermute | solution.py:14
  392.4 10.4 %collective-permute-start = (f32[16,4096]{1,0:T(8,128)S(1)}, f32[16,4096]{1,0:T(8,128)S(1)}, u32[]{:S(2)}, u32[]{:S(2)}) collective-permute-start(f32[16,4096]{1,0:T(8,128)S(1)} %multiply_add_fusion.12), channel_id=1, source_target_pairs={{0,1},{1,2},{2,3},{3,4},{4,5},{5,6},{6,7},{7,8},{8,9},{9,10},{10,1... | collective-permute-start | bytes 786440 | tf_op jit(solution)/shard_map/while/body/eval_jaxpr/ppermute | solution.py:14
  402.9 10.4 %collective-permute-start = (f32[16,4096]{1,0:T(8,128)S(1)}, f32[16,4096]{1,0:T(8,128)S(1)}, u32[]{:S(2)}, u32[]{:S(2)}) collective-permute-start(f32[16,4096]{1,0:T(8,128)S(1)} %multiply_add_fusion.12), channel_id=1, source_target_pairs={{0,1},{1,2},{2,3},{3,4},{4,5},{5,6},{6,7},{7,8},{8,9},{9,10},{10,1... | collective-permute-start | bytes 786440 | tf_op jit(solution)/shard_map/while/body/eval_jaxpr/ppermute | solution.py:14
  413.3 10.4 %collective-permute-start = (f32[16,4096]{1,0:T(8,128)S(1)}, f32[16,4096]{1,0:T(8,128)S(1)}, u32[]{:S(2)}, u32[]{:S(2)}) collective-permute-start(f32[16,4096]{1,0:T(8,128)S(1)} %multiply_add_fusion.12), channel_id=1, source_target_pairs={{0,1},{1,2},{2,3},{3,4},{4,5},{5,6},{6,7},{7,8},{8,9},{9,10},{10,1... | collective-permute-start | bytes 786440 | tf_op jit(solution)/shard_map/while/body/eval_jaxpr/ppermute | solution.py:14
  423.8 11.6 %collective-permute-start = (f32[16,4096]{1,0:T(8,128)S(1)}, f32[16,4096]{1,0:T(8,128)S(1)}, u32[]{:S(2)}, u32[]{:S(2)}) collective-permute-start(f32[16,4096]{1,0:T(8,128)S(1)} %multiply_add_fusion.12), channel_id=1, source_target_pairs={{0,1},{1,2},{2,3},{3,4},{4,5},{5,6},{6,7},{7,8},{8,9},{9,10},{10,1... | collective-permute-start | bytes 786440 | tf_op jit(solution)/shard_map/while/body/eval_jaxpr/ppermute | solution.py:14
  435.4 12.7 %collective-permute-start = (f32[16,4096]{1,0:T(8,128)S(1)}, f32[16,4096]{1,0:T(8,128)S(1)}, u32[]{:S(2)}, u32[]{:S(2)}) collective-permute-start(f32[16,4096]{1,0:T(8,128)S(1)} %multiply_add_fusion.12), channel_id=1, source_target_pairs={{0,1},{1,2},{2,3},{3,4},{4,5},{5,6},{6,7},{7,8},{8,9},{9,10},{10,1... | collective-permute-start | bytes 786440 | tf_op jit(solution)/shard_map/while/body/eval_jaxpr/ppermute | solution.py:14
  448.2 12.5 %collective-permute-start = (f32[16,4096]{1,0:T(8,128)S(1)}, f32[16,4096]{1,0:T(8,128)S(1)}, u32[]{:S(2)}, u32[]{:S(2)}) collective-permute-start(f32[16,4096]{1,0:T(8,128)S(1)} %multiply_add_fusion.12), channel_id=1, source_target_pairs={{0,1},{1,2},{2,3},{3,4},{4,5},{5,6},{6,7},{7,8},{8,9},{9,10},{10,1... | collective-permute-start | bytes 786440 | tf_op jit(solution)/shard_map/while/body/eval_jaxpr/ppermute | solution.py:14
  460.7 11.6 %collective-permute-start = (f32[16,4096]{1,0:T(8,128)S(1)}, f32[16,4096]{1,0:T(8,128)S(1)}, u32[]{:S(2)}, u32[]{:S(2)}) collective-permute-start(f32[16,4096]{1,0:T(8,128)S(1)} %multiply_add_fusion.12), channel_id=1, source_target_pairs={{0,1},{1,2},{2,3},{3,4},{4,5},{5,6},{6,7},{7,8},{8,9},{9,10},{10,1... | collective-permute-start | bytes 786440 | tf_op jit(solution)/shard_map/while/body/eval_jaxpr/ppermute | solution.py:14
  472.4 10.8 %collective-permute-start = (f32[16,4096]{1,0:T(8,128)S(1)}, f32[16,4096]{1,0:T(8,128)S(1)}, u32[]{:S(2)}, u32[]{:S(2)}) collective-permute-start(f32[16,4096]{1,0:T(8,128)S(1)} %multiply_add_fusion.12), channel_id=1, source_target_pairs={{0,1},{1,2},{2,3},{3,4},{4,5},{5,6},{6,7},{7,8},{8,9},{9,10},{10,1... | collective-permute-start | bytes 786440 | tf_op jit(solution)/shard_map/while/body/eval_jaxpr/ppermute | solution.py:14
  483.2 10.4 %collective-permute-start = (f32[16,4096]{1,0:T(8,128)S(1)}, f32[16,4096]{1,0:T(8,128)S(1)}, u32[]{:S(2)}, u32[]{:S(2)}) collective-permute-start(f32[16,4096]{1,0:T(8,128)S(1)} %multiply_add_fusion.12), channel_id=1, source_target_pairs={{0,1},{1,2},{2,3},{3,4},{4,5},{5,6},{6,7},{7,8},{8,9},{9,10},{10,1... | collective-permute-start | bytes 786440 | tf_op jit(solution)/shard_map/while/body/eval_jaxpr/ppermute | solution.py:14
  493.6 10.4 %collective-permute-start = (f32[16,4096]{1,0:T(8,128)S(1)}, f32[16,4096]{1,0:T(8,128)S(1)}, u32[]{:S(2)}, u32[]{:S(2)}) collective-permute-start(f32[16,4096]{1,0:T(8,128)S(1)} %multiply_add_fusion.12), channel_id=1, source_target_pairs={{0,1},{1,2},{2,3},{3,4},{4,5},{5,6},{6,7},{7,8},{8,9},{9,10},{10,1... | collective-permute-start | bytes 786440 | tf_op jit(solution)/shard_map/while/body/eval_jaxpr/ppermute | solution.py:14
  504.0 10.4 %collective-permute-start = (f32[16,4096]{1,0:T(8,128)S(1)}, f32[16,4096]{1,0:T(8,128)S(1)}, u32[]{:S(2)}, u32[]{:S(2)}) collective-permute-start(f32[16,4096]{1,0:T(8,128)S(1)} %multiply_add_fusion.12), channel_id=1, source_target_pairs={{0,1},{1,2},{2,3},{3,4},{4,5},{5,6},{6,7},{7,8},{8,9},{9,10},{10,1... | collective-permute-start | bytes 786440 | tf_op jit(solution)/shard_map/while/body/eval_jaxpr/ppermute | solution.py:14
  514.4 10.6 %collective-permute-start = (f32[16,4096]{1,0:T(8,128)S(1)}, f32[16,4096]{1,0:T(8,128)S(1)}, u32[]{:S(2)}, u32[]{:S(2)}) collective-permute-start(f32[16,4096]{1,0:T(8,128)S(1)} %multiply_add_fusion.12), channel_id=1, source_target_pairs={{0,1},{1,2},{2,3},{3,4},{4,5},{5,6},{6,7},{7,8},{8,9},{9,10},{10,1... | collective-permute-start | bytes 786440 | tf_op jit(solution)/shard_map/while/body/eval_jaxpr/ppermute | solution.py:14
  525.1 11.8 %collective-permute-start = (f32[16,4096]{1,0:T(8,128)S(1)}, f32[16,4096]{1,0:T(8,128)S(1)}, u32[]{:S(2)}, u32[]{:S(2)}) collective-permute-start(f32[16,4096]{1,0:T(8,128)S(1)} %multiply_add_fusion.12), channel_id=1, source_target_pairs={{0,1},{1,2},{2,3},{3,4},{4,5},{5,6},{6,7},{7,8},{8,9},{9,10},{10,1... | collective-permute-start | bytes 786440 | tf_op jit(solution)/shard_map/while/body/eval_jaxpr/ppermute | solution.py:14
  536.9 12.9 %collective-permute-start = (f32[16,4096]{1,0:T(8,128)S(1)}, f32[16,4096]{1,0:T(8,128)S(1)}, u32[]{:S(2)}, u32[]{:S(2)}) collective-permute-start(f32[16,4096]{1,0:T(8,128)S(1)} %multiply_add_fusion.12), channel_id=1, source_target_pairs={{0,1},{1,2},{2,3},{3,4},{4,5},{5,6},{6,7},{7,8},{8,9},{9,10},{10,1... | collective-permute-start | bytes 786440 | tf_op jit(solution)/shard_map/while/body/eval_jaxpr/ppermute | solution.py:14
  549.9 12.3 %collective-permute-start = (f32[16,4096]{1,0:T(8,128)S(1)}, f32[16,4096]{1,0:T(8,128)S(1)}, u32[]{:S(2)}, u32[]{:S(2)}) collective-permute-start(f32[16,4096]{1,0:T(8,128)S(1)} %multiply_add_fusion.12), channel_id=1, source_target_pairs={{0,1},{1,2},{2,3},{3,4},{4,5},{5,6},{6,7},{7,8},{8,9},{9,10},{10,1... | collective-permute-start | bytes 786440 | tf_op jit(solution)/shard_map/while/body/eval_jaxpr/ppermute | solution.py:14
  562.3 11.5 %collective-permute-start = (f32[16,4096]{1,0:T(8,128)S(1)}, f32[16,4096]{1,0:T(8,128)S(1)}, u32[]{:S(2)}, u32[]{:S(2)}) collective-permute-start(f32[16,4096]{1,0:T(8,128)S(1)} %multiply_add_fusion.12), channel_id=1, source_target_pairs={{0,1},{1,2},{2,3},{3,4},{4,5},{5,6},{6,7},{7,8},{8,9},{9,10},{10,1... | collective-permute-start | bytes 786440 | tf_op jit(solution)/shard_map/while/body/eval_jaxpr/ppermute | solution.py:14
  573.8 10.4 %collective-permute-start = (f32[16,4096]{1,0:T(8,128)S(1)}, f32[16,4096]{1,0:T(8,128)S(1)}, u32[]{:S(2)}, u32[]{:S(2)}) collective-permute-start(f32[16,4096]{1,0:T(8,128)S(1)} %multiply_add_fusion.12), channel_id=1, source_target_pairs={{0,1},{1,2},{2,3},{3,4},{4,5},{5,6},{6,7},{7,8},{8,9},{9,10},{10,1... | collective-permute-start | bytes 786440 | tf_op jit(solution)/shard_map/while/body/eval_jaxpr/ppermute | solution.py:14
  584.2 10.4 %collective-permute-start = (f32[16,4096]{1,0:T(8,128)S(1)}, f32[16,4096]{1,0:T(8,128)S(1)}, u32[]{:S(2)}, u32[]{:S(2)}) collective-permute-start(f32[16,4096]{1,0:T(8,128)S(1)} %multiply_add_fusion.12), channel_id=1, source_target_pairs={{0,1},{1,2},{2,3},{3,4},{4,5},{5,6},{6,7},{7,8},{8,9},{9,10},{10,1... | collective-permute-start | bytes 786440 | tf_op jit(solution)/shard_map/while/body/eval_jaxpr/ppermute | solution.py:14
  594.6 10.4 %collective-permute-start = (f32[16,4096]{1,0:T(8,128)S(1)}, f32[16,4096]{1,0:T(8,128)S(1)}, u32[]{:S(2)}, u32[]{:S(2)}) collective-permute-start(f32[16,4096]{1,0:T(8,128)S(1)} %multiply_add_fusion.12), channel_id=1, source_target_pairs={{0,1},{1,2},{2,3},{3,4},{4,5},{5,6},{6,7},{7,8},{8,9},{9,10},{10,1... | collective-permute-start | bytes 786440 | tf_op jit(solution)/shard_map/while/body/eval_jaxpr/ppermute | solution.py:14
  605.0 74.0 %copy-start.6 = (f32[4096]{0:T(1024)S(1)}, f32[4096]{0:T(1024)}, u32[]{:S(2)}) copy-start(f32[4096]{0:T(1024)} %param.32) | copy-start | bytes 49156
where the time goes:
time: 698 us; the launch traced here: 694 us
  waiting for transfers between devices  341 us (49%)
  local copies, waits for them, and re-layouts  118 us (17%)
  starting transfers between devices  100 us (14%)
  other arithmetic  65 us (9%)
  matrix products  60.6 us (9%)
  loops' own time  9.05 us (1%)
    ppermute x32, waiting for transfers between devices, shifted(): return lax.ppermute(block, axis, route)  303 us
    ppermute x32, starting transfers between devices, shifted(): return lax.ppermute(block, axis, route)  64.4 us
    slice x16, local copies, waits for them, and re-layouts, per_device(): lax.scan(carry_only, zero_state, (step, conv, state_in), unroll=8)  37.8 us
    slice x16, local copies, waits for them, and re-layouts, per_device(): lax.scan(with_read, incoming, (step, conv, state_in, state_out), unroll=8)  37.8 us
    dot_general x8, matrix products, block(): jnp.einsum('hij,jhd->ihd', expo.astype(jnp.bfloat16), v_all, preferred_el...  33.5 us
    dot_general x8, matrix products, block(): jnp.einsum('ihd,jhd->hij', query_block, k_all, preferred_element_type=jnp...  24.3 us
    reduce_sum x8, other arithmetic, block(): total = jnp.sum(expo, axis=-1)  22.7 us
    all_to_all x1, waiting for transfers between devices, attend_by_heads(): lax.all_to_all(q_three, 'seq', split_axis=1, concat_axis=0, tiled=True)  20.3 us
  transfers between devices with their start and end apart: 36, of which 33 were waited for; matrix products, arithmetic and copies ran while one was open for 20% of the time, Pallas kernels for 0%

commit v1 on v0

--- a/solution.py
+++ b/solution.py
@@ -106,13 +106,17 @@
 
     zero_state = jnp.zeros(rate.shape, jnp.float32)
     local_end, unused = lax.scan(carry_only, zero_state, (step, conv, state_in), unroll=8)
-    decay_total = jnp.exp(rate * jnp.sum(step, axis=0)[None, :])
-
-    def hop(index, incoming):
-        leaving = decay_total * incoming + local_end
-        return shifted(leaving, "seq", 1)
-
-    incoming = lax.fori_loop(0, lax.axis_size("seq") - 1, hop, zero_state)
+    step_sum = jnp.sum(step, axis=0)[None, :]
+    packed = shifted(jnp.concatenate([step_sum, local_end], 0), "seq", 1)
+    distance = 1
+    while distance < lax.axis_size("seq"):
+        other = shifted(packed, "seq", distance)
+        decay = jnp.exp(rate * packed[:1])
+        packed = jnp.concatenate(
+            [packed[:1] + other[:1], decay * other[1:] + packed[1:]], 0
+        )
+        distance *= 2
+    incoming = packed[1:]
     final, read = lax.scan(with_read, incoming, (step, conv, state_in, state_out), unroll=8)
     mamba_out = (
         (read + skip_gain[None, :] * conv) * jax.nn.silu(inner_gate.astype(jnp.float32))

time: 698 us -> 435 us (0.62)
  the two profiles are of different devices: /device:TPU:14 before, /device:TPU:16 now
where the time goes in v1:
time: 435 us; the launch traced here: 431 us
  local copies, waits for them, and re-layouts  132 us (30%)
  starting transfers between devices  85.9 us (20%)
  other arithmetic  70.6 us (16%)
  waiting for transfers between devices  70.6 us (16%)
  matrix products  61.5 us (14%)
  loops' own time  8.93 us (2%)
    ppermute x7, waiting for transfers between devices, shifted(): return lax.ppermute(block, axis, route)  58.1 us
    ppermute x7, starting transfers between devices, shifted(): return lax.ppermute(block, axis, route)  42.8 us
    slice x16, local copies, waits for them, and re-layouts, per_device(): lax.scan(carry_only, zero_state, (step, conv, state_in), unroll=8)  38 us
    slice x16, local copies, waits for them, and re-layouts, per_device(): lax.scan(with_read, incoming, (step, conv, state_in, state_out), unroll=8)  38 us
    dot_general x8, matrix products, block(): jnp.einsum('hij,jhd->ihd', expo.astype(jnp.bfloat16), v_all, preferred_el...  33.5 us
    dot_general x8, matrix products, block(): jnp.einsum('ihd,jhd->hij', query_block, k_all, preferred_element_type=jnp...  24.3 us
    reduce_sum x8, other arithmetic, block(): total = jnp.sum(expo, axis=-1)  22.7 us
    all_to_all x1, starting transfers between devices, attend_by_heads(): lax.all_to_all(q_three, 'seq', split_axis=1, concat_axis=0, tiled=True)  21 us
  transfers between devices with their start and end apart: 11, of which 8 were waited for; matrix products, arithmetic and copies ran while one was open for 25% of the time, Pallas kernels for 0%

profile of v1, /device:TPU:16, one launch (start us, length us, event | category | flops | bytes accessed | tf_op | source)
XLA Modules:
  0.0 430.8 jit_solution(4084153240199908252)
XLA Ops:
  1.7 3.8 collective-permute-start
  7.6 3.7 fusion.60
  11.4 4.6 %divide_multiply_fusion = f32[128,4096]{1,0:T(8,128)} fusion(bf16[128,4096]{1,0:T(8,128)(2,1)} %param.20, bf16[3,4096]{1,0:T(4,128)(2,1)S(1)} %collective-permute-done, f32[4096]{0:T(1024)S(1)} %copy-done.5, f32[4096]{0:T(1024)S(1)} %bitcast.357, f32[4096]{0:T(1024)S(1)} %bitcast.358, f32[4096]{0:T(1024)S(1)} %bitcast.356, f32[4096]{0:T(1024)S(1)} %bitcast.355), kind=kLoop, calls=%fused_computation.124 | loop fusion | flops 13107200 | bytes 3252224 | tf_op jit(solution)/shard_map/jit(silu)/mul | solution.py:25
  16.0 47.9 %while.36 = (s32[]{:T(128)}, f32[16,4096]{1,0:T(8,128)S(1)}, f32[16,8,4096]{2,1,0:T(8,128)}, f32[16,4096]{1,0:T(8,128)S(1)}, f32[16,8,4096]{2,1,0:T(8,128)}, /*i...) while((s32[]{:T(128)}, f32[16,4096]{1,0:T(8,128)S(1)}, ...), condition=%wide.region_2.3_spmd.clone, body=%wide.region_1.2_spmd.clone.sunk | while | flops 2195466 | bytes 1968919 | solution.py:108
  64.5 3.8 collective-permute-start.1
  68.4 8.0 %collective-permute-done.1 = f32[17,4096]{1,0:T(8,128)S(1)} collective-permute-done((f32[17,4096]{1,0:T(8,128)S(1)}, f32[17,4096]{1,0:T(8,128)S(1)}, u32[]{:S(2)}, u32[]{:S(2)}) %collective-permute-start.1) | collective-permute-done | bytes 278560 | tf_op jit(solution)/shard_map/ppermute | solution.py:14
  76.4 4.4 %collective-permute-start.2 = (f32[17,4096]{1,0:T(8,128)S(1)}, f32[17,4096]{1,0:T(8,128)S(1)}, u32[]{:S(2)}, u32[]{:S(2)}) collective-permute-start(f32[17,4096]{1,0:T(8,128)S(1)} %collective-permute-done.1), channel_id=1, source_target_pairs={{0,1},{1,2},{2,3},{3,4},{4,5},{5,6},{6,7},{7,8},{8,9},{9,10},{10,1... | collective-permute-start | bytes 835592 | tf_op jit(solution)/shard_map/ppermute | solution.py:14
  80.8 7.2 %collective-permute-done.2 = f32[17,4096]{1,0:T(8,128)S(1)} collective-permute-done((f32[17,4096]{1,0:T(8,128)S(1)}, f32[17,4096]{1,0:T(8,128)S(1)}, u32[]{:S(2)}, u32[]{:S(2)}) %collective-permute-start.2) | collective-permute-done | bytes 278560 | tf_op jit(solution)/shard_map/ppermute | solution.py:14
  88.2 7.2 %collective-permute-start.3 = (f32[17,4096]{1,0:T(8,128)S(1)}, f32[17,4096]{1,0:T(8,128)}, u32[]{:S(2)}, u32[]{:S(2)}) collective-permute-start(f32[17,4096]{1,0:T(8,128)S(1)} %pad_maximum_fusion.2), channel_id=1, source_target_pairs={{0,2},{1,3},{2,4},{3,5},{4,6},{5,7},{6,8},{7,9},{8,10},{9,11},{10,... | collective-permute-start | bytes 835592 | tf_op jit(solution)/shard_map/ppermute | solution.py:14
  96.6 9.7 %all-to-all-start.2 = ((bf16[128,32,128]{2,0,1:T(8,128)(2,1)}), bf16[128,32,128]{2,0,1:T(8,128)(2,1)}, u32[]{:S(2)}, u32[]{:S(2)}) async-start(bf16[128,32,128]{2,0,1:T(8,128)(2,1)} %bitcast.298), calls=%async_computation.2 | async-start | bytes 2097152 | tf_op jit(solution)/shard_map/all_to_all | solution.py:36
  106.4 6.8 %collective-permute-done.3 = f32[17,4096]{1,0:T(8,128)} collective-permute-done((f32[17,4096]{1,0:T(8,128)S(1)}, f32[17,4096]{1,0:T(8,128)}, u32[]{:S(2)}, u32[]{:S(2)}) %collective-permute-start.3) | collective-permute-done | bytes 278560 | tf_op jit(solution)/shard_map/ppermute | solution.py:14
  115.3 14.0 %collective-permute-start.4 = (f32[17,4096]{1,0:T(8,128)S(1)}, f32[17,4096]{1,0:T(8,128)}, u32[]{:S(2)}, u32[]{:S(2)}) collective-permute-start(f32[17,4096]{1,0:T(8,128)S(1)} %pad_maximum_fusion.3), channel_id=1, source_target_pairs={{0,4},{1,5},{2,6},{3,7},{4,8},{5,9},{6,10},{7,11},{8,12},{9,13},{1... | collective-permute-start | bytes 835592 | tf_op jit(solution)/shard_map/ppermute | solution.py:14
  131.6 9.2 %collective-permute-done.4 = f32[17,4096]{1,0:T(8,128)} collective-permute-done((f32[17,4096]{1,0:T(8,128)S(1)}, f32[17,4096]{1,0:T(8,128)}, u32[]{:S(2)}, u32[]{:S(2)}) %collective-permute-start.4) | collective-permute-done | bytes 278560 | tf_op jit(solution)/shard_map/ppermute | solution.py:14
  141.9 21.0 %all-to-all-start = ((bf16[128,32,128]{0,2,1:T(8,128)(2,1)}), bf16[128,32,128]{0,2,1:T(8,128)(2,1)}, u32[]{:S(2)}, u32[]{:S(2)}) async-start(bf16[128,32,128]{0,2,1:T(8,128)(2,1)} %bitcast.299), calls=%async_computation | async-start | bytes 2097152 | tf_op jit(solution)/shard_map/all_to_all | solution.py:34
  163.9 3.6 collective-permute-start.5
  168.6 13.5 %collective-permute-done.5 = f32[17,4096]{1,0:T(8,128)S(1)} collective-permute-done((f32[17,4096]{1,0:T(8,128)S(1)}, f32[17,4096]{1,0:T(8,128)S(1)}, u32[]{:S(2)}, u32[]{:S(2)}) %collective-permute-start.5) | collective-permute-done | bytes 278560 | tf_op jit(solution)/shard_map/ppermute | solution.py:14
  182.9 8.5 %all-to-all-done = bf16[128,32,128]{0,2,1:T(8,128)(2,1)} async-done(((bf16[128,32,128]{0,2,1:T(8,128)(2,1)}), bf16[128,32,128]{0,2,1:T(8,128)(2,1)}, u32[]{:S(2)}, u32[]{:S(2)}) %all-to-all-start) | async-done | bytes 1048608 | tf_op jit(solution)/shard_map/all_to_all | solution.py:34
  192.7 5.2 %all-to-all-start.1 = ((bf16[128,32,128]{2,0,1:T(8,128)(2,1)}), bf16[128,32,128]{2,0,1:T(8,128)(2,1)}, u32[]{:S(2)}, u32[]{:S(2)}) async-start(bf16[128,32,128]{2,0,1:T(8,128)(2,1)} %bitcast.297), calls=%async_computation.1 | async-start | bytes 2097152 | tf_op jit(solution)/shard_map/all_to_all | solution.py:35
  198.8 5.9 %collective-permute-start.6 = (f32[17,4096]{1,0:T(8,128)S(1)}, f32[17,4096]{1,0:T(8,128)}, u32[]{:S(2)}, u32[]{:S(2)}) collective-permute-start(f32[17,4096]{1,0:T(8,128)S(1)} %pad_maximum_fusion.5), channel_id=1, source_target_pairs={{0,16},{1,17},{2,18},{3,19},{4,20},{5,21},{6,22},{7,23},{8,24},{9,... | collective-permute-start | bytes 835592 | tf_op jit(solution)/shard_map/ppermute | solution.py:14
  205.5 13.3 %collective-permute-done.6 = f32[17,4096]{1,0:T(8,128)} collective-permute-done((f32[17,4096]{1,0:T(8,128)S(1)}, f32[17,4096]{1,0:T(8,128)}, u32[]{:S(2)}, u32[]{:S(2)}) %collective-permute-start.6) | collective-permute-done | bytes 278560 | tf_op jit(solution)/shard_map/ppermute | solution.py:14
  222.1 4.0 all-to-all-done.1
  226.1 91.3 %while.35 = (s32[]{:T(128)}, bf16[8,512,1,128]{3,1,2,0:T(8,128)(2,1)}, s32[8]{0:T(128)S(1)}, bf16[4096,1,128]{2,0,1:T(8,128)(2,1)}, bf16[4096,1,128]{2,0,1:T(8,1...) while((s32[]{:T(128)}, ...), condition=%wide.region_16.17_spmd.clone, body=%wide.region_13.16_spmd.clone.sunk | while | flops 1107426816 | bytes 27543732 | solution.py:61
  227.5 3.0 fusion.73
  230.5 2.8 fusion.74
  233.3 4.2 fusion.75
  238.9 3.0 fusion.73
  241.9 2.8 fusion.74
  244.8 4.2 fusion.75
  250.3 3.0 fusion.73
  256.2 4.2 fusion.75
  261.7 3.0 fusion.73
  264.7 2.8 fusion.74
  267.6 4.2 fusion.75
  273.1 3.0 fusion.73
  276.2 2.8 fusion.74
  279.0 4.2 fusion.75
  284.5 3.0 fusion.73
  290.4 4.2 fusion.75
  295.9 3.0 fusion.73
  299.0 2.8 fusion.74
  301.8 4.2 fusion.75
  307.4 3.0 fusion.73
  313.2 4.2 fusion.75
  318.0 3.4 reduce.4
  323.5 7.1 %all-to-all-start.3 = ((bf16[32,2,8192]{2,1,0:T(2,128)(2,1)}), bf16[32,2,8192]{2,1,0:T(2,128)(2,1)}, u32[]{:S(2)}, u32[]{:S(2)}) async-start(bf16[32,2,8192]{2,1,0:T(2,128)(2,1)} %reshape.394), calls=%async_computation.3 | async-start | bytes 2097152 | tf_op jit(solution)/shard_map/all_to_all | solution.py:63
  330.7 84.9 %while.34 = (s32[]{:T(128)}, f32[16,4096]{1,0:T(8,128)S(1)}, f32[16,8,4096]{2,1,0:T(8,128)}, f32[16,8,4096]{2,1,0:T(8,128)}, f32[16,4096]{1,0:T(8,128)S(1)}, /*i...) while((s32[]{:T(128)}, f32[16,4096]{1,0:T(8,128)S(1)}, ...), condition=%wide.region_12.13_spmd, body=%wide.region_3.12_spmd.sunk | while | flops 4718601 | bytes 4134561 | solution.py:120
  415.6 4.2 fusion.52
  419.8 5.8 %reshape.395 = bf16[4096,1,128]{2,1,0:T(2,128)(2,1)} reshape(bf16[32,2,8192]{2,1,0:T(2,128)(2,1)} %all-to-all-done.3) | data formatting | bytes 2097152
  (538 shorter events, 171.0 us)
Async XLA Ops:
  0.6 6.9 %copy-start = (bf16[256,4096]{1,0:T(8,128)(2,1)S(1)}, bf16[256,4096]{1,0:T(8,128)(2,1)}, u32[]{:S(2)}) copy-start(bf16[256,4096]{1,0:T(8,128)(2,1)} %param.25) | copy-start | bytes 6291460
  1.7 9.7 %collective-permute-start = (bf16[3,4096]{1,0:T(4,128)(2,1)S(1)}, bf16[3,4096]{1,0:T(4,128)(2,1)S(1)}, u32[]{:S(2)}, u32[]{:S(2)}) collective-permute-start(bf16[3,4096]{1,0:T(4,128)(2,1)S(1)} %slice.283), channel_id=1, source_target_pairs={{0,1},{1,2},{2,3},{3,4},{4,5},{5,6},{6,7},{7,8},{8,9},{9,10},{10,1... | collective-permute-start | bytes 73736 | tf_op jit(solution)/shard_map/ppermute | solution.py:14
  7.6 3.7 copy-start.7
  7.6 3.8 copy-start.5
  16.0 72.1 %copy-start.1 = (f32[16,4096]{1,0:T(8,128)S(1)}, f32[16,4096]{1,0:T(8,128)}, u32[]{:S(2)}) copy-start(f32[16,4096]{1,0:T(8,128)} %param.27) | copy-start | bytes 786436
  63.9 0.6 copy-start.4
  63.9 31.5 %copy-start.2 = (bf16[128,1024]{1,0:T(8,128)(2,1)S(1)}, bf16[128,1024]{1,0:T(8,128)(2,1)}, u32[]{:S(2)}) copy-start(bf16[128,1024]{1,0:T(8,128)(2,1)} %param.33) | copy-start | bytes 786436
  64.5 11.9 %collective-permute-start.1 = (f32[17,4096]{1,0:T(8,128)S(1)}, f32[17,4096]{1,0:T(8,128)S(1)}, u32[]{:S(2)}, u32[]{:S(2)}) collective-permute-start(f32[17,4096]{1,0:T(8,128)S(1)} %pad_maximum_fusion.1), channel_id=1, source_target_pairs={{0,1},{1,2},{2,3},{3,4},{4,5},{5,6},{6,7},{7,8},{8,9},{9,10},{10,1... | collective-permute-start | bytes 835592 | tf_op jit(solution)/shard_map/ppermute | solution.py:14
  76.4 11.6 %collective-permute-start.2 = (f32[17,4096]{1,0:T(8,128)S(1)}, f32[17,4096]{1,0:T(8,128)S(1)}, u32[]{:S(2)}, u32[]{:S(2)}) collective-permute-start(f32[17,4096]{1,0:T(8,128)S(1)} %collective-permute-done.1), channel_id=1, source_target_pairs={{0,1},{1,2},{2,3},{3,4},{4,5},{5,6},{6,7},{7,8},{8,9},{9,10},{10,1... | collective-permute-start | bytes 835592 | tf_op jit(solution)/shard_map/ppermute | solution.py:14
  88.2 25.0 %collective-permute-start.3 = (f32[17,4096]{1,0:T(8,128)S(1)}, f32[17,4096]{1,0:T(8,128)}, u32[]{:S(2)}, u32[]{:S(2)}) collective-permute-start(f32[17,4096]{1,0:T(8,128)S(1)} %pad_maximum_fusion.2), channel_id=1, source_target_pairs={{0,2},{1,3},{2,4},{3,5},{4,6},{5,7},{6,8},{7,9},{8,10},{9,11},{10,... | collective-permute-start | bytes 835592 | tf_op jit(solution)/shard_map/ppermute | solution.py:14
  96.6 45.2 %all-to-all-start.2 = ((bf16[128,32,128]{2,0,1:T(8,128)(2,1)}), bf16[128,32,128]{2,0,1:T(8,128)(2,1)}, u32[]{:S(2)}, u32[]{:S(2)}) async-start(bf16[128,32,128]{2,0,1:T(8,128)(2,1)} %bitcast.298), calls=%async_computation.2 | async-start | bytes 2097152 | tf_op jit(solution)/shard_map/all_to_all | solution.py:36
  115.3 25.5 %collective-permute-start.4 = (f32[17,4096]{1,0:T(8,128)S(1)}, f32[17,4096]{1,0:T(8,128)}, u32[]{:S(2)}, u32[]{:S(2)}) collective-permute-start(f32[17,4096]{1,0:T(8,128)S(1)} %pad_maximum_fusion.3), channel_id=1, source_target_pairs={{0,4},{1,5},{2,6},{3,7},{4,8},{5,9},{6,10},{7,11},{8,12},{9,13},{1... | collective-permute-start | bytes 835592 | tf_op jit(solution)/shard_map/ppermute | solution.py:14
  141.9 49.6 %all-to-all-start = ((bf16[128,32,128]{0,2,1:T(8,128)(2,1)}), bf16[128,32,128]{0,2,1:T(8,128)(2,1)}, u32[]{:S(2)}, u32[]{:S(2)}) async-start(bf16[128,32,128]{0,2,1:T(8,128)(2,1)} %bitcast.299), calls=%async_computation | async-start | bytes 2097152 | tf_op jit(solution)/shard_map/all_to_all | solution.py:34
  163.9 18.2 %collective-permute-start.5 = (f32[17,4096]{1,0:T(8,128)S(1)}, f32[17,4096]{1,0:T(8,128)S(1)}, u32[]{:S(2)}, u32[]{:S(2)}) collective-permute-start(f32[17,4096]{1,0:T(8,128)S(1)} %pad_maximum_fusion.4), channel_id=1, source_target_pairs={{0,8},{1,9},{2,10},{3,11},{4,12},{5,13},{6,14},{7,15},{8,16},{9,17... | collective-permute-start | bytes 835592 | tf_op jit(solution)/shard_map/ppermute | solution.py:14
  182.1 0.7 copy-start.3
  182.9 21.8 %copy-start.8 = (f32[128,16]{0,1:T(8,128)S(1)}, f32[128,16]{0,1:T(8,128)}, u32[]{:S(2)}) copy-start(f32[128,16]{0,1:T(8,128)} %param.29) | copy-start | bytes 24580
  192.7 33.4 %all-to-all-start.1 = ((bf16[128,32,128]{2,0,1:T(8,128)(2,1)}), bf16[128,32,128]{2,0,1:T(8,128)(2,1)}, u32[]{:S(2)}, u32[]{:S(2)}) async-start(bf16[128,32,128]{2,0,1:T(8,128)(2,1)} %bitcast.297), calls=%async_computation.1 | async-start | bytes 2097152 | tf_op jit(solution)/shard_map/all_to_all | solution.py:35
  198.8 19.9 %collective-permute-start.6 = (f32[17,4096]{1,0:T(8,128)S(1)}, f32[17,4096]{1,0:T(8,128)}, u32[]{:S(2)}, u32[]{:S(2)}) collective-permute-start(f32[17,4096]{1,0:T(8,128)S(1)} %pad_maximum_fusion.5), channel_id=1, source_target_pairs={{0,16},{1,17},{2,18},{3,19},{4,20},{5,21},{6,22},{7,23},{8,24},{9,... | collective-permute-start | bytes 835592 | tf_op jit(solution)/shard_map/ppermute | solution.py:14
  323.5 96.3 %all-to-all-start.3 = ((bf16[32,2,8192]{2,1,0:T(2,128)(2,1)}), bf16[32,2,8192]{2,1,0:T(2,128)(2,1)}, u32[]{:S(2)}, u32[]{:S(2)}) async-start(bf16[32,2,8192]{2,1,0:T(2,128)(2,1)} %reshape.394), calls=%async_computation.3 | async-start | bytes 2097152 | tf_op jit(solution)/shard_map/all_to_all | solution.py:63
  330.7 84.9 %copy-start.6 = (f32[4096]{0:T(1024)S(1)}, f32[4096]{0:T(1024)}, u32[]{:S(2)}) copy-start(f32[4096]{0:T(1024)} %param.30) | copy-start | bytes 49156

commit v2 on v0

--- a/solution.py
+++ b/solution.py
@@ -1,11 +1,16 @@
+import functools
 import math
 
 import jax
 import jax.numpy as jnp
 from jax import lax
+from jax.experimental import pallas as pl
 from jax.sharding import PartitionSpec as P
 
 HEAD_DIM = 128
+LANES = 128
+CHANNEL_BLOCK = 512
+INTERPRET = False
 
 
 def shifted(block, axis, distance):
@@ -40,28 +45,105 @@
     scale = HEAD_DIM ** (-0.5)
     columns = jnp.arange(length)
 
-    def block(index):
-        start = index * width
-        query_block = lax.dynamic_slice_in_dim(q_all, start, width, 0)
+    pieces = []
+    for index in range(length // width):
+        stop = (index + 1) * width
+        query_block = q_all[stop - width : stop]
         scores = (
-            jnp.einsum("ihd,jhd->hij", query_block, k_all, preferred_element_type=jnp.float32)
+            jnp.einsum(
+                "ihd,jhd->hij", query_block, k_all[:stop], preferred_element_type=jnp.float32
+            )
             * scale
         )
-        rows = start + jnp.arange(width)
-        allowed = rows[:, None] >= columns[None, :]
+        rows = stop - width + jnp.arange(width)
+        allowed = rows[:, None] >= columns[None, :stop]
         masked = jnp.where(allowed[None], scores, -1e30)
         peak = jnp.max(masked, axis=-1, keepdims=True)
         expo = jnp.where(allowed[None], jnp.exp(masked - peak), 0.0)
         total = jnp.sum(expo, axis=-1)
         summed = jnp.einsum(
-            "hij,jhd->ihd", expo.astype(jnp.bfloat16), v_all, preferred_element_type=jnp.float32
+            "hij,jhd->ihd",
+            expo.astype(jnp.bfloat16),
+            v_all[:stop],
+            preferred_element_type=jnp.float32,
         )
-        return (summed / jnp.transpose(total)[:, :, None]).astype(jnp.bfloat16)
-
-    blocks = lax.map(block, jnp.arange(length // width))
-    merged = blocks.reshape(length, q_all.shape[1], HEAD_DIM)
+        pieces.append((summed / jnp.transpose(total)[:, :, None]).astype(jnp.bfloat16))
+    merged = jnp.concatenate(pieces, 0)
     back = lax.all_to_all(merged, "seq", split_axis=0, concat_axis=1, tiled=True)
     return back.reshape(tokens, -1)
+
+
+def scan_kernel(step_ref, drive_ref, rate_ref, in_ref, out_ref, init_ref, result_ref, *, with_read):
+    length = step_ref.shape[0]
+    chunks = step_ref.shape[1] // LANES
+
+    def body(i, states):
+        first = pl.multiple_of(i * 8, 8)
+        steps = [step_ref[pl.ds(first, 8), pl.ds(c * LANES, LANES)] for c in range(chunks)]
+        drives = [drive_ref[pl.ds(first, 8), pl.ds(c * LANES, LANES)] for c in range(chunks)]
+        reads = [[] for c in range(chunks)]
+        for r in range(8):
+            in_col = in_ref[first + r]
+            out_col = out_ref[first + r]
+            updated = []
+            for c in range(chunks):
+                decay = jnp.exp(steps[c][r : r + 1] * rate_ref[:, pl.ds(c * LANES, LANES)])
+                state = decay * states[c] + drives[c][r : r + 1] * in_col
+                updated.append(state)
+                if with_read:
+                    reads[c].append(jnp.sum(out_col * state, axis=0, keepdims=True))
+            states = tuple(updated)
+        if with_read:
+            for c in range(chunks):
+                result_ref[pl.ds(first, 8), pl.ds(c * LANES, LANES)] = jnp.concatenate(reads[c], 0)
+        return states
+
+    states = tuple(init_ref[:, pl.ds(c * LANES, LANES)] for c in range(chunks))
+    states = lax.fori_loop(0, length // 8, body, states)
+    if not with_read:
+        for c in range(chunks):
+            result_ref[:, pl.ds(c * LANES, LANES)] = states[c]
+
+
+def run_scan(step, drive, rate, in_wide, out_wide, init, with_read):
+    length, channels = step.shape
+    entries = rate.shape[0]
+    rows_spec = pl.BlockSpec((length, CHANNEL_BLOCK), lambda j: (0, j))
+    state_spec = pl.BlockSpec((entries, CHANNEL_BLOCK), lambda j: (0, j))
+    wide_spec = pl.BlockSpec((length, entries, LANES), lambda j: (0, 0, 0))
+    shape = (length, channels) if with_read else (entries, channels)
+    return pl.pallas_call(
+        functools.partial(scan_kernel, with_read=with_read),
+        grid=(channels // CHANNEL_BLOCK,),
+        in_specs=[rows_spec, rows_spec, state_spec, wide_spec, wide_spec, state_spec],
+        out_specs=rows_spec if with_read else state_spec,
+        out_shape=jax.ShapeDtypeStruct(shape, jnp.float32),
+        interpret=INTERPRET,
+    )(step, drive, rate, in_wide, out_wide, init)
+
+
+def exchange(step_sum, local_end, rate):
+    count = lax.axis_size("seq")
+    entries, channels = local_end.shape
+    width = channels // count
+    packed = jnp.concatenate([step_sum[None], local_end], 0).reshape(entries + 1, count, width)
+    gathered = lax.all_to_all(packed, "seq", 1, 1, tiled=True)
+    sums = gathered[0]
+    ends = jnp.transpose(gathered[1:], (1, 0, 2))
+    me = lax.axis_index("seq")
+    rate_block = lax.dynamic_slice_in_dim(rate, me * width, width, 1)
+    place = jnp.arange(count)
+    between = (place[None, :, None] < place[None, None, :]) & (
+        place[None, None, :] < place[:, None, None]
+    )
+    gap = jnp.sum(jnp.where(between[..., None], sums[None, None], 0.0), axis=2)
+    before = place[None, :] < place[:, None]
+    weight = jnp.where(
+        before[:, :, None, None], jnp.exp(rate_block[None, None] * gap[:, :, None, :]), 0.0
+    )
+    incoming = jnp.sum(weight * ends[None], axis=1)
+    back = lax.all_to_all(jnp.transpose(incoming, (1, 0, 2)), "seq", 1, 1, tiled=True)
+    return back.reshape(entries, channels)
 
 
 def per_device(
@@ -87,33 +169,14 @@
         jnp.dot(step_low, step_proj, preferred_element_type=jnp.float32) + step_bias[None, :]
     )
     rate = -jnp.exp(decay_log)
-
-    def carry_only(state, row):
-        step_row, conv_row, in_row = row
-        state = (
-            jnp.exp(step_row[None, :] * rate) * state
-            + (step_row * conv_row)[None, :] * in_row[:, None]
-        )
-        return (state, None)
-
-    def with_read(state, row):
-        step_row, conv_row, in_row, out_row = row
-        state = (
-            jnp.exp(step_row[None, :] * rate) * state
-            + (step_row * conv_row)[None, :] * in_row[:, None]
-        )
-        return (state, jnp.sum(out_row[:, None] * state, axis=0))
-
+    drive = step * conv
+    length, entries = state_in.shape
+    in_wide = jnp.broadcast_to(state_in[:, :, None], (length, entries, LANES))
+    out_wide = jnp.broadcast_to(state_out[:, :, None], (length, entries, LANES))
     zero_state = jnp.zeros(rate.shape, jnp.float32)
-    local_end, unused = lax.scan(carry_only, zero_state, (step, conv, state_in), unroll=8)
-    decay_total = jnp.exp(rate * jnp.sum(step, axis=0)[None, :])
-
-    def hop(index, incoming):
-        leaving = decay_total * incoming + local_end
-        return shifted(leaving, "seq", 1)
-
-    incoming = lax.fori_loop(0, lax.axis_size("seq") - 1, hop, zero_state)
-    final, read = lax.scan(with_read, incoming, (step, conv, state_in, state_out), unroll=8)
+    local_end = run_scan(step, drive, rate, in_wide, out_wide, zero_state, False)
+    incoming = exchange(jnp.sum(step, axis=0), local_end, rate)
+    read = run_scan(step, drive, rate, in_wide, out_wide, incoming, True)
     mamba_out = (
         (read + skip_gain[None, :] * conv) * jax.nn.silu(inner_gate.astype(jnp.float32))
     ).astype(jnp.bfloat16)

time: 698 us -> 264 us (0.38)
  the two profiles are of different devices: /device:TPU:14 before, /device:TPU:16 now
where the time goes in v2:
time: 264 us; the launch traced here: 263 us
  waiting for transfers between devices  72.3 us (27%)
  local copies, waits for them, and re-layouts  47.6 us (18%)
  starting transfers between devices  45.5 us (17%)
  other arithmetic  39.3 us (15%)
  matrix products  29.7 us (11%)
  Pallas kernels  26.9 us (10%)
    all_to_all x1, waiting for transfers between devices, attend_by_heads(): lax.all_to_all(k_wide, 'seq', split_axis=1, concat_axis=0, tiled=True)  28 us
    pallas_call x2, Pallas kernels, run_scan(): pl.pallas_call(functools.partial(scan_kernel, with_read=with_read), grid=...  26.9 us
    all_to_all x1, waiting for transfers between devices, attend_by_heads(): lax.all_to_all(v_wide, 'seq', split_axis=1, concat_axis=0, tiled=True)  21.3 us
    all_to_all x1, waiting for transfers between devices, exchange(): gathered = lax.all_to_all(packed, 'seq', 1, 1, tiled=True)  14.2 us
    reduce_sum x8, other arithmetic, attend_by_heads(): total = jnp.sum(expo, axis=-1)  14.2 us
    dot_general x8, matrix products, attend_by_heads(): jnp.einsum('hij,jhd->ihd', expo.astype(jnp.bfloat16), v_all[:stop], prefe...  12.3 us
    unnamed x105, local copies, waits for them, and re-layouts  12.2 us
    all_to_all x1, starting transfers between devices, exchange(): gathered = lax.all_to_all(packed, 'seq', 1, 1, tiled=True)  10.5 us
  transfers between devices with their start and end apart: 7, of which 5 were waited for; matrix products, arithmetic and copies ran while one was open for 35% of the time, Pallas kernels for 6%

profile of v2, /device:TPU:16, one launch (start us, length us, event | category | flops | bytes accessed | tf_op | source)
XLA Modules:
  0.0 262.6 jit_solution(6051758102334353676)
XLA Ops:
  1.7 3.8 %collective-permute-start = (bf16[3,4096]{1,0:T(4,128)(2,1)S(1)}, bf16[3,4096]{1,0:T(4,128)(2,1)S(1)}, u32[]{:S(2)}, u32[]{:S(2)}) collective-permute-start(bf16[3,4096]{1,0:T(4,128)(2,1)S(1)} %slice.154), channel_id=1, source_target_pairs={{0,1},{1,2},{2,3},{3,4},{4,5},{5,6},{6,7},{7,8},{8,9},{9,10},{10,1... | collective-permute-start | bytes 73736 | tf_op jit(solution)/shard_map/ppermute | solution.py:19
  5.5 1.7 exponential_negate_fusion.rate_ref
  9.9 7.2 %fusion.164 = (f32[128,4096]{1,0:T(8,128)}, f32[128,4096]{1,0:T(8,128)}, f32[4096]{0:T(1024)S(1)}, f32[128,4096]{1,0:T(8,128)}) fusion(f32[4096]{0:T(1024)} %param.17, bf16[128,4096]{1,0:T(8,128)(2,1)} %param.14, f32[4096]{0:T(1024)S(1)} %bitcast.269, bf16[3,4096]{1,0:T(4,128)(2,1)S(1)} %collective-permute-done, f32[4096]{0:T(1024)S(1)} %bitcast.270, ...), kind=kOutput, calls=%fused_computation.152 | convolution fusion | flops 286257152 | bytes 9641984 | tf_op jit(solution)/shard_map/dot_general | solution.py:169
  17.1 1.3 broadcast_in_dim.100.out_ref
  18.4 1.3 broadcast_in_dim.99.in_ref
  20.4 10.4 %shard_map.149 = f32[16,4096]{1,0:T(8,128)} custom-call(f32[128,4096]{1,0:T(8,128)} %get-tuple-element.21.step_ref, f32[128,4096]{1,0:T(8,128)} %get-tuple-element.6.drive_ref, f32[16,4096]{1,0:T(8,128)} %exponential_negate_fusion.rate_ref, f32[128,16,128]{2,1,0:T(8,128)} %broadcast_in_dim.99.in_ref, f32[128,16,128]{2,1,0:T(8,128)} %broadcast_in_dim.100.out_ref, ...), custom_call_target="tpu_custom_call" | custom-call | tf_op jit(solution)/shard_map/pallas_call | solution.py:115
  32.6 10.5 %all-to-all-start = ((f32[17,32,128]{2,0,1:T(8,128)}), f32[17,32,128]{2,0,1:T(8,128)S(1)}, u32[]{:S(2)}, u32[]{:S(2)}) async-start(f32[17,32,128]{2,0,1:T(8,128)} %pad_maximum_fusion.1), calls=%async_computation | async-start | bytes 786432 | tf_op jit(solution)/shard_map/all_to_all | solution.py:130
  43.3 14.2 %all-to-all-done = f32[17,32,128]{2,0,1:T(8,128)S(1)} async-done(((f32[17,32,128]{2,0,1:T(8,128)}), f32[17,32,128]{2,0,1:T(8,128)S(1)}, u32[]{:S(2)}, u32[]{:S(2)}) %all-to-all-start) | async-done | bytes 278560 | tf_op jit(solution)/shard_map/all_to_all | solution.py:130
  58.7 5.1 %all-to-all-start.3 = ((bf16[128,32,128]{2,0,1:T(8,128)(2,1)}), bf16[128,32,128]{2,0,1:T(8,128)(2,1)S(1)}, u32[]{:S(2)}, u32[]{:S(2)}) async-start(bf16[128,32,128]{2,0,1:T(8,128)(2,1)} %bitcast.12), calls=%async_computation.3 | async-start | bytes 2097152 | tf_op jit(solution)/shard_map/all_to_all | solution.py:40
  63.9 28.0 %all-to-all-done.3 = bf16[128,32,128]{2,0,1:T(8,128)(2,1)S(1)} async-done(((bf16[128,32,128]{2,0,1:T(8,128)(2,1)}), bf16[128,32,128]{2,0,1:T(8,128)(2,1)S(1)}, u32[]{:S(2)}, u32[]{:S(2)}) %all-to-all-start.3) | async-done | bytes 1048608 | tf_op jit(solution)/shard_map/all_to_all | solution.py:40
  92.0 1.3 broadcast_in_dim.178
  93.2 4.9 %all-to-all-start.4 = ((bf16[128,32,128]{2,0,1:T(8,128)(2,1)}), bf16[128,32,128]{2,0,1:T(8,128)(2,1)S(1)}, u32[]{:S(2)}, u32[]{:S(2)}) async-start(bf16[128,32,128]{2,0,1:T(8,128)(2,1)} %bitcast.16), calls=%async_computation.4 | async-start | bytes 2097152 | tf_op jit(solution)/shard_map/all_to_all | solution.py:41
  98.1 1.3 copy.96
  105.0 21.3 %all-to-all-done.4 = bf16[128,32,128]{2,0,1:T(8,128)(2,1)S(1)} async-done(((bf16[128,32,128]{2,0,1:T(8,128)(2,1)}), bf16[128,32,128]{2,0,1:T(8,128)(2,1)S(1)}, u32[]{:S(2)}, u32[]{:S(2)}) %all-to-all-start.4) | async-done | bytes 1048608 | tf_op jit(solution)/shard_map/all_to_all | solution.py:41
  126.4 4.9 %all-to-all-start.2 = ((bf16[128,32,128]{0,2,1:T(8,128)(2,1)}), bf16[128,32,128]{0,2,1:T(8,128)(2,1)S(1)}, u32[]{:S(2)}, u32[]{:S(2)}) async-start(bf16[128,32,128]{0,2,1:T(8,128)(2,1)} %bitcast.8), calls=%async_computation.2 | async-start | bytes 2097152 | tf_op jit(solution)/shard_map/all_to_all | solution.py:39
  133.9 7.2 %select_reduce_fusion = f32[32,32,128]{2,1,0:T(8,128)S(1)} fusion(f32[32,128]{1,0:T(8,128)S(1)} %bitcast.266, pred[32,32,32]{2,1,0:T(8,128)(4,1)S(1)} %broadcast_and_fusion), kind=kLoop, calls=%fused_computation | loop fusion | flops 8257536 | bytes 573440 | tf_op jit(solution)/shard_map/reduce_sum | solution.py:139
  141.0 3.0 %multiply_reduce_fusion = f32[32,16,128]{2,1,0:T(8,128)} fusion(f32[32,16,128]{2,1,0:T(8,128)S(1)} %slice_bitcast_fusion, f32[32,32,128]{2,1,0:T(8,128)S(1)} %select_reduce_fusion, f32[16,128]{1,0:T(8,128)S(1)} %constant_dynamic-slice_fusion, pred[32,32]{1,0:T(8,128)(4,1)S(1)} %get-tuple-element.39), kind=kLoop, calls=%fused_computation.6 | loop fusion | flops 8323072 | bytes 1057792 | tf_op jit(solution)/shard_map/reduce_sum | solution.py:144
  156.1 3.5 %all-to-all-done.2 = bf16[128,32,128]{0,2,1:T(8,128)(2,1)S(1)} async-done(((bf16[128,32,128]{0,2,1:T(8,128)(2,1)}), bf16[128,32,128]{0,2,1:T(8,128)(2,1)S(1)}, u32[]{:S(2)}, u32[]{:S(2)}) %all-to-all-start.2) | async-done | bytes 1048608 | tf_op jit(solution)/shard_map/all_to_all | solution.py:39
  159.6 6.6 %all-to-all-start.1 = ((f32[16,32,128]{2,0,1:T(8,128)}), f32[16,32,128]{2,0,1:T(8,128)}, u32[]{:S(2)}, u32[]{:S(2)}) async-start(f32[16,32,128]{2,0,1:T(8,128)} %bitcast.7), calls=%async_computation.1 | async-start | bytes 524288 | tf_op jit(solution)/shard_map/all_to_all | solution.py:145
  168.1 1.7 copy.100
  169.7 1.7 copy.101
  171.4 1.7 copy.102
  173.1 1.7 copy.103
  176.4 1.3 fusion.167
  178.7 1.4 fusion.61
  180.1 1.5 fusion.30
  181.7 1.3 fusion.34
  183.7 1.4 fusion.21
  186.0 1.8 fusion.19
  189.0 1.8 fusion.8
  192.0 2.3 fusion.10
  194.3 1.4 fusion.170
  195.8 1.9 fusion.1
  197.7 2.0 fusion
  199.8 2.8 %fusion.4 = f32[512]{0:T(512)S(1)} fusion(f32[512,4096]{1,0:T(8,128)S(1)} %get-tuple-element.37, f32[512]{0:T(512)S(1)} %get-tuple-element.36, s32[512]{0:T(512)S(1)} %copy-done.29), kind=kLoop, calls=%fused_computation.19 | loop fusion | flops 12582400 | bytes 8394752 | tf_op jit(solution)/shard_map/reduce_sum | solution.py:63
  206.8 2.2 fusion.95
  209.0 2.0 fusion.71
  211.0 3.2 %fusion.119 = bf16[4096,1,128]{2,0,1:T(8,128)(2,1)S(1)} fusion(bf16[4096,1,128]{2,0,1:T(8,128)(2,1)S(1)} %fusion.71, bf16[4096,128]{1,0:T(8,128)(2,1)S(1)} %bitcast.232, f32[512,4096]{1,0:T(8,128)S(1)} %get-tuple-element.37, f32[512]{0:T(512)S(1)} %get-tuple-element.36, s32[512]{0:T(512)S(1)} %copy-done.29, f32[512]{0:T(512)S(1)} %fusion.4), kind=kOutput, calls=%fused_computation.91 | convolution fusion | flops 549584896 | bytes 9574400 | tf_op jit(solution)/shard_map/hij,jhd->ihd/dot_general | solution.py:64
  214.7 1.4 reduce.32
  217.3 9.5 %all-to-all-start.5 = ((bf16[32,2,8192]{2,1,0:T(2,128)(2,1)}), bf16[32,2,8192]{2,1,0:T(2,128)(2,1)S(1)}, u32[]{:S(2)}, u32[]{:S(2)}) async-start(bf16[32,2,8192]{2,1,0:T(2,128)(2,1)} %reshape.425), calls=%async_computation.5 | async-start | bytes 2097152 | tf_op jit(solution)/shard_map/all_to_all | solution.py:72
  226.9 1.7 copy_bitcast_fusion.init_ref
  228.5 16.5 %shard_map.150 = f32[128,4096]{1,0:T(8,128)} custom-call(f32[128,4096]{1,0:T(8,128)} %get-tuple-element.21.step_ref, f32[128,4096]{1,0:T(8,128)} %get-tuple-element.6.drive_ref, f32[16,4096]{1,0:T(8,128)} %exponential_negate_fusion.rate_ref, f32[128,16,128]{2,1,0:T(8,128)} %broadcast_in_dim.99.in_ref, f32[128,16,128]{2,1,0:T(8,128)} %broadcast_in_dim.100.out_ref, ...), custom_call_target="tpu_custom_call" | custom-call | tf_op jit(solution)/shard_map/pallas_call | solution.py:115
  245.0 3.6 %fusion.27 = bf16[128,4096]{1,0:T(8,128)(2,1)} fusion(bf16[128,4096]{1,0:T(8,128)(2,1)} %param.15, f32[128,4096]{1,0:T(8,128)} %shard_map.150, f32[128,4096]{1,0:T(8,128)S(1)} %copy-done.2, f32[4096]{0:T(1024)S(1)} %copy-done.27), kind=kLoop, calls=%fused_computation.46 | loop fusion | flops 4718592 | bytes 6307840 | tf_op jit(solution)/shard_map/convert_element_type | solution.py:182
  248.6 5.3 %all-to-all-done.5 = bf16[32,2,8192]{2,1,0:T(2,128)(2,1)S(1)} async-done(((bf16[32,2,8192]{2,1,0:T(2,128)(2,1)}), bf16[32,2,8192]{2,1,0:T(2,128)(2,1)S(1)}, u32[]{:S(2)}, u32[]{:S(2)}) %all-to-all-start.5) | async-done | bytes 1048608 | tf_op jit(solution)/shard_map/all_to_all | solution.py:72
  253.8 3.5 %reshape.426 = bf16[4096,1,128]{2,1,0:T(2,128)(2,1)} reshape(bf16[32,2,8192]{2,1,0:T(2,128)(2,1)S(1)} %all-to-all-done.5) | data formatting | bytes 2097152
  257.3 1.7 copy.110
  259.0 1.3 copy.108
  260.4 2.3 copy.109
  (159 shorter events, 42.1 us)
Async XLA Ops:
  0.6 9.2 %copy-start = (bf16[256,4096]{1,0:T(8,128)(2,1)S(1)}, bf16[256,4096]{1,0:T(8,128)(2,1)}, u32[]{:S(2)}) copy-start(bf16[256,4096]{1,0:T(8,128)(2,1)} %param.19) | copy-start | bytes 6291460
  1.7 8.2 %collective-permute-start = (bf16[3,4096]{1,0:T(4,128)(2,1)S(1)}, bf16[3,4096]{1,0:T(4,128)(2,1)S(1)}, u32[]{:S(2)}, u32[]{:S(2)}) collective-permute-start(bf16[3,4096]{1,0:T(4,128)(2,1)S(1)} %slice.154), channel_id=1, source_target_pairs={{0,1},{1,2},{2,3},{3,4},{4,5},{5,6},{6,7},{7,8},{8,9},{9,10},{10,1... | collective-permute-start | bytes 73736 | tf_op jit(solution)/shard_map/ppermute | solution.py:19
  20.4 22.8 %copy-start.14 = (bf16[128,1024]{1,0:T(8,128)(2,1)S(1)}, bf16[128,1024]{1,0:T(8,128)(2,1)}, u32[]{:S(2)}) copy-start(bf16[128,1024]{1,0:T(8,128)(2,1)} %param.26) | copy-start | bytes 786436
  30.8 33.0 %copy-start.15 = (bf16[128,1024]{1,0:T(8,128)(2,1)S(1)}, bf16[128,1024]{1,0:T(8,128)(2,1)}, u32[]{:S(2)}) copy-start(bf16[128,1024]{1,0:T(8,128)(2,1)} %param.27) | copy-start | bytes 786436
  32.6 65.5 %copy-start.3 = (bf16[128,4096]{1,0:T(8,128)(2,1)S(1)}, bf16[128,4096]{1,0:T(8,128)(2,1)}, u32[]{:S(2)}) copy-start(bf16[128,4096]{1,0:T(8,128)(2,1)} %param.25) | copy-start | bytes 3145732
  32.6 24.8 %all-to-all-start = ((f32[17,32,128]{2,0,1:T(8,128)}), f32[17,32,128]{2,0,1:T(8,128)S(1)}, u32[]{:S(2)}, u32[]{:S(2)}) async-start(f32[17,32,128]{2,0,1:T(8,128)} %pad_maximum_fusion.1), calls=%async_computation | async-start | bytes 786432 | tf_op jit(solution)/shard_map/all_to_all | solution.py:130
  58.7 33.2 %all-to-all-start.3 = ((bf16[128,32,128]{2,0,1:T(8,128)(2,1)}), bf16[128,32,128]{2,0,1:T(8,128)(2,1)S(1)}, u32[]{:S(2)}, u32[]{:S(2)}) async-start(bf16[128,32,128]{2,0,1:T(8,128)(2,1)} %bitcast.12), calls=%async_computation.3 | async-start | bytes 2097152 | tf_op jit(solution)/shard_map/all_to_all | solution.py:40
  93.2 33.2 %all-to-all-start.4 = ((bf16[128,32,128]{2,0,1:T(8,128)(2,1)}), bf16[128,32,128]{2,0,1:T(8,128)(2,1)S(1)}, u32[]{:S(2)}, u32[]{:S(2)}) async-start(bf16[128,32,128]{2,0,1:T(8,128)(2,1)} %bitcast.16), calls=%async_computation.4 | async-start | bytes 2097152 | tf_op jit(solution)/shard_map/all_to_all | solution.py:41
  126.4 33.2 %all-to-all-start.2 = ((bf16[128,32,128]{0,2,1:T(8,128)(2,1)}), bf16[128,32,128]{0,2,1:T(8,128)(2,1)S(1)}, u32[]{:S(2)}, u32[]{:S(2)}) async-start(bf16[128,32,128]{0,2,1:T(8,128)(2,1)} %bitcast.8), calls=%async_computation.2 | async-start | bytes 2097152 | tf_op jit(solution)/shard_map/all_to_all | solution.py:39
  159.6 57.7 %all-to-all-start.1 = ((f32[16,32,128]{2,0,1:T(8,128)}), f32[16,32,128]{2,0,1:T(8,128)}, u32[]{:S(2)}, u32[]{:S(2)}) async-start(f32[16,32,128]{2,0,1:T(8,128)} %bitcast.7), calls=%async_computation.1 | async-start | bytes 524288 | tf_op jit(solution)/shard_map/all_to_all | solution.py:145
  167.1 13.0 %copy-start.28 = (s32[1024]{0:T(1024)S(1)}, s32[1024]{0:T(1024)}, u32[]{:S(2)}) copy-start(s32[1024]{0:T(1024)} %iota_add_fusion.5) | copy-start | bytes 12292
  167.1 13.0 %copy-start.33 = (s32[512]{0:T(512)S(1)}, s32[512]{0:T(512)}, u32[]{:S(2)}) copy-start(s32[512]{0:T(512)} %iota_add_fusion.13) | copy-start | bytes 6148
  176.4 3.7 %copy-start.22 = (bf16[4,128,1,128]{3,1,0,2:T(8,128)(2,1)S(1)}, bf16[4,128,1,128]{3,1,0,2:T(8,128)(2,1)}, u32[]{:S(2)}) copy-start(bf16[4,128,1,128]{3,1,0,2:T(8,128)(2,1)} %copy.100) | copy-start | bytes 393220
  177.7 5.2 %copy-start.13 = (bf16[12,128,1,128]{3,1,0,2:T(8,128)(2,1)S(1)}, bf16[12,128,1,128]{3,1,0,2:T(8,128)(2,1)}, u32[]{:S(2)}) copy-start(bf16[12,128,1,128]{3,1,0,2:T(8,128)(2,1)} %slice.205) | copy-start | bytes 1179652
  177.7 5.2 %copy-start.21 = (bf16[4,128,1,128]{3,1,0,2:T(8,128)(2,1)S(1)}, bf16[4,128,1,128]{3,1,0,2:T(8,128)(2,1)}, u32[]{:S(2)}) copy-start(bf16[4,128,1,128]{3,1,0,2:T(8,128)(2,1)} %copy.101) | copy-start | bytes 393220
  177.7 5.2 %copy-start.26 = (s32[1536]{0:T(1024)S(1)}, s32[1536]{0:T(1024)}, u32[]{:S(2)}) copy-start(s32[1536]{0:T(1024)} %iota_add_fusion.4) | copy-start | bytes 18436
  177.7 5.2 %copy-start.34 = (s32[512]{0:T(512)S(1)}, s32[512]{0:T(512)}, u32[]{:S(2)}) copy-start(s32[512]{0:T(512)} %iota_add_fusion.12) | copy-start | bytes 6148
  181.6 3.4 %copy-start.41 = (f32[512]{0:T(512)}, f32[512]{0:T(512)S(1)}, u32[]{:S(2)}) copy-start(f32[512]{0:T(512)S(1)} %get-tuple-element.24) | copy-start | bytes 6148
  181.6 3.4 %copy-start.11 = (bf16[16,128,1,128]{3,1,0,2:T(8,128)(2,1)S(1)}, bf16[16,128,1,128]{3,1,0,2:T(8,128)(2,1)}, u32[]{:S(2)}) copy-start(bf16[16,128,1,128]{3,1,0,2:T(8,128)(2,1)} %slice.208) | copy-start | bytes 1572868
  181.6 3.4 %copy-start.20 = (bf16[4,128,1,128]{3,1,0,2:T(8,128)(2,1)S(1)}, bf16[4,128,1,128]{3,1,0,2:T(8,128)(2,1)}, u32[]{:S(2)}) copy-start(bf16[4,128,1,128]{3,1,0,2:T(8,128)(2,1)} %copy.102) | copy-start | bytes 393220
  181.6 3.4 %copy-start.25 = (s32[2048]{0:T(1024)S(1)}, s32[2048]{0:T(1024)}, u32[]{:S(2)}) copy-start(s32[2048]{0:T(1024)} %iota_add_fusion.3) | copy-start | bytes 24580
  181.6 3.4 %copy-start.32 = (s32[512]{0:T(512)S(1)}, s32[512]{0:T(512)}, u32[]{:S(2)}) copy-start(s32[512]{0:T(512)} %iota_add_fusion.11) | copy-start | bytes 6148
  183.7 1.4 copy-start.46
  185.1 2.8 %copy-start.9 = (bf16[20,128,1,128]{3,1,0,2:T(8,128)(2,1)S(1)}, bf16[20,128,1,128]{3,1,0,2:T(8,128)(2,1)}, u32[]{:S(2)}) copy-start(bf16[20,128,1,128]{3,1,0,2:T(8,128)(2,1)} %slice.211) | copy-start | bytes 1966084
  185.1 2.8 %copy-start.19 = (bf16[4,128,1,128]{3,1,0,2:T(8,128)(2,1)S(1)}, bf16[4,128,1,128]{3,1,0,2:T(8,128)(2,1)}, u32[]{:S(2)}) copy-start(bf16[4,128,1,128]{3,1,0,2:T(8,128)(2,1)} %copy.103) | copy-start | bytes 393220
  185.1 2.8 %copy-start.23 = (s32[2560]{0:T(1024)S(1)}, s32[2560]{0:T(1024)}, u32[]{:S(2)}) copy-start(s32[2560]{0:T(1024)} %iota_add_fusion.2) | copy-start | bytes 30724
  185.1 2.8 %copy-start.31 = (s32[512]{0:T(512)S(1)}, s32[512]{0:T(512)}, u32[]{:S(2)}) copy-start(s32[512]{0:T(512)} %iota_add_fusion.10) | copy-start | bytes 6148
  186.0 1.8 copy-start.39
  188.9 3.1 %copy-start.37 = (f32[512]{0:T(512)}, f32[512]{0:T(512)S(1)}, u32[]{:S(2)}) copy-start(f32[512]{0:T(512)S(1)} %get-tuple-element.30) | copy-start | bytes 6148
  188.9 1.8 copy-start.7
  188.9 1.8 copy-start.18
  188.9 1.8 copy-start.24
  189.0 1.8 copy-start.30
  192.0 2.3 copy-start.5
  192.0 2.3 copy-start.17
  192.0 2.3 copy-start.36
  195.8 1.9 copy-start.29
  199.8 2.9 %copy-start.16 = (bf16[8,128,1,128]{3,1,0,2:T(8,128)(2,1)S(1)}, bf16[8,128,1,128]{3,1,0,2:T(8,128)(2,1)}, u32[]{:S(2)}) copy-start(bf16[8,128,1,128]{3,1,0,2:T(8,128)(2,1)} %slice.203) | copy-start | bytes 786436
  199.8 2.9 %copy-start.42 = (f32[512]{0:T(512)S(1)}, f32[512]{0:T(512)}, u32[]{:S(2)}) copy-start(f32[512]{0:T(512)} %copy-done.41) | copy-start | bytes 6148
  199.8 2.9 %copy-start.45 = (f32[512]{0:T(512)S(1)}, f32[512]{0:T(512)}, u32[]{:S(2)}) copy-start(f32[512]{0:T(512)} %fusion.34) | copy-start | bytes 6148
  204.5 1.2 copy-start.8
  204.5 1.2 copy-start.38
  204.5 1.2 copy-start.43
  206.8 2.2 copy-start.4
  217.3 36.5 %all-to-all-start.5 = ((bf16[32,2,8192]{2,1,0:T(2,128)(2,1)}), bf16[32,2,8192]{2,1,0:T(2,128)(2,1)S(1)}, u32[]{:S(2)}, u32[]{:S(2)}) async-start(bf16[32,2,8192]{2,1,0:T(2,128)(2,1)} %reshape.425), calls=%async_computation.5 | async-start | bytes 2097152 | tf_op jit(solution)/shard_map/all_to_all | solution.py:72
  228.5 16.5 %copy-start.2 = (f32[128,4096]{1,0:T(8,128)S(1)}, f32[128,4096]{1,0:T(8,128)}, u32[]{:S(2)}) copy-start(f32[128,4096]{1,0:T(8,128)} %get-tuple-element.7) | copy-start | bytes 6291460
  228.5 16.5 %copy-start.27 = (f32[4096]{0:T(1024)S(1)}, f32[4096]{0:T(1024)}, u32[]{:S(2)}) copy-start(f32[4096]{0:T(1024)} %param.24) | copy-start | bytes 49156
  253.8 8.8 %copy-start.1 = (bf16[256,4096]{1,0:T(8,128)(2,1)S(1)}, bf16[256,4096]{1,0:T(8,128)(2,1)}, u32[]{:S(2)}) copy-start(bf16[256,4096]{1,0:T(8,128)(2,1)} %param.19) | copy-start | bytes 6291460
  (8 other events, 8.3 us)

commit v3 on v2

--- a/solution.py
+++ b/solution.py
@@ -35,11 +35,12 @@
     group = q_three.shape[1] // k_three.shape[1]
     k_wide = jnp.repeat(k_three, group, axis=1)
     v_wide = jnp.repeat(v_three, group, axis=1)
-    q_all, k_all, v_all = (
-        lax.all_to_all(q_three, "seq", split_axis=1, concat_axis=0, tiled=True),
-        lax.all_to_all(k_wide, "seq", split_axis=1, concat_axis=0, tiled=True),
-        lax.all_to_all(v_wide, "seq", split_axis=1, concat_axis=0, tiled=True),
-    )
+    joined = lax.all_to_all(
+        jnp.concatenate([q_three, k_wide, v_wide], 2), "seq", split_axis=1, concat_axis=0, tiled=True
+    )
+    q_all = joined[:, :, :HEAD_DIM]
+    k_all = joined[:, :, HEAD_DIM : 2 * HEAD_DIM]
+    v_all = joined[:, :, 2 * HEAD_DIM :]
     length = q_all.shape[0]
     width = math.gcd(length, 512)
     scale = HEAD_DIM ** (-0.5)

time: 264 us -> 228 us (0.86)
  local copies, waits for them, and re-layouts: 47.6 us -> 25 us
  starting transfers between devices: 45.5 us -> 34.2 us
    slice x23 -> x0, local copies, waits for them, and re-layouts: 22.2 us -> none  [the longest x9 10.2 us: attend_by_heads(): query_block = q_all[stop - width:stop]]
    all_to_all x3 -> x1, starting transfers between devices: 14.9 us -> 5.11 us  [attend_by_heads(): lax.all_to_all(jnp.concatenate([q_three, k_wide, v_wide], 2), 'seq', spli...]
    all_to_all x1, waiting for transfers between devices: 14.2 us -> 11 us  [exchange(): gathered = lax.all_to_all(packed, 'seq', 1, 1, tiled=True)]
    reduce_sum x8, other arithmetic: 14.2 us -> 11.3 us  [attend_by_heads(): total = jnp.sum(expo, axis=-1)]
    all_to_all x0 -> x1, local copies, waits for them, and re-layouts: none -> 2.81 us  [attend_by_heads(): lax.all_to_all(jnp.concatenate([q_three, k_wide, v_wide], 2), 'seq', spli...]
    all_to_all x3 -> x1, waiting for transfers between devices: 52.9 us -> 55.4 us  [attend_by_heads(): lax.all_to_all(jnp.concatenate([q_three, k_wide, v_wide], 2), 'seq', spli...]
    unnamed x105 -> x50, local copies, waits for them, and re-layouts: 12.2 us -> 11.6 us
  transfers between devices with their start and end apart: 7 -> 5, of which waited for: 5 -> 3; matrix products, arithmetic and copies ran while one was open for 35% -> 31% of each run, Pallas kernels for 6% -> 7%
where the time goes in v3:
time: 228 us; the launch traced here: 227 us
  waiting for transfers between devices  72.8 us (32%)
  other arithmetic  38.3 us (17%)
  starting transfers between devices  34.2 us (15%)
  matrix products  28.6 us (13%)
  Pallas kernels  26.9 us (12%)
  local copies, waits for them, and re-layouts  25 us (11%)
    all_to_all x1, waiting for transfers between devices, attend_by_heads(): lax.all_to_all(jnp.concatenate([q_three, k_wide, v_wide], 2), 'seq', spli...  55.4 us
    pallas_call x2, Pallas kernels, run_scan(): pl.pallas_call(functools.partial(scan_kernel, with_read=with_read), grid=...  26.9 us
    dot_general x8, matrix products, attend_by_heads(): jnp.einsum('hij,jhd->ihd', expo.astype(jnp.bfloat16), v_all[:stop], prefe...  12.3 us
    unnamed x50, local copies, waits for them, and re-layouts  11.6 us
    reduce_sum x8, other arithmetic, attend_by_heads(): total = jnp.sum(expo, axis=-1)  11.3 us
    all_to_all x1, waiting for transfers between devices, exchange(): gathered = lax.all_to_all(packed, 'seq', 1, 1, tiled=True)  11 us
    all_to_all x1, starting transfers between devices, exchange(): gathered = lax.all_to_all(packed, 'seq', 1, 1, tiled=True)  10.4 us
    all_to_all x1, starting transfers between devices, attend_by_heads(): lax.all_to_all(merged, 'seq', split_axis=0, concat_axis=1, tiled=True)  9.78 us
  transfers between devices with their start and end apart: 5, of which 3 were waited for; matrix products, arithmetic and copies ran while one was open for 31% of the time, Pallas kernels for 7%

profile of v3, /device:TPU:16, one launch (start us, length us, event | category | flops | bytes accessed | tf_op | source)
XLA Modules:
  0.0 226.9 jit_solution(7680000613218634974)
XLA Ops:
  0.6 1.0 slice.161
  1.7 3.8 %collective-permute-start = (bf16[3,4096]{1,0:T(4,128)(2,1)S(1)}, bf16[3,4096]{1,0:T(4,128)(2,1)S(1)}, u32[]{:S(2)}, u32[]{:S(2)}) collective-permute-start(bf16[3,4096]{1,0:T(4,128)(2,1)S(1)} %slice.161), channel_id=1, source_target_pairs={{0,1},{1,2},{2,3},{3,4},{4,5},{5,6},{6,7},{7,8},{8,9},{9,10},{10,1... | collective-permute-start | bytes 73736 | tf_op jit(solution)/shard_map/ppermute | solution.py:19
  5.5 1.7 exponential_negate_fusion.rate_ref
  7.2 1.1 fusion.169
  8.2 0.8 copy.65
  9.9 7.1 %fusion.168 = (f32[128,4096]{1,0:T(8,128)}, f32[128,4096]{1,0:T(8,128)}, f32[4096]{0:T(1024)S(1)}, f32[128,4096]{1,0:T(8,128)}) fusion(f32[4096]{0:T(1024)} %param.17, bf16[128,4096]{1,0:T(8,128)(2,1)} %param.14, f32[4096]{0:T(1024)S(1)} %bitcast.278, bf16[3,4096]{1,0:T(4,128)(2,1)S(1)} %collective-permute-done, f32[4096]{0:T(1024)S(1)} %bitcast.279, ...), kind=kOutput, calls=%fused_computation.179 | convolution fusion | flops 286257152 | bytes 9641984 | tf_op jit(solution)/shard_map/dot_general | solution.py:170
  17.0 1.3 broadcast_in_dim.100.out_ref
  18.3 1.3 broadcast_in_dim.99.in_ref
  20.3 10.4 %shard_map.149 = f32[16,4096]{1,0:T(8,128)} custom-call(f32[128,4096]{1,0:T(8,128)} %get-tuple-element.13.step_ref, f32[128,4096]{1,0:T(8,128)} %get-tuple-element.6.drive_ref, f32[16,4096]{1,0:T(8,128)} %exponential_negate_fusion.rate_ref, f32[128,16,128]{2,1,0:T(8,128)} %broadcast_in_dim.99.in_ref, f32[128,16,128]{2,1,0:T(8,128)} %broadcast_in_dim.100.out_ref, ...), custom_call_target="tpu_custom_call" | custom-call | tf_op jit(solution)/shard_map/pallas_call | solution.py:116
  30.8 1.1 copy_bitcast_fusion.1
  32.6 10.4 %all-to-all-start = ((f32[17,32,128]{2,0,1:T(8,128)}), f32[17,32,128]{2,0,1:T(8,128)S(1)}, u32[]{:S(2)}, u32[]{:S(2)}) async-start(f32[17,32,128]{2,0,1:T(8,128)} %pad_maximum_fusion.2), calls=%async_computation | async-start | bytes 786432 | tf_op jit(solution)/shard_map/all_to_all | solution.py:131
  44.6 1.8 pad_maximum_fusion
  46.4 11.0 %all-to-all-done = f32[17,32,128]{2,0,1:T(8,128)S(1)} async-done(((f32[17,32,128]{2,0,1:T(8,128)}), f32[17,32,128]{2,0,1:T(8,128)S(1)}, u32[]{:S(2)}, u32[]{:S(2)}) %all-to-all-start) | async-done | bytes 278560 | tf_op jit(solution)/shard_map/all_to_all | solution.py:131
  57.3 5.1 %all-to-all-start.2 = ((bf16[128,32,384]{0,2,1:T(8,128)(2,1)}), bf16[128,32,384]{0,2,1:T(8,128)(2,1)S(1)}, u32[]{:S(2)}, u32[]{:S(2)}) async-start(bf16[128,32,384]{0,2,1:T(8,128)(2,1)} %pad_maximum_fusion), calls=%async_computation.2 | async-start | bytes 6291456 | tf_op jit(solution)/shard_map/all_to_all | solution.py:38
  70.8 7.2 %select_reduce_fusion = f32[32,32,128]{2,1,0:T(8,128)S(1)} fusion(f32[32,128]{1,0:T(8,128)S(1)} %bitcast.275, pred[32,32,32]{2,1,0:T(8,128)(4,1)S(1)} %broadcast_and_fusion), kind=kLoop, calls=%fused_computation | loop fusion | flops 8257536 | bytes 573440 | tf_op jit(solution)/shard_map/reduce_sum | solution.py:140
  77.9 3.0 %multiply_reduce_fusion = f32[32,16,128]{2,1,0:T(8,128)} fusion(f32[32,16,128]{2,1,0:T(8,128)S(1)} %slice_bitcast_fusion.28, f32[32,32,128]{2,1,0:T(8,128)S(1)} %select_reduce_fusion, f32[16,128]{1,0:T(8,128)S(1)} %constant_dynamic-slice_fusion, pred[32,32]{1,0:T(8,128)(4,1)S(1)} %get-tuple-element.31), kind=kLoop, calls=%fused_computation.6 | loop fusion | flops 8323072 | bytes 1057792 | tf_op jit(solution)/shard_map/reduce_sum | solution.py:145
  81.0 55.4 %all-to-all-done.2 = bf16[128,32,384]{0,2,1:T(8,128)(2,1)S(1)} async-done(((bf16[128,32,384]{0,2,1:T(8,128)(2,1)}), bf16[128,32,384]{0,2,1:T(8,128)(2,1)S(1)}, u32[]{:S(2)}, u32[]{:S(2)}) %all-to-all-start.2) | async-done | bytes 3145760 | tf_op jit(solution)/shard_map/all_to_all | solution.py:38
  136.4 5.1 %all-to-all-start.1 = ((f32[16,32,128]{2,0,1:T(8,128)}), f32[16,32,128]{2,0,1:T(8,128)S(1)}, u32[]{:S(2)}, u32[]{:S(2)}) async-start(f32[16,32,128]{2,0,1:T(8,128)} %bitcast.274), calls=%async_computation.1 | async-start | bytes 524288 | tf_op jit(solution)/shard_map/all_to_all | solution.py:146
  141.5 2.8 %copy.71 = bf16[32,128,1,384]{3,1,0,2:T(8,128)(2,1)} copy(bf16[32,128,1,384]{1,3,0,2:T(8,128)(2,1)S(1)} %bitcast.250) | data formatting | bytes 6291456 | tf_op jit(solution)/shard_map/all_to_all | solution.py:38
  144.3 1.4 fusion.170
  146.0 1.3 fusion.61
  147.4 1.7 fusion
  150.4 0.8 fusion.57
  152.8 0.9 fusion.131
  153.7 0.9 fusion.14
  154.6 1.3 fusion.19
  155.9 1.4 fusion.107
  157.3 1.1 fusion.172
  158.3 1.2 fusion.8
  159.6 1.5 fusion.83
  161.1 1.3 fusion.3
  162.4 2.0 fusion.10
  164.4 1.9 fusion.95
  166.4 1.4 fusion.173
  167.8 2.0 fusion.1
  169.8 1.7 fusion.71
  171.5 3.1 %fusion.4 = f32[512]{0:T(512)S(1)} fusion(f32[512,4096]{1,0:T(8,128)S(1)} %get-tuple-element.29, f32[512]{0:T(512)S(1)} %get-tuple-element.28, s32[512]{0:T(512)S(1)} %copy-done.13), kind=kLoop, calls=%fused_computation.19 | loop fusion | flops 12582400 | bytes 8394752 | tf_op jit(solution)/shard_map/reduce_sum | solution.py:64
  174.6 2.7 %fusion.119 = bf16[4096,1,128]{0,2,1:T(8,128)(2,1)S(1)} fusion(bf16[4096,1,128]{0,2,1:T(8,128)(2,1)S(1)} %fusion.71, f32[512,4096]{1,0:T(8,128)S(1)} %get-tuple-element.29, f32[512]{0:T(512)S(1)} %get-tuple-element.28, s32[512]{0:T(512)S(1)} %copy-done.13, bf16[4096,1,384]{2,0,1:T(8,128)(2,1)S(1)} %bitcast.271, f32[512]{0:T(512)S(1)} %fusion.4), kind=kOutput, calls=%fused_computation.92 | convolution fusion | flops 549584896 | bytes 9574400 | tf_op jit(solution)/shard_map/hij,jhd->ihd/dot_general | solution.py:65
  178.0 1.5 reduce.32
  180.1 1.1 reshape.379
  181.2 9.8 %all-to-all-start.3 = ((bf16[32,2,8192]{2,1,0:T(2,128)(2,1)}), bf16[32,2,8192]{2,1,0:T(2,128)(2,1)S(1)}, u32[]{:S(2)}, u32[]{:S(2)}) async-start(bf16[32,2,8192]{2,1,0:T(2,128)(2,1)} %reshape.379), calls=%async_computation.3 | async-start | bytes 2097152 | tf_op jit(solution)/shard_map/all_to_all | solution.py:73
  191.7 16.4 %shard_map.150 = f32[128,4096]{1,0:T(8,128)} custom-call(f32[128,4096]{1,0:T(8,128)} %get-tuple-element.13.step_ref, f32[128,4096]{1,0:T(8,128)} %get-tuple-element.6.drive_ref, f32[16,4096]{1,0:T(8,128)} %exponential_negate_fusion.rate_ref, f32[128,16,128]{2,1,0:T(8,128)} %broadcast_in_dim.99.in_ref, f32[128,16,128]{2,1,0:T(8,128)} %broadcast_in_dim.100.out_ref, ...), custom_call_target="tpu_custom_call" | custom-call | tf_op jit(solution)/shard_map/pallas_call | solution.py:116
  208.2 3.6 %fusion.27 = bf16[128,4096]{1,0:T(8,128)(2,1)} fusion(bf16[128,4096]{1,0:T(8,128)(2,1)} %param.15, f32[128,4096]{1,0:T(8,128)} %shard_map.150, f32[128,4096]{1,0:T(8,128)S(1)} %copy-done.3, f32[4096]{0:T(1024)S(1)} %copy-done.11), kind=kLoop, calls=%fused_computation.47 | loop fusion | flops 4718592 | bytes 6307840 | tf_op jit(solution)/shard_map/convert_element_type | solution.py:183
  211.7 6.4 %all-to-all-done.3 = bf16[32,2,8192]{2,1,0:T(2,128)(2,1)S(1)} async-done(((bf16[32,2,8192]{2,1,0:T(2,128)(2,1)}), bf16[32,2,8192]{2,1,0:T(2,128)(2,1)S(1)}, u32[]{:S(2)}, u32[]{:S(2)}) %all-to-all-start.3) | async-done | bytes 1048608 | tf_op jit(solution)/shard_map/all_to_all | solution.py:73
  218.1 3.5 %reshape.380 = bf16[4096,1,128]{2,1,0:T(2,128)(2,1)} reshape(bf16[32,2,8192]{2,1,0:T(2,128)(2,1)S(1)} %all-to-all-done.3) | data formatting | bytes 2097152
  221.6 1.7 copy.77
  223.3 1.3 copy.73
  224.6 2.3 copy.74
  (79 shorter events, 17.1 us)
Async XLA Ops:
  0.6 9.2 %copy-start = (bf16[256,4096]{1,0:T(8,128)(2,1)S(1)}, bf16[256,4096]{1,0:T(8,128)(2,1)}, u32[]{:S(2)}) copy-start(bf16[256,4096]{1,0:T(8,128)(2,1)} %param.19) | copy-start | bytes 6291460
  1.7 8.2 %collective-permute-start = (bf16[3,4096]{1,0:T(4,128)(2,1)S(1)}, bf16[3,4096]{1,0:T(4,128)(2,1)S(1)}, u32[]{:S(2)}, u32[]{:S(2)}) collective-permute-start(bf16[3,4096]{1,0:T(4,128)(2,1)S(1)} %slice.161), channel_id=1, source_target_pairs={{0,1},{1,2},{2,3},{3,4},{4,5},{5,6},{6,7},{7,8},{8,9},{9,10},{10,1... | collective-permute-start | bytes 73736 | tf_op jit(solution)/shard_map/ppermute | solution.py:19
  20.3 22.7 %copy-start.5 = (bf16[128,1024]{1,0:T(8,128)(2,1)S(1)}, bf16[128,1024]{1,0:T(8,128)(2,1)}, u32[]{:S(2)}) copy-start(bf16[128,1024]{1,0:T(8,128)(2,1)} %param.26) | copy-start | bytes 786436
  20.3 22.9 %copy-start.6 = (bf16[128,1024]{1,0:T(8,128)(2,1)S(1)}, bf16[128,1024]{1,0:T(8,128)(2,1)}, u32[]{:S(2)}) copy-start(bf16[128,1024]{1,0:T(8,128)(2,1)} %param.27) | copy-start | bytes 786436
  30.8 12.6 %copy-start.4 = (bf16[128,4096]{1,0:T(8,128)(2,1)S(1)}, bf16[128,4096]{1,0:T(8,128)(2,1)}, u32[]{:S(2)}) copy-start(bf16[128,4096]{1,0:T(8,128)(2,1)} %param.25) | copy-start | bytes 3145732
  32.6 24.7 %all-to-all-start = ((f32[17,32,128]{2,0,1:T(8,128)}), f32[17,32,128]{2,0,1:T(8,128)S(1)}, u32[]{:S(2)}, u32[]{:S(2)}) async-start(f32[17,32,128]{2,0,1:T(8,128)} %pad_maximum_fusion.2), calls=%async_computation | async-start | bytes 786432 | tf_op jit(solution)/shard_map/all_to_all | solution.py:131
  57.3 79.1 %all-to-all-start.2 = ((bf16[128,32,384]{0,2,1:T(8,128)(2,1)}), bf16[128,32,384]{0,2,1:T(8,128)(2,1)S(1)}, u32[]{:S(2)}, u32[]{:S(2)}) async-start(bf16[128,32,384]{0,2,1:T(8,128)(2,1)} %pad_maximum_fusion), calls=%async_computation.2 | async-start | bytes 6291456 | tf_op jit(solution)/shard_map/all_to_all | solution.py:38
  136.4 44.8 %all-to-all-start.1 = ((f32[16,32,128]{2,0,1:T(8,128)}), f32[16,32,128]{2,0,1:T(8,128)S(1)}, u32[]{:S(2)}, u32[]{:S(2)}) async-start(f32[16,32,128]{2,0,1:T(8,128)} %bitcast.274), calls=%async_computation.1 | async-start | bytes 524288 | tf_op jit(solution)/shard_map/all_to_all | solution.py:146
  141.5 2.8 %copy-start.18 = (s32[512]{0:T(512)S(1)}, s32[512]{0:T(512)}, u32[]{:S(2)}) copy-start(s32[512]{0:T(512)} %iota_add_fusion.6) | copy-start | bytes 6148
  144.3 3.0 %copy-start.2 = (bf16[32,128,1,384]{3,1,0,2:T(8,128)(2,1)S(1)}, bf16[32,128,1,384]{3,1,0,2:T(8,128)(2,1)}, u32[]{:S(2)}) copy-start(bf16[32,128,1,384]{3,1,0,2:T(8,128)(2,1)} %copy.71) | copy-start | bytes 9437188
  144.3 3.0 %copy-start.13 = (s32[512]{0:T(512)S(1)}, s32[512]{0:T(512)}, u32[]{:S(2)}) copy-start(s32[512]{0:T(512)} %iota_add_fusion.7) | copy-start | bytes 6148
  147.3 1.8 copy-start.12
  147.4 1.8 copy-start.17
  150.4 0.8 copy-start.10
  150.4 0.8 copy-start.19
  152.7 0.9 copy-start.9
  152.7 0.9 copy-start.16
  155.9 1.4 copy-start.7
  155.9 1.4 copy-start.15
  159.5 1.6 copy-start.8
  159.5 1.6 copy-start.14
  164.4 1.9 copy-start.20
  181.2 36.9 %all-to-all-start.3 = ((bf16[32,2,8192]{2,1,0:T(2,128)(2,1)}), bf16[32,2,8192]{2,1,0:T(2,128)(2,1)S(1)}, u32[]{:S(2)}, u32[]{:S(2)}) async-start(bf16[32,2,8192]{2,1,0:T(2,128)(2,1)} %reshape.379), calls=%async_computation.3 | async-start | bytes 2097152 | tf_op jit(solution)/shard_map/all_to_all | solution.py:73
  191.7 16.4 %copy-start.3 = (f32[128,4096]{1,0:T(8,128)S(1)}, f32[128,4096]{1,0:T(8,128)}, u32[]{:S(2)}) copy-start(f32[128,4096]{1,0:T(8,128)} %get-tuple-element.7) | copy-start | bytes 6291460
  191.7 16.4 %copy-start.11 = (f32[4096]{0:T(1024)S(1)}, f32[4096]{0:T(1024)}, u32[]{:S(2)}) copy-start(f32[4096]{0:T(1024)} %param.24) | copy-start | bytes 49156
  218.1 8.8 %copy-start.1 = (bf16[256,4096]{1,0:T(8,128)(2,1)S(1)}, bf16[256,4096]{1,0:T(8,128)(2,1)}, u32[]{:S(2)}) copy-start(bf16[256,4096]{1,0:T(8,128)(2,1)} %param.19) | copy-start | bytes 6291460

commit v4 on v3

--- a/solution.py
+++ b/solution.py
@@ -30,14 +30,16 @@
     return jax.nn.silu(total + conv_bias[None, :])
 
 
-def attend_by_heads(q_three, k_three, v_three):
-    tokens = q_three.shape[0]
+def send_heads(q_three, k_three, v_three):
     group = q_three.shape[1] // k_three.shape[1]
     k_wide = jnp.repeat(k_three, group, axis=1)
     v_wide = jnp.repeat(v_three, group, axis=1)
-    joined = lax.all_to_all(
+    return lax.all_to_all(
         jnp.concatenate([q_three, k_wide, v_wide], 2), "seq", split_axis=1, concat_axis=0, tiled=True
     )
+
+
+def attend_by_heads(joined, tokens):
     q_all = joined[:, :, :HEAD_DIM]
     k_all = joined[:, :, HEAD_DIM : 2 * HEAD_DIM]
     v_all = joined[:, :, 2 * HEAD_DIM :]
@@ -123,11 +125,12 @@
     )(step, drive, rate, in_wide, out_wide, init)
 
 
-def exchange(step_sum, local_end, rate):
+def exchange(step_sum, local_end, rate, joined):
     count = lax.axis_size("seq")
     entries, channels = local_end.shape
     width = channels // count
     packed = jnp.concatenate([step_sum[None], local_end], 0).reshape(entries + 1, count, width)
+    packed, joined = lax.optimization_barrier((packed, joined))
     gathered = lax.all_to_all(packed, "seq", 1, 1, tiled=True)
     sums = gathered[0]
     ends = jnp.transpose(gathered[1:], (1, 0, 2))
@@ -144,7 +147,7 @@
     )
     incoming = jnp.sum(weight * ends[None], axis=1)
     back = lax.all_to_all(jnp.transpose(incoming, (1, 0, 2)), "seq", 1, 1, tiled=True)
-    return back.reshape(entries, channels)
+    return back.reshape(entries, channels), joined
 
 
 def per_device(
@@ -176,16 +179,18 @@
     out_wide = jnp.broadcast_to(state_out[:, :, None], (length, entries, LANES))
     zero_state = jnp.zeros(rate.shape, jnp.float32)
     local_end = run_scan(step, drive, rate, in_wide, out_wide, zero_state, False)
-    incoming = exchange(jnp.sum(step, axis=0), local_end, rate)
+    tokens = query_heads.shape[0]
+    joined = send_heads(
+        query_heads.reshape(tokens, -1, HEAD_DIM),
+        key_heads.reshape(tokens, -1, HEAD_DIM),
+        value_heads.reshape(tokens, -1, HEAD_DIM),
+    )
+    incoming, joined = exchange(jnp.sum(step, axis=0), local_end, rate, joined)
     read = run_scan(step, drive, rate, in_wide, out_wide, incoming, True)
     mamba_out = (
         (read + skip_gain[None, :] * conv) * jax.nn.silu(inner_gate.astype(jnp.float32))
     ).astype(jnp.bfloat16)
-    tokens = query_heads.shape[0]
-    q_three = query_heads.reshape(tokens, -1, HEAD_DIM)
-    k_three = key_heads.reshape(tokens, -1, HEAD_DIM)
-    v_three = value_heads.reshape(tokens, -1, HEAD_DIM)
-    attention_out = attend_by_heads(q_three, k_three, v_three)
+    attention_out = attend_by_heads(joined, tokens)
     return (mamba_out, attention_out)
 
 

time: 228 us -> 235 us (1.031)
  waiting for transfers between devices: 72.8 us -> 59.8 us
  starting transfers between devices: 34.2 us -> 47 us
  local copies, waits for them, and re-layouts: 25 us -> 30.5 us
  matrix products: 28.6 us -> 31.9 us
    all_to_all x1, waiting for transfers between devices: 55.4 us -> 0.01 us  [send_heads(): lax.all_to_all(jnp.concatenate([q_three, k_wide, v_wide], 2), 'seq', spli...]
    ppermute x1, waiting for transfers between devices: 0.01 us -> 51.9 us  [shifted(): return lax.ppermute(block, axis, route)]
    all_to_all x1, waiting for transfers between devices: 11 us -> 0.01 us  [exchange(): gathered = lax.all_to_all(packed, 'seq', 1, 1, tiled=True)]
    all_to_all x1, starting transfers between devices: 5.11 us -> 11.6 us  [send_heads(): lax.all_to_all(jnp.concatenate([q_three, k_wide, v_wide], 2), 'seq', spli...]
    all_to_all x1, starting transfers between devices: 5.1 us -> 10 us  [exchange(): lax.all_to_all(jnp.transpose(incoming, (1, 0, 2)), 'seq', 1, 1, tiled=True)]
    reshape x3, local copies, waits for them, and re-layouts: 1.06 us -> 4.75 us  [the longest x1 1.8 us: per_device(): value_heads.reshape(tokens, -1, HEAD_DIM)]
    all_to_all x1, starting transfers between devices: 10.4 us -> 13.9 us  [exchange(): gathered = lax.all_to_all(packed, 'seq', 1, 1, tiled=True)]
    dot_general x8, matrix products: 12.3 us -> 15.4 us  [attend_by_heads(): jnp.einsum('hij,jhd->ihd', expo.astype(jnp.bfloat16), v_all[:stop], prefe...]
  transfers between devices with their start and end apart: 5 -> 5, of which waited for: 3 -> 3; matrix products, arithmetic and copies ran while one was open for 31% -> 28% of each run, Pallas kernels for 7% -> 11%
where the time goes in v4:
time: 235 us; the launch traced here: 234 us
  waiting for transfers between devices  59.8 us (25%)
  starting transfers between devices  47 us (20%)
  other arithmetic  36.5 us (16%)
  matrix products  31.9 us (14%)
  local copies, waits for them, and re-layouts  30.5 us (13%)
  Pallas kernels  26.8 us (11%)
    ppermute x1, waiting for transfers between devices, shifted(): return lax.ppermute(block, axis, route)  51.9 us
    pallas_call x2, Pallas kernels, run_scan(): pl.pallas_call(functools.partial(scan_kernel, with_read=with_read), grid=...  26.8 us
    dot_general x8, matrix products, attend_by_heads(): jnp.einsum('hij,jhd->ihd', expo.astype(jnp.bfloat16), v_all[:stop], prefe...  15.4 us
    all_to_all x1, starting transfers between devices, exchange(): gathered = lax.all_to_all(packed, 'seq', 1, 1, tiled=True)  13.9 us
    unnamed x78, local copies, waits for them, and re-layouts  11.9 us
    all_to_all x1, starting transfers between devices, send_heads(): lax.all_to_all(jnp.concatenate([q_three, k_wide, v_wide], 2), 'seq', spli...  11.6 us
    reduce_sum x8, other arithmetic, attend_by_heads(): total = jnp.sum(expo, axis=-1)  11 us
    all_to_all x1, starting transfers between devices, exchange(): lax.all_to_all(jnp.transpose(incoming, (1, 0, 2)), 'seq', 1, 1, tiled=True)  10 us
  transfers between devices with their start and end apart: 5, of which 3 were waited for; matrix products, arithmetic and copies ran while one was open for 28% of the time, Pallas kernels for 11%

profile of v4, /device:TPU:16, one launch (start us, length us, event | category | flops | bytes accessed | tf_op | source)
XLA Modules:
  0.0 233.8 jit_solution(2067600441336930071)
XLA Ops:
  0.6 1.3 copy.75
  1.9 1.8 copy.76
  3.7 1.6 copy.67
  5.3 1.2 broadcast_in_dim.172
  6.8 1.8 pad_maximum_fusion
  8.7 11.6 %all-to-all-start = ((bf16[128,32,384]{0,2,1:T(8,128)(2,1)}), bf16[128,32,384]{0,2,1:T(8,128)(2,1)}, u32[]{:S(2)}, u32[]{:S(2)}) async-start(bf16[128,32,384]{0,2,1:T(8,128)(2,1)} %pad_maximum_fusion), calls=%async_computation | async-start | bytes 6291456 | tf_op jit(solution)/shard_map/all_to_all | solution.py:37
  21.1 3.6 %collective-permute-start = (bf16[3,4096]{1,0:T(4,128)(2,1)S(1)}, bf16[3,4096]{1,0:T(4,128)(2,1)S(1)}, u32[]{:S(2)}, u32[]{:S(2)}) collective-permute-start(bf16[3,4096]{1,0:T(4,128)(2,1)S(1)} %slice.161), channel_id=1, source_target_pairs={{0,1},{1,2},{2,3},{3,4},{4,5},{5,6},{6,7},{7,8},{8,9},{9,10},{10,1... | collective-permute-start | bytes 73736 | tf_op jit(solution)/shard_map/ppermute | solution.py:19
  33.6 51.9 %collective-permute-done = bf16[3,4096]{1,0:T(4,128)(2,1)S(1)} collective-permute-done((bf16[3,4096]{1,0:T(4,128)(2,1)S(1)}, bf16[3,4096]{1,0:T(4,128)(2,1)S(1)}, u32[]{:S(2)}, u32[]{:S(2)}) %collective-permute-start) | collective-permute-done | bytes 24608 | tf_op jit(solution)/shard_map/ppermute | solution.py:19
  85.5 7.3 %fusion.216 = (f32[128,4096]{1,0:T(8,128)}, f32[128,4096]{1,0:T(8,128)}, f32[4096]{0:T(1024)S(1)}, f32[128,4096]{1,0:T(8,128)}) fusion(f32[4096]{0:T(1024)S(1)} %copy-done.33, bf16[128,4096]{1,0:T(8,128)(2,1)} %param.14, f32[4096]{0:T(1024)S(1)} %bitcast.276, bf16[3,4096]{1,0:T(4,128)(2,1)S(1)} %collective-permute-done, f32[4096]{0:T(1024)S(1)} %bitcast.277, ...), kind=kOutput, calls=%fused_computation.203 | convolution fusion | flops 286257152 | bytes 9641984 | tf_op jit(solution)/shard_map/dot_general | solution.py:173
  92.8 1.3 broadcast_in_dim.100.out_ref
  94.1 1.3 broadcast_in_dim.99.in_ref
  96.1 10.4 %shard_map.149 = f32[16,4096]{1,0:T(8,128)} custom-call(f32[128,4096]{1,0:T(8,128)} %get-tuple-element.17.step_ref, f32[128,4096]{1,0:T(8,128)} %get-tuple-element.10.drive_ref, f32[16,4096]{1,0:T(8,128)} %copy-done.4, f32[128,16,128]{2,1,0:T(8,128)} %broadcast_in_dim.99.in_ref, f32[128,16,128]{2,1,0:T(8,128)} %broadcast_in_dim.100.out_ref, ...), custom_call_target="tpu_custom_call" | custom-call | tf_op jit(solution)/shard_map/pallas_call | solution.py:118
  106.5 1.0 copy_bitcast_fusion.1
  108.3 4.7 %copy.70 = bf16[32,128,1,384]{3,1,0,2:T(8,128)(2,1)} copy(bf16[32,128,1,384]{1,3,0,2:T(8,128)(2,1)} %bitcast.11) | data formatting | bytes 6291456 | tf_op jit(solution)/shard_map/all_to_all | solution.py:37
  113.0 13.9 %all-to-all-start.1 = ((f32[17,32,128]{2,0,1:T(8,128)}), f32[17,32,128]{2,0,1:T(8,128)S(1)}, u32[]{:S(2)}, u32[]{:S(2)}) async-start(f32[17,32,128]{2,0,1:T(8,128)} %pad_maximum_fusion.2), calls=%async_computation.1 | async-start | bytes 786432 | tf_op jit(solution)/shard_map/all_to_all | solution.py:134
  127.0 1.4 fusion.218
  128.7 1.3 fusion.61
  130.0 1.7 fusion
  135.4 0.9 fusion.131
  136.3 0.9 fusion.14
  137.2 1.3 fusion.19
  138.5 1.3 fusion.107
  139.8 1.1 fusion.220
  140.9 1.2 fusion.8
  142.0 1.4 fusion.83
  143.5 1.3 fusion.3
  144.8 2.0 fusion.10
  146.8 1.8 fusion.95
  148.6 1.4 fusion.221
  150.1 1.9 fusion.1
  152.0 2.8 %fusion.4 = f32[512]{0:T(512)S(1)} fusion(f32[512,4096]{1,0:T(8,128)S(1)} %get-tuple-element.33, f32[512]{0:T(512)S(1)} %get-tuple-element.32, s32[512]{0:T(512)S(1)} %copy-done.19), kind=kLoop, calls=%fused_computation.19 | loop fusion | flops 12582400 | bytes 8394752 | tf_op jit(solution)/shard_map/reduce_sum | solution.py:66
  154.9 1.6 fusion.71
  156.6 7.1 %select_reduce_fusion = f32[32,32,128]{2,1,0:T(8,128)S(1)} fusion(f32[32,128]{1,0:T(8,128)S(1)} %bitcast.273, pred[32,32,32]{2,1,0:T(8,128)(4,1)S(1)} %copy-done.7), kind=kLoop, calls=%fused_computation | loop fusion | flops 8257536 | bytes 573440 | tf_op jit(solution)/shard_map/reduce_sum | solution.py:143
  163.8 3.0 %multiply_reduce_fusion = f32[32,16,128]{2,1,0:T(8,128)} fusion(f32[32,16,128]{2,1,0:T(8,128)S(1)} %slice_bitcast_fusion, f32[32,32,128]{2,1,0:T(8,128)S(1)} %select_reduce_fusion, f32[16,128]{1,0:T(8,128)S(1)} %copy-done.27, pred[32,32]{1,0:T(8,128)(4,1)S(1)} %copy-done.17), kind=kLoop, calls=%fused_computation.6 | loop fusion | flops 8323072 | bytes 1057792 | tf_op jit(solution)/shard_map/reduce_sum | solution.py:148
  166.8 10.0 %all-to-all-start.2 = ((f32[16,32,128]{2,0,1:T(8,128)}), f32[16,32,128]{2,0,1:T(8,128)S(1)}, u32[]{:S(2)}, u32[]{:S(2)}) async-start(f32[16,32,128]{2,0,1:T(8,128)} %bitcast.15), calls=%async_computation.2 | async-start | bytes 524288 | tf_op jit(solution)/shard_map/all_to_all | solution.py:149
  176.9 6.3 %fusion.119 = bf16[4096,1,128]{0,2,1:T(8,128)(2,1)S(1)} fusion(bf16[4096,1,128]{0,2,1:T(8,128)(2,1)S(1)} %fusion.71, f32[512,4096]{1,0:T(8,128)} %copy-done.2, f32[512]{0:T(512)S(1)} %copy-done.31, s32[512]{0:T(512)S(1)} %copy-done.19, bf16[4096,1,384]{2,0,1:T(8,128)(2,1)} %bitcast.257, f32[512]{0:T(512)S(1)} %fusion.4), kind=kOutput, calls=%fused_computation.92 | convolution fusion | flops 549584896 | bytes 9574400 | tf_op jit(solution)/shard_map/hij,jhd->ihd/dot_general | solution.py:67
  183.7 1.4 reduce.32
  185.7 1.1 reshape.379
  186.9 1.7 all-to-all-done.2
  189.3 7.8 %all-to-all-start.3 = ((bf16[32,2,8192]{2,1,0:T(2,128)(2,1)}), bf16[32,2,8192]{2,1,0:T(2,128)(2,1)S(1)}, u32[]{:S(2)}, u32[]{:S(2)}) async-start(bf16[32,2,8192]{2,1,0:T(2,128)(2,1)} %reshape.379), calls=%async_computation.3 | async-start | bytes 2097152 | tf_op jit(solution)/shard_map/all_to_all | solution.py:75
  197.1 1.7 copy_bitcast_fusion.init_ref
  198.8 16.4 %shard_map.150 = f32[128,4096]{1,0:T(8,128)} custom-call(f32[128,4096]{1,0:T(8,128)} %get-tuple-element.17.step_ref, f32[128,4096]{1,0:T(8,128)} %get-tuple-element.10.drive_ref, f32[16,4096]{1,0:T(8,128)} %copy-done.4, f32[128,16,128]{2,1,0:T(8,128)} %broadcast_in_dim.99.in_ref, f32[128,16,128]{2,1,0:T(8,128)} %broadcast_in_dim.100.out_ref, ...), custom_call_target="tpu_custom_call" | custom-call | tf_op jit(solution)/shard_map/pallas_call | solution.py:118
  215.2 3.6 %fusion.27 = bf16[128,4096]{1,0:T(8,128)(2,1)} fusion(bf16[128,4096]{1,0:T(8,128)(2,1)} %param.15, f32[128,4096]{1,0:T(8,128)} %shard_map.150, f32[128,4096]{1,0:T(8,128)S(1)} %copy-done.5, f32[4096]{0:T(1024)S(1)} %copy-done.14), kind=kLoop, calls=%fused_computation.47 | loop fusion | flops 4718592 | bytes 6307840 | tf_op jit(solution)/shard_map/convert_element_type | solution.py:192
  218.8 6.2 %all-to-all-done.3 = bf16[32,2,8192]{2,1,0:T(2,128)(2,1)S(1)} async-done(((bf16[32,2,8192]{2,1,0:T(2,128)(2,1)}), bf16[32,2,8192]{2,1,0:T(2,128)(2,1)S(1)}, u32[]{:S(2)}, u32[]{:S(2)}) %all-to-all-start.3) | async-done | bytes 1048608 | tf_op jit(solution)/shard_map/all_to_all | solution.py:75
  225.0 3.5 %reshape.380 = bf16[4096,1,128]{2,1,0:T(2,128)(2,1)} reshape(bf16[32,2,8192]{2,1,0:T(2,128)(2,1)S(1)} %all-to-all-done.3) | data formatting | bytes 2097152
  228.4 1.7 copy.77
  230.2 1.3 copy.73
  231.5 2.3 copy.74
  (107 shorter events, 17.2 us)
Async XLA Ops:
  0.6 84.8 %copy-start = (bf16[256,4096]{1,0:T(8,128)(2,1)S(1)}, bf16[256,4096]{1,0:T(8,128)(2,1)}, u32[]{:S(2)}) copy-start(bf16[256,4096]{1,0:T(8,128)(2,1)} %param.19) | copy-start | bytes 6291460
  8.6 22.0 %copy-start.8 = (f32[16,4096]{1,0:T(8,128)S(1)}, f32[16,4096]{1,0:T(8,128)}, u32[]{:S(2)}) copy-start(f32[16,4096]{1,0:T(8,128)} %param.21) | copy-start | bytes 786436
  8.6 24.7 %copy-start.9 = (f32[4,4096]{1,0:T(4,128)S(1)}, f32[4,4096]{1,0:T(4,128)}, u32[]{:S(2)}) copy-start(f32[4,4096]{1,0:T(4,128)} %param.16) | copy-start | bytes 196612
  8.6 24.7 %copy-start.25 = (f32[128,16]{0,1:T(8,128)S(1)}, f32[128,16]{0,1:T(8,128)}, u32[]{:S(2)}) copy-start(f32[128,16]{0,1:T(8,128)} %param.22) | copy-start | bytes 24580
  8.6 24.8 %copy-start.26 = (f32[128,16]{0,1:T(8,128)S(1)}, f32[128,16]{0,1:T(8,128)}, u32[]{:S(2)}) copy-start(f32[128,16]{0,1:T(8,128)} %param.23) | copy-start | bytes 24580
  8.6 76.8 %copy-start.32 = (bf16[128,256]{1,0:T(8,128)(2,1)S(1)}, bf16[128,256]{1,0:T(8,128)(2,1)}, u32[]{:S(2)}) copy-start(bf16[128,256]{1,0:T(8,128)(2,1)} %param.18) | copy-start | bytes 196612
  8.6 76.8 %copy-start.33 = (f32[4096]{0:T(1024)S(1)}, f32[4096]{0:T(1024)}, u32[]{:S(2)}) copy-start(f32[4096]{0:T(1024)} %param.17) | copy-start | bytes 49156
  8.6 76.8 %copy-start.34 = (f32[4096]{0:T(1024)S(1)}, f32[4096]{0:T(1024)}, u32[]{:S(2)}) copy-start(f32[4096]{0:T(1024)} %param.20) | copy-start | bytes 49156
  8.7 99.6 %all-to-all-start = ((bf16[128,32,384]{0,2,1:T(8,128)(2,1)}), bf16[128,32,384]{0,2,1:T(8,128)(2,1)}, u32[]{:S(2)}, u32[]{:S(2)}) async-start(bf16[128,32,384]{0,2,1:T(8,128)(2,1)} %pad_maximum_fusion), calls=%async_computation | async-start | bytes 6291456 | tf_op jit(solution)/shard_map/all_to_all | solution.py:37
  21.1 64.4 %collective-permute-start = (bf16[3,4096]{1,0:T(4,128)(2,1)S(1)}, bf16[3,4096]{1,0:T(4,128)(2,1)S(1)}, u32[]{:S(2)}, u32[]{:S(2)}) collective-permute-start(bf16[3,4096]{1,0:T(4,128)(2,1)S(1)} %slice.161), channel_id=1, source_target_pairs={{0,1},{1,2},{2,3},{3,4},{4,5},{5,6},{6,7},{7,8},{8,9},{9,10},{10,1... | collective-permute-start | bytes 73736 | tf_op jit(solution)/shard_map/ppermute | solution.py:19
  30.6 62.2 %copy-start.16 = (pred[32,32]{1,0:T(8,128)(4,1)}, pred[32,32]{1,0:T(8,128)(4,1)S(1)}, u32[]{:S(2)}) copy-start(pred[32,32]{1,0:T(8,128)(4,1)S(1)} %get-tuple-element.35) | copy-start | bytes 3076
  30.7 62.1 %copy-start.4 = (f32[16,4096]{1,0:T(8,128)}, f32[16,4096]{1,0:T(8,128)S(1)}, u32[]{:S(2)}) copy-start(f32[16,4096]{1,0:T(8,128)S(1)} %exponential_negate_fusion.rate_ref) | copy-start | bytes 786436
  33.3 95.1 %copy-start.24 = (s32[512]{0:T(512)}, s32[512]{0:T(512)S(1)}, u32[]{:S(2)}) copy-start(s32[512]{0:T(512)S(1)} %iota_add_fusion.6) | copy-start | bytes 6148
  113.0 17.0 %copy-start.18 = (s32[512]{0:T(512)S(1)}, s32[512]{0:T(512)}, u32[]{:S(2)}) copy-start(s32[512]{0:T(512)} %iota_add_fusion.7) | copy-start | bytes 6148
  113.0 43.5 %all-to-all-start.1 = ((f32[17,32,128]{2,0,1:T(8,128)}), f32[17,32,128]{2,0,1:T(8,128)S(1)}, u32[]{:S(2)}, u32[]{:S(2)}) async-start(f32[17,32,128]{2,0,1:T(8,128)} %pad_maximum_fusion.2), calls=%async_computation.1 | async-start | bytes 786432 | tf_op jit(solution)/shard_map/all_to_all | solution.py:134
  126.9 3.0 %copy-start.3 = (bf16[32,128,1,384]{3,1,0,2:T(8,128)(2,1)S(1)}, bf16[32,128,1,384]{3,1,0,2:T(8,128)(2,1)}, u32[]{:S(2)}) copy-start(bf16[32,128,1,384]{3,1,0,2:T(8,128)(2,1)} %copy.70) | copy-start | bytes 9437188
  130.0 1.8 copy-start.15
  130.0 1.8 copy-start.23
  131.8 20.3 %copy-start.2 = (f32[512,4096]{1,0:T(8,128)}, f32[512,4096]{1,0:T(8,128)S(1)}, u32[]{:S(2)}) copy-start(f32[512,4096]{1,0:T(8,128)S(1)} %get-tuple-element.33) | copy-start | bytes 25165828
  131.8 20.2 %copy-start.30 = (f32[512]{0:T(512)}, f32[512]{0:T(512)S(1)}, u32[]{:S(2)}) copy-start(f32[512]{0:T(512)S(1)} %get-tuple-element.32) | copy-start | bytes 6148
  133.0 0.8 copy-start.13
  133.0 0.8 copy-start.28
  135.3 0.9 copy-start.12
  135.3 0.9 copy-start.22
  138.5 1.3 copy-start.10
  138.5 1.3 copy-start.21
  142.0 1.5 copy-start.11
  142.0 1.5 copy-start.20
  146.8 1.8 copy-start.29
  150.1 2.0 copy-start.19
  154.9 1.7 copy-start.7
  154.9 8.9 %copy-start.17 = (pred[32,32]{1,0:T(8,128)(4,1)S(1)}, pred[32,32]{1,0:T(8,128)(4,1)}, u32[]{:S(2)}) copy-start(pred[32,32]{1,0:T(8,128)(4,1)} %copy-done.16) | copy-start | bytes 3076
  154.9 8.9 %copy-start.27 = (f32[16,128]{1,0:T(8,128)S(1)}, f32[16,128]{1,0:T(8,128)}, u32[]{:S(2)}) copy-start(f32[16,128]{1,0:T(8,128)} %constant_dynamic-slice_fusion) | copy-start | bytes 24580
  156.5 20.3 %copy-start.31 = (f32[512]{0:T(512)S(1)}, f32[512]{0:T(512)}, u32[]{:S(2)}) copy-start(f32[512]{0:T(512)} %copy-done.30) | copy-start | bytes 6148
  166.8 21.8 %all-to-all-start.2 = ((f32[16,32,128]{2,0,1:T(8,128)}), f32[16,32,128]{2,0,1:T(8,128)S(1)}, u32[]{:S(2)}, u32[]{:S(2)}) async-start(f32[16,32,128]{2,0,1:T(8,128)} %bitcast.15), calls=%async_computation.2 | async-start | bytes 524288 | tf_op jit(solution)/shard_map/all_to_all | solution.py:149
  188.6 0.7 copy-start.6
  189.3 35.7 %all-to-all-start.3 = ((bf16[32,2,8192]{2,1,0:T(2,128)(2,1)}), bf16[32,2,8192]{2,1,0:T(2,128)(2,1)S(1)}, u32[]{:S(2)}, u32[]{:S(2)}) async-start(bf16[32,2,8192]{2,1,0:T(2,128)(2,1)} %reshape.379), calls=%async_computation.3 | async-start | bytes 2097152 | tf_op jit(solution)/shard_map/all_to_all | solution.py:75
  198.8 16.4 %copy-start.5 = (f32[128,4096]{1,0:T(8,128)S(1)}, f32[128,4096]{1,0:T(8,128)}, u32[]{:S(2)}) copy-start(f32[128,4096]{1,0:T(8,128)} %get-tuple-element.11) | copy-start | bytes 6291460
  198.8 16.4 %copy-start.14 = (f32[4096]{0:T(1024)S(1)}, f32[4096]{0:T(1024)}, u32[]{:S(2)}) copy-start(f32[4096]{0:T(1024)} %param.24) | copy-start | bytes 49156
  225.0 8.8 %copy-start.1 = (bf16[256,4096]{1,0:T(8,128)(2,1)S(1)}, bf16[256,4096]{1,0:T(8,128)(2,1)}, u32[]{:S(2)}) copy-start(bf16[256,4096]{1,0:T(8,128)(2,1)} %param.19) | copy-start | bytes 6291460

commit v5 on v4

--- a/solution.py
+++ b/solution.py
@@ -39,7 +39,7 @@
     )
 
 
-def attend_by_heads(joined, tokens):
+def attend_by_heads(joined, tokens, midway):
     q_all = joined[:, :, :HEAD_DIM]
     k_all = joined[:, :, HEAD_DIM : 2 * HEAD_DIM]
     v_all = joined[:, :, 2 * HEAD_DIM :]
@@ -50,6 +50,8 @@
 
     pieces = []
     for index in range(length // width):
+        if index == length // width // 2:
+            q_all, k_all, v_all = midway(q_all, k_all, v_all)
         stop = (index + 1) * width
         query_block = q_all[stop - width : stop]
         scores = (
@@ -125,13 +127,16 @@
     )(step, drive, rate, in_wide, out_wide, init)
 
 
-def exchange(step_sum, local_end, rate, joined):
+def exchange_send(step_sum, local_end, joined):
     count = lax.axis_size("seq")
     entries, channels = local_end.shape
-    width = channels // count
-    packed = jnp.concatenate([step_sum[None], local_end], 0).reshape(entries + 1, count, width)
+    packed = jnp.concatenate([step_sum[None], local_end], 0).reshape(entries + 1, count, -1)
     packed, joined = lax.optimization_barrier((packed, joined))
-    gathered = lax.all_to_all(packed, "seq", 1, 1, tiled=True)
+    return lax.all_to_all(packed, "seq", 1, 1, tiled=True), joined
+
+
+def exchange_prefix(gathered, rate):
+    count, width = gathered.shape[1:]
     sums = gathered[0]
     ends = jnp.transpose(gathered[1:], (1, 0, 2))
     me = lax.axis_index("seq")
@@ -145,9 +150,13 @@
     weight = jnp.where(
         before[:, :, None, None], jnp.exp(rate_block[None, None] * gap[:, :, None, :]), 0.0
     )
-    incoming = jnp.sum(weight * ends[None], axis=1)
+    return jnp.sum(weight * ends[None], axis=1)
+
+
+def exchange_return(incoming):
+    count, entries, width = incoming.shape
     back = lax.all_to_all(jnp.transpose(incoming, (1, 0, 2)), "seq", 1, 1, tiled=True)
-    return back.reshape(entries, channels), joined
+    return back.reshape(entries, count * width)
 
 
 def per_device(
@@ -168,6 +177,9 @@
 ):
     reach = conv_weight.shape[0] - 1
     rim = shifted(inner_x[-reach:], "seq", 1)
+    rim, query_heads, key_heads, value_heads = lax.optimization_barrier(
+        (rim, query_heads, key_heads, value_heads)
+    )
     conv = convolve(jnp.concatenate([rim, inner_x], 0), conv_weight, conv_bias)
     step = jax.nn.softplus(
         jnp.dot(step_low, step_proj, preferred_element_type=jnp.float32) + step_bias[None, :]
@@ -185,12 +197,19 @@
         key_heads.reshape(tokens, -1, HEAD_DIM),
         value_heads.reshape(tokens, -1, HEAD_DIM),
     )
-    incoming, joined = exchange(jnp.sum(step, axis=0), local_end, rate, joined)
+    gathered, joined = exchange_send(jnp.sum(step, axis=0), local_end, joined)
+    prefix = []
+
+    def midway(q_all, k_all, v_all):
+        prefix.append(exchange_prefix(gathered, rate))
+        return lax.optimization_barrier((prefix[0], q_all, k_all, v_all))[1:]
+
+    attention_out = attend_by_heads(joined, tokens, midway)
+    incoming = exchange_return(prefix[0])
     read = run_scan(step, drive, rate, in_wide, out_wide, incoming, True)
     mamba_out = (
         (read + skip_gain[None, :] * conv) * jax.nn.silu(inner_gate.astype(jnp.float32))
     ).astype(jnp.bfloat16)
-    attention_out = attend_by_heads(joined, tokens)
     return (mamba_out, attention_out)
 
 

time: 235 us -> 220 us (0.936)
  waiting for transfers between devices: 59.8 us -> 48.1 us
  starting transfers between devices: 47 us -> 41 us
  local copies, waits for them, and re-layouts: 30.5 us -> 34.1 us
  matrix products: 31.9 us -> 28.6 us
    ppermute x1, waiting for transfers between devices: 51.9 us -> 0.98 us  [shifted(): return lax.ppermute(block, axis, route)]
    all_to_all x1, waiting for transfers between devices: 0.01 us -> 41.3 us  [send_heads(): lax.all_to_all(jnp.concatenate([q_three, k_wide, v_wide], 2), 'seq', spli...]
    all_to_all x2, starting transfers between devices: 24 us -> 13.7 us  [the longest x1 9.44 us: exchange_return(): lax.all_to_all(jnp.transpose(incoming, (1, 0, 2)), 'seq', 1, 1, tiled=True)]
    dot_general x8, matrix products: 15.4 us -> 11.6 us  [attend_by_heads(): jnp.einsum('hij,jhd->ihd', expo.astype(jnp.bfloat16), v_all[:stop], prefe...]
    slice x1 -> x2, local copies, waits for them, and re-layouts: 0.01 us -> 3.76 us  [the longest x1 3.75 us: attend_by_heads(): v_all = joined[:, :, 2 * HEAD_DIM:]]
    unnamed x78 -> x69, local copies, waits for them, and re-layouts: 11.9 us -> 10.3 us
  transfers between devices with their start and end apart: 5 -> 5, of which waited for: 3 -> 4; matrix products, arithmetic and copies ran while one was open for 28% -> 30% of each run, Pallas kernels for 11% -> 12%
where the time goes in v5:
time: 220 us; the launch traced here: 218 us
  waiting for transfers between devices  48.1 us (22%)
  starting transfers between devices  41 us (19%)
  other arithmetic  38.6 us (18%)
  local copies, waits for them, and re-layouts  34.1 us (16%)
  matrix products  28.6 us (13%)
  Pallas kernels  26.8 us (12%)
    all_to_all x1, waiting for transfers between devices, send_heads(): lax.all_to_all(jnp.concatenate([q_three, k_wide, v_wide], 2), 'seq', spli...  41.3 us
    pallas_call x2, Pallas kernels, run_scan(): pl.pallas_call(functools.partial(scan_kernel, with_read=with_read), grid=...  26.8 us
    all_to_all x1, starting transfers between devices, send_heads(): lax.all_to_all(jnp.concatenate([q_three, k_wide, v_wide], 2), 'seq', spli...  13.3 us
    dot_general x8, matrix products, attend_by_heads(): jnp.einsum('hij,jhd->ihd', expo.astype(jnp.bfloat16), v_all[:stop], prefe...  11.6 us
    reduce_sum x8, other arithmetic, attend_by_heads(): total = jnp.sum(expo, axis=-1)  11.2 us
    unnamed x69, local copies, waits for them, and re-layouts  10.3 us
    all_to_all x1, starting transfers between devices, attend_by_heads(): lax.all_to_all(merged, 'seq', split_axis=0, concat_axis=1, tiled=True)  9.58 us
    all_to_all x1, starting transfers between devices, exchange_return(): lax.all_to_all(jnp.transpose(incoming, (1, 0, 2)), 'seq', 1, 1, tiled=True)  9.44 us
  transfers between devices with their start and end apart: 5, of which 4 were waited for; matrix products, arithmetic and copies ran while one was open for 30% of the time, Pallas kernels for 12%

profile of v5, /device:TPU:16, one launch (start us, length us, event | category | flops | bytes accessed | tf_op | source)
XLA Modules:
  0.0 218.5 jit_solution(6545927489746875412)
XLA Ops:
  0.6 1.0 slice.153
  1.7 4.4 %collective-permute-start = (bf16[3,4096]{1,0:T(4,128)(2,1)S(1)}, bf16[3,4096]{1,0:T(4,128)(2,1)}, u32[]{:S(2)}, u32[]{:S(2)}) collective-permute-start(bf16[3,4096]{1,0:T(4,128)(2,1)S(1)} %slice.153), channel_id=1, source_target_pairs={{0,1},{1,2},{2,3},{3,4},{4,5},{5,6},{6,7},{7,8},{8,9},{9,10},{10,1... | collective-permute-start | bytes 73736 | tf_op jit(solution)/shard_map/ppermute | solution.py:19
  6.1 1.0 collective-permute-done
  7.1 1.1 copy.75
  8.2 1.8 copy.76
  10.0 1.6 copy.67
  11.6 1.2 broadcast_in_dim.172
  13.0 1.8 pad_maximum_fusion
  14.9 13.3 %all-to-all-start = ((bf16[128,32,384]{0,2,1:T(8,128)(2,1)}), bf16[128,32,384]{0,2,1:T(8,128)(2,1)}, u32[]{:S(2)}, u32[]{:S(2)}) async-start(bf16[128,32,384]{0,2,1:T(8,128)(2,1)} %pad_maximum_fusion), calls=%async_computation | async-start | bytes 6291456 | tf_op jit(solution)/shard_map/all_to_all | solution.py:37
  37.0 7.8 %fusion.214 = (f32[128,4096]{1,0:T(8,128)}, f32[128,4096]{1,0:T(8,128)}, f32[4096]{0:T(1024)S(1)}, f32[128,4096]{1,0:T(8,128)}) fusion(f32[4096]{0:T(1024)S(1)} %copy-done.29, bf16[128,4096]{1,0:T(8,128)(2,1)} %param.14, f32[4096]{0:T(1024)S(1)} %bitcast.270, bf16[3,4096]{1,0:T(4,128)(2,1)} %collective-permute-done, f32[4096]{0:T(1024)S(1)} %bitcast.271, ...), kind=kOutput, calls=%fused_computation.201 | convolution fusion | flops 286257152 | bytes 9641984 | tf_op jit(solution)/shard_map/dot_general | solution.py:185
  44.8 1.3 broadcast_in_dim.101.out_ref
  46.1 1.3 broadcast_in_dim.99.in_ref
  48.1 10.4 %shard_map.149 = f32[16,4096]{1,0:T(8,128)} custom-call(f32[128,4096]{1,0:T(8,128)} %get-tuple-element.34.step_ref, f32[128,4096]{1,0:T(8,128)} %get-tuple-element.24.drive_ref, f32[16,4096]{1,0:T(8,128)} %copy-done.3, f32[128,16,128]{2,1,0:T(8,128)} %broadcast_in_dim.99.in_ref, f32[128,16,128]{2,1,0:T(8,128)} %broadcast_in_dim.101.out_ref, ...), custom_call_target="tpu_custom_call" | custom-call | tf_op jit(solution)/shard_map/pallas_call | solution.py:120
  58.5 1.0 copy_bitcast_fusion.1
  60.3 41.3 %all-to-all-done = bf16[128,32,384]{0,2,1:T(8,128)(2,1)} async-done(((bf16[128,32,384]{0,2,1:T(8,128)(2,1)}), bf16[128,32,384]{0,2,1:T(8,128)(2,1)}, u32[]{:S(2)}, u32[]{:S(2)}) %all-to-all-start) | async-done | bytes 3145760 | tf_op jit(solution)/shard_map/all_to_all | solution.py:37
  101.6 4.6 %copy.70 = bf16[32,128,1,384]{3,1,0,2:T(8,128)(2,1)} copy(bf16[32,128,1,384]{1,3,0,2:T(8,128)(2,1)} %bitcast.11) | data formatting | bytes 6291456 | tf_op jit(solution)/shard_map/all_to_all | solution.py:37
  106.3 4.3 %all-to-all-start.1 = ((f32[17,32,128]{2,0,1:T(8,128)}), f32[17,32,128]{2,0,1:T(8,128)S(1)}, u32[]{:S(2)}, u32[]{:S(2)}) async-start(f32[17,32,128]{2,0,1:T(8,128)} %pad_maximum_fusion.2), calls=%async_computation.1 | async-start | bytes 786432 | tf_op jit(solution)/shard_map/all_to_all | solution.py:135
  110.6 3.8 %fusion.215 = (bf16[4096,1,128]{2,0,1:T(8,128)(2,1)}, bf16[4096,1,128]{2,0,1:T(8,128)(2,1)}, bf16[4096,1,128]{2,0,1:T(8,128)(2,1)}) fusion(bf16[4096,1,384]{2,0,1:T(8,128)(2,1)} %bitcast.250), kind=kLoop, calls=%fused_computation.202 | loop fusion | bytes 6291456 | tf_op jit(solution)/shard_map/slice | solution.py:45
  115.0 1.0 fusion.61
  119.6 0.9 fusion.14
  120.5 1.2 fusion.19
  122.7 1.3 fusion.107
  124.5 8.3 %select_reduce_fusion = f32[32,32,128]{2,1,0:T(8,128)S(1)} fusion(f32[32,128]{1,0:T(8,128)S(1)} %bitcast.267, pred[32,32,32]{2,1,0:T(8,128)(4,1)} %broadcast_and_fusion), kind=kLoop, calls=%fused_computation | loop fusion | flops 8257536 | bytes 573440 | tf_op jit(solution)/shard_map/reduce_sum | solution.py:148
  132.8 3.8 %multiply_reduce_fusion = f32[32,16,128]{2,1,0:T(8,128)} fusion(f32[32,16,128]{2,1,0:T(8,128)S(1)} %slice_bitcast_fusion, f32[32,32,128]{2,1,0:T(8,128)S(1)} %select_reduce_fusion, f32[16,128]{1,0:T(8,128)} %constant_dynamic-slice_fusion, pred[32,32]{1,0:T(8,128)(4,1)} %copy-done.17), kind=kLoop, calls=%fused_computation.6 | loop fusion | flops 8323072 | bytes 1057792 | tf_op jit(solution)/shard_map/reduce_sum | solution.py:153
  136.6 9.4 %all-to-all-start.2 = ((f32[16,32,128]{2,0,1:T(8,128)}), f32[16,32,128]{2,0,1:T(8,128)S(1)}, u32[]{:S(2)}, u32[]{:S(2)}) async-start(f32[16,32,128]{2,0,1:T(8,128)} %bitcast.266), calls=%async_computation.2 | async-start | bytes 524288 | tf_op jit(solution)/shard_map/all_to_all | solution.py:158
  146.1 2.0 fusion
  148.2 1.1 fusion.219
  149.3 1.2 fusion.8
  150.4 1.3 fusion.3
  151.7 2.1 fusion.10
  153.8 1.2 fusion.83
  155.0 1.8 fusion.95
  156.8 2.4 %fusion.220 = (f32[512]{0:T(512)S(1)}, f32[512,3584]{1,0:T(8,128)S(1)}) fusion(bf16[4096,1,128]{2,0,1:T(8,128)(2,1)S(1)} %copy-done.7, bf16[4096,1,128]{2,0,1:T(8,128)(2,1)} %get-tuple-element.18, s32[3584]{0:T(1024)S(1)} %iota_add_fusion, s32[512]{0:T(512)S(1)} %copy-done.27), kind=kOutput, calls=%fused_computation.207 | convolution fusion | flops 477101568 | bytes 8409088 | tf_op jit(solution)/shard_map/ihd,jhd->hij/dot_general | solution.py:58
  159.2 1.9 fusion.1
  161.1 1.6 fusion.71
  162.8 3.1 %fusion.4 = f32[512]{0:T(512)S(1)} fusion(f32[512,4096]{1,0:T(8,128)S(1)} %get-tuple-element.50, f32[512]{0:T(512)S(1)} %get-tuple-element.49, s32[512]{0:T(512)S(1)} %copy-done.18), kind=kLoop, calls=%fused_computation.19 | loop fusion | flops 12582400 | bytes 8394752 | tf_op jit(solution)/shard_map/reduce_sum | solution.py:68
  165.9 2.9 %fusion.119 = bf16[4096,1,128]{0,2,1:T(8,128)(2,1)S(1)} fusion(bf16[4096,1,128]{0,2,1:T(8,128)(2,1)S(1)} %fusion.71, f32[512,4096]{1,0:T(8,128)S(1)} %get-tuple-element.50, f32[512]{0:T(512)S(1)} %get-tuple-element.49, s32[512]{0:T(512)S(1)} %copy-done.18, bf16[4096,1,128]{2,0,1:T(8,128)(2,1)S(1)} %copy-done.6, f32[512]{0:T(512)S(1)} %fusion.4), kind=kOutput, calls=%fused_computation.92 | convolution fusion | flops 549584896 | bytes 9574400 | tf_op jit(solution)/shard_map/hij,jhd->ihd/dot_general | solution.py:69
  169.3 1.3 reduce.32
  171.3 1.1 reshape.379
  173.1 9.6 %all-to-all-start.3 = ((bf16[32,2,8192]{2,1,0:T(2,128)(2,1)}), bf16[32,2,8192]{2,1,0:T(2,128)(2,1)S(1)}, u32[]{:S(2)}, u32[]{:S(2)}) async-start(bf16[32,2,8192]{2,1,0:T(2,128)(2,1)} %reshape.379), calls=%async_computation.3 | async-start | bytes 2097152 | tf_op jit(solution)/shard_map/all_to_all | solution.py:77
  182.7 1.7 copy_bitcast_fusion.init_ref
  184.4 16.5 %shard_map.150 = f32[128,4096]{1,0:T(8,128)} custom-call(f32[128,4096]{1,0:T(8,128)} %get-tuple-element.34.step_ref, f32[128,4096]{1,0:T(8,128)} %get-tuple-element.24.drive_ref, f32[16,4096]{1,0:T(8,128)} %copy-done.3, f32[128,16,128]{2,1,0:T(8,128)} %broadcast_in_dim.99.in_ref, f32[128,16,128]{2,1,0:T(8,128)} %broadcast_in_dim.101.out_ref, ...), custom_call_target="tpu_custom_call" | custom-call | tf_op jit(solution)/shard_map/pallas_call | solution.py:120
  200.8 3.6 %fusion.27 = bf16[128,4096]{1,0:T(8,128)(2,1)} fusion(bf16[128,4096]{1,0:T(8,128)(2,1)} %param.15, f32[128,4096]{1,0:T(8,128)} %shard_map.150, f32[128,4096]{1,0:T(8,128)S(1)} %copy-done.4, f32[4096]{0:T(1024)S(1)} %copy-done.15), kind=kLoop, calls=%fused_computation.47 | loop fusion | flops 4718592 | bytes 6307840 | tf_op jit(solution)/shard_map/convert_element_type | solution.py:212
  204.4 5.3 %all-to-all-done.3 = bf16[32,2,8192]{2,1,0:T(2,128)(2,1)S(1)} async-done(((bf16[32,2,8192]{2,1,0:T(2,128)(2,1)}), bf16[32,2,8192]{2,1,0:T(2,128)(2,1)S(1)}, u32[]{:S(2)}, u32[]{:S(2)}) %all-to-all-start.3) | async-done | bytes 1048608 | tf_op jit(solution)/shard_map/all_to_all | solution.py:77
  209.7 3.5 %reshape.380 = bf16[4096,1,128]{2,1,0:T(2,128)(2,1)} reshape(bf16[32,2,8192]{2,1,0:T(2,128)(2,1)S(1)} %all-to-all-done.3) | data formatting | bytes 2097152
  213.2 1.7 copy.77
  214.9 1.3 copy.73
  216.2 2.3 %copy.74 = bf16[128,4096]{1,0:T(8,128)(2,1)} copy(bf16[128,4096]{0,1:T(8,128)(2,1)} %bitcast.260) | data formatting | bytes 2097152
  (100 shorter events, 18.0 us)
Async XLA Ops:
  0.6 36.3 %copy-start = (bf16[256,4096]{1,0:T(8,128)(2,1)S(1)}, bf16[256,4096]{1,0:T(8,128)(2,1)}, u32[]{:S(2)}) copy-start(bf16[256,4096]{1,0:T(8,128)(2,1)} %param.19) | copy-start | bytes 6291460
  1.7 5.4 %collective-permute-start = (bf16[3,4096]{1,0:T(4,128)(2,1)S(1)}, bf16[3,4096]{1,0:T(4,128)(2,1)}, u32[]{:S(2)}, u32[]{:S(2)}) collective-permute-start(bf16[3,4096]{1,0:T(4,128)(2,1)S(1)} %slice.153), channel_id=1, source_target_pairs={{0,1},{1,2},{2,3},{3,4},{4,5},{5,6},{6,7},{7,8},{8,9},{9,10},{10,1... | collective-permute-start | bytes 73736 | tf_op jit(solution)/shard_map/ppermute | solution.py:19
  14.8 13.3 %copy-start.24 = (f32[128,16]{0,1:T(8,128)S(1)}, f32[128,16]{0,1:T(8,128)}, u32[]{:S(2)}) copy-start(f32[128,16]{0,1:T(8,128)} %param.22) | copy-start | bytes 24580
  14.8 13.5 %copy-start.25 = (f32[128,16]{0,1:T(8,128)S(1)}, f32[128,16]{0,1:T(8,128)}, u32[]{:S(2)}) copy-start(f32[128,16]{0,1:T(8,128)} %param.23) | copy-start | bytes 24580
  14.8 19.4 %copy-start.9 = (f32[16,4096]{1,0:T(8,128)S(1)}, f32[16,4096]{1,0:T(8,128)}, u32[]{:S(2)}) copy-start(f32[16,4096]{1,0:T(8,128)} %param.21) | copy-start | bytes 786436
  14.9 22.1 %copy-start.10 = (f32[4,4096]{1,0:T(4,128)S(1)}, f32[4,4096]{1,0:T(4,128)}, u32[]{:S(2)}) copy-start(f32[4,4096]{1,0:T(4,128)} %param.16) | copy-start | bytes 196612
  14.9 22.1 %copy-start.28 = (bf16[128,256]{1,0:T(8,128)(2,1)S(1)}, bf16[128,256]{1,0:T(8,128)(2,1)}, u32[]{:S(2)}) copy-start(bf16[128,256]{1,0:T(8,128)(2,1)} %param.18) | copy-start | bytes 196612
  14.9 22.1 %copy-start.29 = (f32[4096]{0:T(1024)S(1)}, f32[4096]{0:T(1024)}, u32[]{:S(2)}) copy-start(f32[4096]{0:T(1024)} %param.17) | copy-start | bytes 49156
  14.9 22.1 %copy-start.30 = (f32[4096]{0:T(1024)S(1)}, f32[4096]{0:T(1024)}, u32[]{:S(2)}) copy-start(f32[4096]{0:T(1024)} %param.20) | copy-start | bytes 49156
  14.9 86.8 %all-to-all-start = ((bf16[128,32,384]{0,2,1:T(8,128)(2,1)}), bf16[128,32,384]{0,2,1:T(8,128)(2,1)}, u32[]{:S(2)}, u32[]{:S(2)}) async-start(bf16[128,32,384]{0,2,1:T(8,128)(2,1)} %pad_maximum_fusion), calls=%async_computation | async-start | bytes 6291456 | tf_op jit(solution)/shard_map/all_to_all | solution.py:37
  32.4 82.2 %copy-start.23 = (s32[512]{0:T(512)}, s32[512]{0:T(512)S(1)}, u32[]{:S(2)}) copy-start(s32[512]{0:T(512)S(1)} %iota_add_fusion.6) | copy-start | bytes 6148
  34.3 10.5 %copy-start.17 = (pred[32,32]{1,0:T(8,128)(4,1)}, pred[32,32]{1,0:T(8,128)(4,1)S(1)}, u32[]{:S(2)}) copy-start(pred[32,32]{1,0:T(8,128)(4,1)S(1)} %get-tuple-element.52) | copy-start | bytes 3076
  34.3 10.5 %copy-start.3 = (f32[16,4096]{1,0:T(8,128)}, f32[16,4096]{1,0:T(8,128)S(1)}, u32[]{:S(2)}) copy-start(f32[16,4096]{1,0:T(8,128)S(1)} %exponential_negate_fusion.rate_ref) | copy-start | bytes 786436
  106.3 18.2 %all-to-all-start.1 = ((f32[17,32,128]{2,0,1:T(8,128)}), f32[17,32,128]{2,0,1:T(8,128)S(1)}, u32[]{:S(2)}, u32[]{:S(2)}) async-start(f32[17,32,128]{2,0,1:T(8,128)} %pad_maximum_fusion.2), calls=%async_computation.1 | async-start | bytes 786432 | tf_op jit(solution)/shard_map/all_to_all | solution.py:135
  110.6 3.8 %copy-start.2 = (bf16[32,128,1,384]{3,1,0,2:T(8,128)(2,1)S(1)}, bf16[32,128,1,384]{3,1,0,2:T(8,128)(2,1)}, u32[]{:S(2)}) copy-start(bf16[32,128,1,384]{3,1,0,2:T(8,128)(2,1)} %copy.70) | copy-start | bytes 9437188
  114.4 1.6 copy-start.16
  114.4 1.6 copy-start.22
  117.3 0.8 copy-start.14
  117.3 0.8 copy-start.26
  118.1 1.5 copy-start.13
  118.1 1.5 copy-start.21
  124.0 22.0 %copy-start.7 = (bf16[4096,1,128]{2,0,1:T(8,128)(2,1)S(1)}, bf16[4096,1,128]{2,0,1:T(8,128)(2,1)}, u32[]{:S(2)}) copy-start(bf16[4096,1,128]{2,0,1:T(8,128)(2,1)} %get-tuple-element.19) | copy-start | bytes 3145732
  124.1 22.0 %copy-start.8 = (bf16[4096,1,128]{2,0,1:T(8,128)(2,1)S(1)}, bf16[4096,1,128]{2,0,1:T(8,128)(2,1)}, u32[]{:S(2)}) copy-start(bf16[4096,1,128]{2,0,1:T(8,128)(2,1)} %get-tuple-element.18) | copy-start | bytes 3145732
  132.8 13.3 %copy-start.18 = (s32[512]{0:T(512)S(1)}, s32[512]{0:T(512)}, u32[]{:S(2)}) copy-start(s32[512]{0:T(512)} %iota_add_fusion.7) | copy-start | bytes 6148
  136.6 35.8 %all-to-all-start.2 = ((f32[16,32,128]{2,0,1:T(8,128)}), f32[16,32,128]{2,0,1:T(8,128)S(1)}, u32[]{:S(2)}, u32[]{:S(2)}) async-start(f32[16,32,128]{2,0,1:T(8,128)} %bitcast.266), calls=%async_computation.2 | async-start | bytes 524288 | tf_op jit(solution)/shard_map/all_to_all | solution.py:158
  146.1 2.1 copy-start.11
  146.1 2.1 copy-start.20
  149.3 1.2 copy-start.12
  149.3 1.2 copy-start.19
  151.7 2.1 copy-start.6
  155.0 1.8 copy-start.27
  172.4 0.7 copy-start.5
  173.1 36.6 %all-to-all-start.3 = ((bf16[32,2,8192]{2,1,0:T(2,128)(2,1)}), bf16[32,2,8192]{2,1,0:T(2,128)(2,1)S(1)}, u32[]{:S(2)}, u32[]{:S(2)}) async-start(bf16[32,2,8192]{2,1,0:T(2,128)(2,1)} %reshape.379), calls=%async_computation.3 | async-start | bytes 2097152 | tf_op jit(solution)/shard_map/all_to_all | solution.py:77
  184.4 16.5 %copy-start.4 = (f32[128,4096]{1,0:T(8,128)S(1)}, f32[128,4096]{1,0:T(8,128)}, u32[]{:S(2)}) copy-start(f32[128,4096]{1,0:T(8,128)} %get-tuple-element.25) | copy-start | bytes 6291460
  184.4 16.5 %copy-start.15 = (f32[4096]{0:T(1024)S(1)}, f32[4096]{0:T(1024)}, u32[]{:S(2)}) copy-start(f32[4096]{0:T(1024)} %param.24) | copy-start | bytes 49156
  209.7 8.8 %copy-start.1 = (bf16[256,4096]{1,0:T(8,128)(2,1)S(1)}, bf16[256,4096]{1,0:T(8,128)(2,1)}, u32[]{:S(2)}) copy-start(bf16[256,4096]{1,0:T(8,128)(2,1)} %param.19) | copy-start | bytes 6291460

commit v6 on v5

--- a/solution.py
+++ b/solution.py
@@ -31,12 +31,16 @@
 
 
 def send_heads(q_three, k_three, v_three):
-    group = q_three.shape[1] // k_three.shape[1]
+    tokens, heads = q_three.shape[:2]
+    count = lax.axis_size("seq")
+    group = heads // k_three.shape[1]
     k_wide = jnp.repeat(k_three, group, axis=1)
     v_wide = jnp.repeat(v_three, group, axis=1)
-    return lax.all_to_all(
-        jnp.concatenate([q_three, k_wide, v_wide], 2), "seq", split_axis=1, concat_axis=0, tiled=True
-    )
+    joined = jnp.concatenate([q_three, k_wide, v_wide], 2).reshape(tokens, count, heads // count, -1)
+    arrived = lax.all_to_all(
+        jnp.transpose(joined, (1, 0, 2, 3)), "seq", split_axis=0, concat_axis=0, tiled=True
+    )
+    return arrived.reshape(count * tokens, heads // count, -1)
 
 
 def attend_by_heads(joined, tokens, midway):
@@ -74,8 +78,11 @@
         )
         pieces.append((summed / jnp.transpose(total)[:, :, None]).astype(jnp.bfloat16))
     merged = jnp.concatenate(pieces, 0)
-    back = lax.all_to_all(merged, "seq", split_axis=0, concat_axis=1, tiled=True)
-    return back.reshape(tokens, -1)
+    count = length // tokens
+    back = lax.all_to_all(
+        merged.reshape(count, tokens, -1), "seq", split_axis=0, concat_axis=0, tiled=True
+    )
+    return jnp.transpose(back, (1, 0, 2)).reshape(tokens, -1)
 
 
 def scan_kernel(step_ref, drive_ref, rate_ref, in_ref, out_ref, init_ref, result_ref, *, with_read):
@@ -145,7 +152,11 @@
     between = (place[None, :, None] < place[None, None, :]) & (
         place[None, None, :] < place[:, None, None]
     )
-    gap = jnp.sum(jnp.where(between[..., None], sums[None, None], 0.0), axis=2)
+    gap = jnp.dot(
+        between.reshape(count * count, count).astype(jnp.float32),
+        sums,
+        precision=lax.Precision.HIGHEST,
+    ).reshape(count, count, width)
     before = place[None, :] < place[:, None]
     weight = jnp.where(
         before[:, :, None, None], jnp.exp(rate_block[None, None] * gap[:, :, None, :]), 0.0

time: 220 us -> 200 us (0.909)
  other arithmetic: 38.6 us -> 28.9 us
  local copies, waits for them, and re-layouts: 34.1 us -> 24.4 us
    unnamed x69 -> x68, local copies, waits for them, and re-layouts: 10.3 us -> 1.88 us
    reduce_sum x1 -> x0, other arithmetic: 8.25 us -> none  [exchange_prefix(): gap = jnp.sum(jnp.where(between[..., None], sums[None, None], 0.0), axis=2)]
    concatenate x2 -> x0, other arithmetic: 3.13 us -> none  [the longest x1 1.81 us: send_heads(): jnp.concatenate([q_three, k_wide, v_wide], 2)]
    all_to_all x2 -> x1, local copies, waits for them, and re-layouts: 5.96 us -> 4.64 us  [send_heads(): lax.all_to_all(jnp.transpose(joined, (1, 0, 2, 3)), 'seq', split_axis=0,...]
  transfers between devices with their start and end apart: 5 -> 5, of which waited for: 4 -> 4; matrix products, arithmetic and copies ran while one was open for 30% -> 32% of each run, Pallas kernels for 12% -> 13%
where the time goes in v6:
time: 200 us; the launch traced here: 199 us
  waiting for transfers between devices  49.8 us (25%)
  starting transfers between devices  40.4 us (20%)
  other arithmetic  28.9 us (14%)
  matrix products  27.9 us (14%)
  Pallas kernels  26.7 us (13%)
  local copies, waits for them, and re-layouts  24.4 us (12%)
    all_to_all x1, waiting for transfers between devices, send_heads(): lax.all_to_all(jnp.transpose(joined, (1, 0, 2, 3)), 'seq', split_axis=0,...  42.2 us
    pallas_call x2, Pallas kernels, run_scan(): pl.pallas_call(functools.partial(scan_kernel, with_read=with_read), grid=...  26.7 us
    all_to_all x1, starting transfers between devices, send_heads(): lax.all_to_all(jnp.transpose(joined, (1, 0, 2, 3)), 'seq', split_axis=0,...  13.2 us
    dot_general x8, matrix products, attend_by_heads(): jnp.einsum('hij,jhd->ihd', expo.astype(jnp.bfloat16), v_all[:stop], prefe...  11.6 us
    reduce_sum x8, other arithmetic, attend_by_heads(): total = jnp.sum(expo, axis=-1)  11.2 us
    all_to_all x1, starting transfers between devices, attend_by_heads(): lax.all_to_all(merged.reshape(count, tokens, -1), 'seq', split_axis=0, co...  9.59 us
    all_to_all x1, starting transfers between devices, exchange_return(): lax.all_to_all(jnp.transpose(incoming, (1, 0, 2)), 'seq', 1, 1, tiled=True)  9.49 us
    dot_general x8, matrix products, attend_by_heads(): jnp.einsum('ihd,jhd->hij', query_block, k_all[:stop], preferred_element_t...  8.98 us
  transfers between devices with their start and end apart: 5, of which 4 were waited for; matrix products, arithmetic and copies ran while one was open for 32% of the time, Pallas kernels for 13%

profile of v6, /device:TPU:16, one launch (start us, length us, event | category | flops | bytes accessed | tf_op | source)
XLA Modules:
  0.0 199.4 jit_solution(7225143791440177185)
XLA Ops:
  0.6 1.0 slice.153
  1.7 3.8 %collective-permute-start = (bf16[3,4096]{1,0:T(4,128)(2,1)S(1)}, bf16[3,4096]{1,0:T(4,128)(2,1)S(1)}, u32[]{:S(2)}, u32[]{:S(2)}) collective-permute-start(bf16[3,4096]{1,0:T(4,128)(2,1)S(1)} %slice.153), channel_id=1, source_target_pairs={{0,1},{1,2},{2,3},{3,4},{4,5},{5,6},{6,7},{7,8},{8,9},{9,10},{10,1... | collective-permute-start | bytes 73736 | tf_op jit(solution)/shard_map/ppermute | solution.py:19
  5.5 1.6 collective-permute-done
  7.1 1.1 copy.58
  8.2 1.8 copy.59
  10.0 1.6 copy.49
  11.6 1.2 broadcast_in_dim.82
  13.0 1.8 maximum_bitcast_fusion
  14.9 13.2 %all-to-all-start = ((bf16[32,128,1,384]{1,3,2,0:T(8,128)(2,1)}), bf16[32,128,1,384]{1,3,2,0:T(8,128)(2,1)}, u32[]{:S(2)}, u32[]{:S(2)}) async-start(bf16[32,128,1,384]{1,3,2,0:T(8,128)(2,1)} %maximum_bitcast_fusion), calls=%async_computation | async-start | bytes 6291456 | tf_op jit(solution)/shard_map/all_to_all | solution.py:40
  36.8 7.0 %fusion.218 = (f32[128,4096]{1,0:T(8,128)}, f32[128,4096]{1,0:T(8,128)}, f32[4096]{0:T(1024)S(1)}, f32[128,4096]{1,0:T(8,128)}) fusion(f32[4096]{0:T(1024)S(1)} %copy-done.30, bf16[128,4096]{1,0:T(8,128)(2,1)} %param.14, f32[4096]{0:T(1024)S(1)} %bitcast.281, bf16[3,4096]{1,0:T(4,128)(2,1)S(1)} %collective-permute-done, f32[4096]{0:T(1024)S(1)} %bitcast.282, ...), kind=kOutput, calls=%fused_computation.203 | convolution fusion | flops 286257152 | bytes 9641984 | tf_op jit(solution)/shard_map/dot_general | solution.py:196
  43.8 1.3 broadcast_in_dim.78.out_ref
  45.1 1.3 broadcast_in_dim.76.in_ref
  46.4 0.7 broadcast_in_dim.80.init_ref
  47.1 10.4 %shard_map.149 = f32[16,4096]{1,0:T(8,128)} custom-call(f32[128,4096]{1,0:T(8,128)} %get-tuple-element.34.step_ref, f32[128,4096]{1,0:T(8,128)} %get-tuple-element.24.drive_ref, f32[16,4096]{1,0:T(8,128)} %copy-done.3, f32[128,16,128]{2,1,0:T(8,128)} %broadcast_in_dim.76.in_ref, f32[128,16,128]{2,1,0:T(8,128)} %broadcast_in_dim.78.out_ref, ...), custom_call_target="tpu_custom_call" | custom-call | tf_op jit(solution)/shard_map/pallas_call | solution.py:127
  57.5 1.0 copy_bitcast_fusion.1
  58.5 0.8 pad_maximum_fusion.1
  59.3 42.2 %all-to-all-done = bf16[32,128,1,384]{1,3,2,0:T(8,128)(2,1)} async-done(((bf16[32,128,1,384]{1,3,2,0:T(8,128)(2,1)}), bf16[32,128,1,384]{1,3,2,0:T(8,128)(2,1)}, u32[]{:S(2)}, u32[]{:S(2)}) %all-to-all-start) | async-done | bytes 3145760 | tf_op jit(solution)/shard_map/all_to_all | solution.py:40
  101.5 4.6 %copy.53 = bf16[32,128,1,384]{3,1,0,2:T(8,128)(2,1)} copy(bf16[32,128,1,384]{1,3,2,0:T(8,128)(2,1)} %all-to-all-done) | data formatting | bytes 6291456 | tf_op jit(solution)/shard_map/all_to_all | solution.py:40
  106.2 4.3 %all-to-all-start.1 = ((f32[17,32,128]{2,0,1:T(8,128)}), f32[17,32,128]{2,0,1:T(8,128)S(1)}, u32[]{:S(2)}, u32[]{:S(2)}) async-start(f32[17,32,128]{2,0,1:T(8,128)} %pad_maximum_fusion.1), calls=%async_computation.1 | async-start | bytes 786432 | tf_op jit(solution)/shard_map/all_to_all | solution.py:142
  110.5 3.8 %fusion.219 = (bf16[4096,1,128]{2,0,1:T(8,128)(2,1)}, bf16[4096,1,128]{2,0,1:T(8,128)(2,1)}, bf16[4096,1,128]{2,0,1:T(8,128)(2,1)}) fusion(bf16[4096,1,384]{2,0,1:T(8,128)(2,1)} %bitcast.261), kind=kLoop, calls=%fused_computation.204 | loop fusion | bytes 6291456 | tf_op jit(solution)/shard_map/slice | solution.py:49
  114.9 1.0 fusion.61
  117.2 0.8 fusion.57
  118.1 0.7 fusion.222
  118.8 0.8 fusion.21
  119.6 0.9 fusion.14
  120.5 1.2 fusion.19
  121.7 0.9 fusion.131
  122.7 1.3 fusion.107
  124.8 3.0 %multiply_reduce_fusion = f32[32,16,128]{2,1,0:T(8,128)} fusion(f32[32,16,128]{2,1,0:T(8,128)S(1)} %slice_bitcast_fusion, f32[32,32,128]{2,1,0:T(8,128)S(1)} %fusion.169, f32[16,128]{1,0:T(8,128)S(1)} %copy-done.26, pred[32,32]{1,0:T(8,128)(4,1)S(1)} %copy-done.15), kind=kLoop, calls=%fused_computation.5 | loop fusion | flops 8323072 | bytes 1057792 | tf_op jit(solution)/shard_map/reduce_sum | solution.py:164
  127.9 9.5 %all-to-all-start.2 = ((f32[16,32,128]{2,0,1:T(8,128)}), f32[16,32,128]{2,0,1:T(8,128)S(1)}, u32[]{:S(2)}, u32[]{:S(2)}) async-start(f32[16,32,128]{2,0,1:T(8,128)} %bitcast.17), calls=%async_computation.2 | async-start | bytes 524288 | tf_op jit(solution)/shard_map/all_to_all | solution.py:169
  137.4 2.7 %fusion = (f32[512]{0:T(512)S(1)}, f32[512,4096]{1,0:T(8,128)S(1)}) fusion(s32[512]{0:T(512)S(1)} %copy-done.18, bf16[4096,1,128]{2,0,1:T(8,128)(2,1)S(1)} %copy-done.5, bf16[4096,1,128]{2,0,1:T(8,128)(2,1)} %get-tuple-element.18), kind=kOutput, calls=%fused_computation.8 | convolution fusion | flops 545259008 | bytes 9572352 | tf_op jit(solution)/shard_map/ihd,jhd->hij/dot_general | solution.py:62
  140.1 1.1 fusion.223
  141.2 1.2 fusion.8
  142.4 1.3 fusion.3
  143.6 2.1 %fusion.10 = f32[512]{0:T(512)S(1)} fusion(f32[512,3072]{1,0:T(8,128)S(1)} %get-tuple-element.46, f32[512]{0:T(512)S(1)} %get-tuple-element.45, s32[3072]{0:T(1024)S(1)} %copy-done.11, s32[512]{0:T(512)S(1)} %copy-done.19), kind=kLoop, calls=%fused_computation.25 | loop fusion | flops 9436672 | bytes 6309888 | tf_op jit(solution)/shard_map/reduce_sum | solution.py:72
  145.7 1.2 fusion.83
  147.0 1.8 fusion.95
  148.8 1.4 fusion.224
  150.2 2.2 %fusion.1 = f32[512]{0:T(512)S(1)} fusion(f32[512,3584]{1,0:T(8,128)S(1)} %get-tuple-element.48, f32[512]{0:T(512)S(1)} %get-tuple-element.47, s32[3584]{0:T(1024)S(1)} %iota_add_fusion, s32[512]{0:T(512)S(1)} %copy-done.28), kind=kLoop, calls=%fused_computation.12 | loop fusion | flops 7339520 | bytes 7360512 | tf_op jit(solution)/shard_map/reduce_sum | solution.py:72
  152.4 1.6 fusion.71
  154.0 2.8 %fusion.4 = f32[512]{0:T(512)S(1)} fusion(f32[512,4096]{1,0:T(8,128)S(1)} %get-tuple-element.50, f32[512]{0:T(512)S(1)} %get-tuple-element.49, s32[512]{0:T(512)S(1)} %copy-done.18), kind=kLoop, calls=%fused_computation.18 | loop fusion | flops 12582400 | bytes 8394752 | tf_op jit(solution)/shard_map/reduce_sum | solution.py:72
  156.9 2.9 %fusion.119 = bf16[4096,1,128]{0,2,1:T(8,128)(2,1)S(1)} fusion(bf16[4096,1,128]{0,2,1:T(8,128)(2,1)S(1)} %fusion.71, f32[512,4096]{1,0:T(8,128)S(1)} %get-tuple-element.50, f32[512]{0:T(512)S(1)} %get-tuple-element.49, s32[512]{0:T(512)S(1)} %copy-done.18, bf16[4096,1,128]{2,0,1:T(8,128)(2,1)S(1)} %copy-done.4, f32[512]{0:T(512)S(1)} %fusion.4), kind=kOutput, calls=%fused_computation.91 | convolution fusion | flops 549584896 | bytes 9574400 | tf_op jit(solution)/shard_map/hij,jhd->ihd/dot_general | solution.py:73
  160.0 1.4 copy.56
  161.4 9.6 %all-to-all-start.3 = ((bf16[32,128,128]{1,2,0:T(8,128)(2,1)}), bf16[32,128,128]{1,2,0:T(8,128)(2,1)S(1)}, u32[]{:S(2)}, u32[]{:S(2)}) async-start(bf16[32,128,128]{1,2,0:T(8,128)(2,1)} %copy.56), calls=%async_computation.3 | async-start | bytes 2097152 | tf_op jit(solution)/shard_map/all_to_all | solution.py:82
  171.8 16.3 %shard_map.150 = f32[128,4096]{1,0:T(8,128)} custom-call(f32[128,4096]{1,0:T(8,128)} %get-tuple-element.34.step_ref, f32[128,4096]{1,0:T(8,128)} %get-tuple-element.24.drive_ref, f32[16,4096]{1,0:T(8,128)} %copy-done.3, f32[128,16,128]{2,1,0:T(8,128)} %broadcast_in_dim.76.in_ref, f32[128,16,128]{2,1,0:T(8,128)} %broadcast_in_dim.78.out_ref, ...), custom_call_target="tpu_custom_call" | custom-call | tf_op jit(solution)/shard_map/pallas_call | solution.py:127
  188.1 4.3 %fusion.27 = bf16[128,4096]{1,0:T(8,128)(2,1)} fusion(bf16[128,4096]{1,0:T(8,128)(2,1)} %param.15, f32[128,4096]{1,0:T(8,128)} %shard_map.150, f32[128,4096]{1,0:T(8,128)} %get-tuple-element.25, f32[4096]{0:T(1024)S(1)} %copy-done.14), kind=kLoop, calls=%fused_computation.46 | loop fusion | flops 4718592 | bytes 6307840 | tf_op jit(solution)/shard_map/convert_element_type | solution.py:223
  192.4 5.6 %all-to-all-done.3 = bf16[32,128,128]{1,2,0:T(8,128)(2,1)S(1)} async-done(((bf16[32,128,128]{1,2,0:T(8,128)(2,1)}), bf16[32,128,128]{1,2,0:T(8,128)(2,1)S(1)}, u32[]{:S(2)}, u32[]{:S(2)}) %all-to-all-start.3) | async-done | bytes 1048608 | tf_op jit(solution)/shard_map/all_to_all | solution.py:82
  198.1 1.3 copy.57
  (96 shorter events, 12.5 us)
Async XLA Ops:
  0.6 36.1 %copy-start = (bf16[256,4096]{1,0:T(8,128)(2,1)S(1)}, bf16[256,4096]{1,0:T(8,128)(2,1)}, u32[]{:S(2)}) copy-start(bf16[256,4096]{1,0:T(8,128)(2,1)} %param.19) | copy-start | bytes 6291460
  1.7 5.4 %collective-permute-start = (bf16[3,4096]{1,0:T(4,128)(2,1)S(1)}, bf16[3,4096]{1,0:T(4,128)(2,1)S(1)}, u32[]{:S(2)}, u32[]{:S(2)}) collective-permute-start(bf16[3,4096]{1,0:T(4,128)(2,1)S(1)} %slice.153), channel_id=1, source_target_pairs={{0,1},{1,2},{2,3},{3,4},{4,5},{5,6},{6,7},{7,8},{8,9},{9,10},{10,1... | collective-permute-start | bytes 73736 | tf_op jit(solution)/shard_map/ppermute | solution.py:19
  14.8 13.2 %copy-start.24 = (f32[128,16]{0,1:T(8,128)S(1)}, f32[128,16]{0,1:T(8,128)}, u32[]{:S(2)}) copy-start(f32[128,16]{0,1:T(8,128)} %param.22) | copy-start | bytes 24580
  14.8 13.4 %copy-start.25 = (f32[128,16]{0,1:T(8,128)S(1)}, f32[128,16]{0,1:T(8,128)}, u32[]{:S(2)}) copy-start(f32[128,16]{0,1:T(8,128)} %param.23) | copy-start | bytes 24580
  14.8 19.9 %copy-start.8 = (f32[16,4096]{1,0:T(8,128)S(1)}, f32[16,4096]{1,0:T(8,128)}, u32[]{:S(2)}) copy-start(f32[16,4096]{1,0:T(8,128)} %param.21) | copy-start | bytes 786436
  14.8 21.8 %copy-start.9 = (f32[4,4096]{1,0:T(4,128)S(1)}, f32[4,4096]{1,0:T(4,128)}, u32[]{:S(2)}) copy-start(f32[4,4096]{1,0:T(4,128)} %param.16) | copy-start | bytes 196612
  14.9 21.9 %copy-start.29 = (bf16[128,256]{1,0:T(8,128)(2,1)S(1)}, bf16[128,256]{1,0:T(8,128)(2,1)}, u32[]{:S(2)}) copy-start(bf16[128,256]{1,0:T(8,128)(2,1)} %param.18) | copy-start | bytes 196612
  14.9 21.9 %copy-start.30 = (f32[4096]{0:T(1024)S(1)}, f32[4096]{0:T(1024)}, u32[]{:S(2)}) copy-start(f32[4096]{0:T(1024)} %param.17) | copy-start | bytes 49156
  14.9 21.9 %copy-start.31 = (f32[4096]{0:T(1024)S(1)}, f32[4096]{0:T(1024)}, u32[]{:S(2)}) copy-start(f32[4096]{0:T(1024)} %param.20) | copy-start | bytes 49156
  14.9 86.7 %all-to-all-start = ((bf16[32,128,1,384]{1,3,2,0:T(8,128)(2,1)}), bf16[32,128,1,384]{1,3,2,0:T(8,128)(2,1)}, u32[]{:S(2)}, u32[]{:S(2)}) async-start(bf16[32,128,1,384]{1,3,2,0:T(8,128)(2,1)} %maximum_bitcast_fusion), calls=%async_computation | async-start | bytes 6291456 | tf_op jit(solution)/shard_map/all_to_all | solution.py:40
  32.4 82.3 %copy-start.23 = (s32[512]{0:T(512)}, s32[512]{0:T(512)S(1)}, u32[]{:S(2)}) copy-start(s32[512]{0:T(512)S(1)} %iota_add_fusion.6) | copy-start | bytes 6148
  34.8 9.0 %copy-start.3 = (f32[16,4096]{1,0:T(8,128)}, f32[16,4096]{1,0:T(8,128)S(1)}, u32[]{:S(2)}) copy-start(f32[16,4096]{1,0:T(8,128)S(1)} %exponential_negate_fusion.rate_ref) | copy-start | bytes 786436
  106.2 18.2 %all-to-all-start.1 = ((f32[17,32,128]{2,0,1:T(8,128)}), f32[17,32,128]{2,0,1:T(8,128)S(1)}, u32[]{:S(2)}, u32[]{:S(2)}) async-start(f32[17,32,128]{2,0,1:T(8,128)} %pad_maximum_fusion.1), calls=%async_computation.1 | async-start | bytes 786432 | tf_op jit(solution)/shard_map/all_to_all | solution.py:142
  110.5 3.8 %copy-start.2 = (bf16[32,128,1,384]{3,1,0,2:T(8,128)(2,1)S(1)}, bf16[32,128,1,384]{3,1,0,2:T(8,128)(2,1)}, u32[]{:S(2)}) copy-start(bf16[32,128,1,384]{3,1,0,2:T(8,128)(2,1)} %copy.53) | copy-start | bytes 9437188
  114.3 1.7 copy-start.17
  114.3 1.7 copy-start.22
  117.2 0.8 copy-start.13
  117.2 0.8 copy-start.27
  118.0 1.5 copy-start.12
  118.1 1.5 copy-start.21
  122.7 1.8 copy-start.15
  122.7 1.8 copy-start.16
  122.7 2.2 %copy-start.26 = (f32[16,128]{1,0:T(8,128)S(1)}, f32[16,128]{1,0:T(8,128)}, u32[]{:S(2)}) copy-start(f32[16,128]{1,0:T(8,128)} %constant_dynamic-slice_fusion) | copy-start | bytes 24580
  124.0 13.3 %copy-start.5 = (bf16[4096,1,128]{2,0,1:T(8,128)(2,1)S(1)}, bf16[4096,1,128]{2,0,1:T(8,128)(2,1)}, u32[]{:S(2)}) copy-start(bf16[4096,1,128]{2,0,1:T(8,128)(2,1)} %get-tuple-element.19) | copy-start | bytes 3145732
  124.0 13.3 %copy-start.18 = (s32[512]{0:T(512)S(1)}, s32[512]{0:T(512)}, u32[]{:S(2)}) copy-start(s32[512]{0:T(512)} %iota_add_fusion.7) | copy-start | bytes 6148
  127.9 33.6 %all-to-all-start.2 = ((f32[16,32,128]{2,0,1:T(8,128)}), f32[16,32,128]{2,0,1:T(8,128)S(1)}, u32[]{:S(2)}, u32[]{:S(2)}) async-start(f32[16,32,128]{2,0,1:T(8,128)} %bitcast.17), calls=%async_computation.2 | async-start | bytes 524288 | tf_op jit(solution)/shard_map/all_to_all | solution.py:169
  137.4 2.7 %copy-start.7 = (bf16[4096,1,128]{2,0,1:T(8,128)(2,1)S(1)}, bf16[4096,1,128]{2,0,1:T(8,128)(2,1)}, u32[]{:S(2)}) copy-start(bf16[4096,1,128]{2,0,1:T(8,128)(2,1)} %get-tuple-element.18) | copy-start | bytes 3145732
  137.4 2.7 %copy-start.10 = (s32[2560]{0:T(1024)S(1)}, s32[2560]{0:T(1024)}, u32[]{:S(2)}) copy-start(s32[2560]{0:T(1024)} %iota_add_fusion.2) | copy-start | bytes 30724
  137.4 2.7 %copy-start.20 = (s32[512]{0:T(512)S(1)}, s32[512]{0:T(512)}, u32[]{:S(2)}) copy-start(s32[512]{0:T(512)} %iota_add_fusion.10) | copy-start | bytes 6148
  141.2 1.2 copy-start.11
  141.2 1.2 copy-start.19
  143.6 2.1 %copy-start.4 = (bf16[4096,1,128]{2,0,1:T(8,128)(2,1)S(1)}, bf16[4096,1,128]{2,0,1:T(8,128)(2,1)}, u32[]{:S(2)}) copy-start(bf16[4096,1,128]{2,0,1:T(8,128)(2,1)} %get-tuple-element.17) | copy-start | bytes 3145732
  147.0 1.8 copy-start.6
  147.0 1.8 copy-start.28
  161.4 36.6 %all-to-all-start.3 = ((bf16[32,128,128]{1,2,0:T(8,128)(2,1)}), bf16[32,128,128]{1,2,0:T(8,128)(2,1)S(1)}, u32[]{:S(2)}, u32[]{:S(2)}) async-start(bf16[32,128,128]{1,2,0:T(8,128)(2,1)} %copy.56), calls=%async_computation.3 | async-start | bytes 2097152 | tf_op jit(solution)/shard_map/all_to_all | solution.py:82
  171.8 16.3 %copy-start.14 = (f32[4096]{0:T(1024)S(1)}, f32[4096]{0:T(1024)}, u32[]{:S(2)}) copy-start(f32[4096]{0:T(1024)} %param.24) | copy-start | bytes 49156
  188.1 11.3 %copy-start.1 = (bf16[256,4096]{1,0:T(8,128)(2,1)S(1)}, bf16[256,4096]{1,0:T(8,128)(2,1)}, u32[]{:S(2)}) copy-start(bf16[256,4096]{1,0:T(8,128)(2,1)} %param.19) | copy-start | bytes 6291460

commit v7 on v6

--- a/solution.py
+++ b/solution.py
@@ -43,41 +43,73 @@
     return arrived.reshape(count * tokens, heads // count, -1)
 
 
-def attend_by_heads(joined, tokens, midway):
-    q_all = joined[:, :, :HEAD_DIM]
-    k_all = joined[:, :, HEAD_DIM : 2 * HEAD_DIM]
-    v_all = joined[:, :, 2 * HEAD_DIM :]
-    length = q_all.shape[0]
-    width = math.gcd(length, 512)
-    scale = HEAD_DIM ** (-0.5)
-    columns = jnp.arange(length)
-
-    pieces = []
-    for index in range(length // width):
-        if index == length // width // 2:
-            q_all, k_all, v_all = midway(q_all, k_all, v_all)
-        stop = (index + 1) * width
-        query_block = q_all[stop - width : stop]
-        scores = (
-            jnp.einsum(
-                "ihd,jhd->hij", query_block, k_all[:stop], preferred_element_type=jnp.float32
-            )
-            * scale
+def attention_kernel(q_ref, k_ref, v_ref, o_ref, *, tile, scale, first):
+    index = pl.program_id(1) + first
+    query = q_ref[0]
+    rows = lax.broadcasted_iota(jnp.int32, (tile, tile), 0)
+    cols = lax.broadcasted_iota(jnp.int32, (tile, tile), 1)
+    diagonal = rows >= cols
+
+    def scores(j):
+        keys = k_ref[0, pl.ds(pl.multiple_of(j * tile, tile), tile), :]
+        product = lax.dot_general(
+            query, keys, (((1,), (1,)), ((), ())), preferred_element_type=jnp.float32
         )
-        rows = stop - width + jnp.arange(width)
-        allowed = rows[:, None] >= columns[None, :stop]
-        masked = jnp.where(allowed[None], scores, -1e30)
-        peak = jnp.max(masked, axis=-1, keepdims=True)
-        expo = jnp.where(allowed[None], jnp.exp(masked - peak), 0.0)
-        total = jnp.sum(expo, axis=-1)
-        summed = jnp.einsum(
-            "hij,jhd->ihd",
-            expo.astype(jnp.bfloat16),
-            v_all[:stop],
+        return product * scale
+
+    def peak_step(j, peak):
+        return jnp.maximum(peak, jnp.max(scores(j), axis=1, keepdims=True))
+
+    peak = jnp.full((tile, 1), -jnp.inf, jnp.float32)
+    peak = lax.fori_loop(0, index, peak_step, peak)
+    last = jnp.where(diagonal, scores(index), -1e30)
+    peak = jnp.maximum(peak, jnp.max(last, axis=1, keepdims=True))
+
+    def add_block(j, expo, carry):
+        total, summed = carry
+        values = v_ref[0, pl.ds(pl.multiple_of(j * tile, tile), tile), :]
+        summed = summed + lax.dot_general(
+            expo.astype(jnp.bfloat16), values, (((1,), (0,)), ((), ())),
             preferred_element_type=jnp.float32,
         )
-        pieces.append((summed / jnp.transpose(total)[:, :, None]).astype(jnp.bfloat16))
-    merged = jnp.concatenate(pieces, 0)
+        return total + jnp.sum(expo, axis=1, keepdims=True), summed
+
+    def sum_step(j, carry):
+        return add_block(j, jnp.exp(scores(j) - peak), carry)
+
+    carry = (jnp.zeros((tile, 1), jnp.float32), jnp.zeros((tile, HEAD_DIM), jnp.float32))
+    carry = lax.fori_loop(0, index, sum_step, carry)
+    expo = jnp.where(diagonal, jnp.exp(last - peak), 0.0)
+    total, summed = add_block(index, expo, carry)
+    o_ref[0] = (summed / total).astype(o_ref.dtype)
+
+
+def attend_heads(q_all, k_all, v_all, first, blocks):
+    heads, length, _ = q_all.shape
+    tile = length // blocks
+    head_spec = pl.BlockSpec((1, length, HEAD_DIM), lambda h, i: (h, 0, 0))
+    tile_spec = pl.BlockSpec((1, tile, HEAD_DIM), lambda h, i: (h, i + first, 0))
+    out_spec = pl.BlockSpec((1, tile, HEAD_DIM), lambda h, i: (h, i, 0))
+    return pl.pallas_call(
+        functools.partial(attention_kernel, tile=tile, scale=HEAD_DIM ** (-0.5), first=first),
+        grid=(heads, blocks // 2),
+        in_specs=[tile_spec, head_spec, head_spec],
+        out_specs=out_spec,
+        out_shape=jax.ShapeDtypeStruct((heads, length // 2, HEAD_DIM), jnp.bfloat16),
+        interpret=INTERPRET,
+    )(q_all, k_all, v_all)
+
+
+def attend_by_heads(joined, tokens, midway):
+    length = joined.shape[0]
+    blocks = length // math.gcd(length, 512)
+    heads_first = [jnp.transpose(x, (1, 0, 2)) for x in (
+        joined[:, :, :HEAD_DIM], joined[:, :, HEAD_DIM : 2 * HEAD_DIM], joined[:, :, 2 * HEAD_DIM :]
+    )]
+    early, heads_first = midway(attend_heads(*heads_first, 0, blocks), heads_first)
+    late = attend_heads(*heads_first, blocks // 2, blocks)
+    merged = jnp.transpose(jnp.concatenate([early, late], 1), (1, 0, 2))
+    length = merged.shape[0]
     count = length // tokens
     back = lax.all_to_all(
         merged.reshape(count, tokens, -1), "seq", split_axis=0, concat_axis=0, tiled=True
@@ -211,9 +243,10 @@
     gathered, joined = exchange_send(jnp.sum(step, axis=0), local_end, joined)
     prefix = []
 
-    def midway(q_all, k_all, v_all):
-        prefix.append(exchange_prefix(gathered, rate))
-        return lax.optimization_barrier((prefix[0], q_all, k_all, v_all))[1:]
+    def midway(early, heads_first):
+        arrived, early = lax.optimization_barrier((gathered, early))
+        prefix.append(exchange_prefix(arrived, rate))
+        return lax.optimization_barrier((early, prefix[0], heads_first))[::2]
 
     attention_out = attend_by_heads(joined, tokens, midway)
     incoming = exchange_return(prefix[0])

time: 200 us -> 205 us (1.025)
  Pallas kernels: 26.7 us -> 63.6 us
  matrix products: 27.9 us -> 7.39 us
  other arithmetic: 28.9 us -> 11.9 us
  waiting for transfers between devices: 49.8 us -> 57.8 us
  local copies, waits for them, and re-layouts: 24.4 us -> 21.8 us
    pallas_call x0 -> x2, Pallas kernels: none -> 36.9 us  [attend_heads(): pl.pallas_call(functools.partial(attention_kernel, tile=tile, scale=HEAD_...]
    dot_general x16 -> x0, matrix products: 20.6 us -> none  [the longest x8 11.6 us: attend_by_heads(): jnp.einsum('hij,jhd->ihd', expo.astype(jnp.bfloat16), v_all[:stop], prefe...]
    reduce_sum x8 -> x0, other arithmetic: 11.2 us -> none  [attend_by_heads(): total = jnp.sum(expo, axis=-1)]
    transpose x0 -> x2, local copies, waits for them, and re-layouts: none -> 8.27 us  [the longest x1 4.67 us: send_heads(): jnp.transpose(joined, (1, 0, 2, 3))]
    all_to_all x1, waiting for transfers between devices: 42.2 us -> 50.4 us  [send_heads(): lax.all_to_all(jnp.transpose(joined, (1, 0, 2, 3)), 'seq', split_axis=0,...]
    all_to_all x1 -> x0, local copies, waits for them, and re-layouts: 4.64 us -> none  [send_heads(): lax.all_to_all(jnp.transpose(joined, (1, 0, 2, 3)), 'seq', split_axis=0,...]
    add x7 -> x0, other arithmetic: 4.06 us -> none  [attend_by_heads(): rows = stop - width + jnp.arange(width)]
    slice x2 -> x0, local copies, waits for them, and re-layouts: 3.81 us -> none  [the longest x1 3.8 us: attend_by_heads(): v_all = joined[:, :, 2 * HEAD_DIM:]]
  transfers between devices with their start and end apart: 5 -> 5, of which waited for: 4 -> 3; matrix products, arithmetic and copies ran while one was open for 32% -> 11% of each run, Pallas kernels for 13% -> 31%
where the time goes in v7:
time: 205 us; the launch traced here: 204 us
  Pallas kernels  63.6 us (31%)
  waiting for transfers between devices  57.8 us (28%)
  starting transfers between devices  40.8 us (20%)
  local copies, waits for them, and re-layouts  21.8 us (11%)
  other arithmetic  11.9 us (6%)
  matrix products  7.39 us (4%)
    all_to_all x1, waiting for transfers between devices, send_heads(): lax.all_to_all(jnp.transpose(joined, (1, 0, 2, 3)), 'seq', split_axis=0,...  50.4 us
    pallas_call x2, Pallas kernels, attend_heads(): pl.pallas_call(functools.partial(attention_kernel, tile=tile, scale=HEAD_...  36.9 us
    pallas_call x2, Pallas kernels, run_scan(): pl.pallas_call(functools.partial(scan_kernel, with_read=with_read), grid=...  26.7 us
    all_to_all x1, starting transfers between devices, send_heads(): lax.all_to_all(jnp.transpose(joined, (1, 0, 2, 3)), 'seq', split_axis=0,...  13.2 us
    all_to_all x1, starting transfers between devices, exchange_return(): lax.all_to_all(jnp.transpose(incoming, (1, 0, 2)), 'seq', 1, 1, tiled=True)  9.92 us
    all_to_all x1, starting transfers between devices, attend_by_heads(): lax.all_to_all(merged.reshape(count, tokens, -1), 'seq', split_axis=0, co...  9.78 us
    dot_general x1, matrix products, per_device(): jnp.dot(step_low, step_proj, preferred_element_type=jnp.float32)  7.04 us
    all_to_all x1, waiting for transfers between devices, attend_by_heads(): lax.all_to_all(merged.reshape(count, tokens, -1), 'seq', split_axis=0, co...  5.8 us
  transfers between devices with their start and end apart: 5, of which 3 were waited for; matrix products, arithmetic and copies ran while one was open for 11% of the time, Pallas kernels for 31%

profile of v7, /device:TPU:16, one launch (start us, length us, event | category | flops | bytes accessed | tf_op | source)
XLA Modules:
  0.0 204.2 jit_solution(15135274945626385840)
XLA Ops:
  0.6 0.0 copy-start
  0.6 1.0 slice.40
  1.7 3.8 %collective-permute-start = (bf16[3,4096]{1,0:T(4,128)(2,1)S(1)}, bf16[3,4096]{1,0:T(4,128)(2,1)S(1)}, u32[]{:S(2)}, u32[]{:S(2)}) collective-permute-start(bf16[3,4096]{1,0:T(4,128)(2,1)S(1)} %slice.40), channel_id=1, source_target_pairs={{0,1},{1,2},{2,3},{3,4},{4,5},{5,6},{6,7},{7,8},{8,9},{9,10},{10,1... | collective-permute-start | bytes 73736 | tf_op jit(solution)/shard_map/ppermute | solution.py:19
  5.5 1.6 collective-permute-done
  7.1 1.8 copy.51
  8.9 1.1 copy.52
  10.0 1.6 copy.44
  11.6 1.2 broadcast_in_dim.22
  12.8 0.2 broadcast_in_dim.23
  13.0 1.8 maximum_bitcast_fusion
  14.8 4.7 %copy.47 = bf16[32,128,1,384]{3,1,2,0:T(8,128)(2,1)} copy(bf16[32,128,1,384]{1,3,0,2:T(8,128)(2,1)} %maximum_bitcast_fusion) | data formatting | bytes 6291456 | tf_op jit(solution)/shard_map/transpose | solution.py:41
  19.5 0.0 copy-start.8
  19.5 0.0 copy-start.9
  19.5 0.0 copy-start.10
  19.5 13.2 %all-to-all-start = ((bf16[32,128,1,384]{3,1,2,0:T(8,128)(2,1)}), bf16[32,128,1,384]{3,1,2,0:T(8,128)(2,1)}, u32[]{:S(2)}, u32[]{:S(2)}) async-start(bf16[32,128,1,384]{3,1,2,0:T(8,128)(2,1)} %copy.47), calls=%async_computation | async-start | bytes 6291456 | tf_op jit(solution)/shard_map/all_to_all | solution.py:40
  32.7 0.0 copy-done.6
  32.7 0.1 copy.41
  32.8 0.0 copy-done.7
  32.9 0.1 copy.42
  33.0 0.0 copy-done.3
  33.0 0.0 copy-start.1
  33.1 0.0 copy-done.4
  33.2 7.0 %fusion.11 = (f32[128,4096]{1,0:T(8,128)}, f32[128,4096]{1,0:T(8,128)}, f32[4096]{0:T(1024)S(1)}, f32[128,4096]{1,0:T(8,128)}) fusion(f32[4096]{0:T(1024)S(1)} %copy-done.9, bf16[128,4096]{1,0:T(8,128)(2,1)} %param.14, f32[4096]{0:T(1024)S(1)} %bitcast.54, bf16[3,4096]{1,0:T(4,128)(2,1)S(1)} %collective-permute-done, f32[4096]{0:T(1024)S(1)} %bitcast.55, ...), kind=kOutput, calls=%fused_computation.35 | convolution fusion | flops 286257152 | bytes 9641984 | tf_op jit(solution)/shard_map/dot_general | solution.py:228
  40.2 0.0 copy-done.1
  40.2 1.3 broadcast_in_dim.18.in_ref
  41.5 1.3 broadcast_in_dim.19.out_ref
  42.8 0.7 broadcast_in_dim.21.init_ref
  43.6 10.4 %shard_map.149 = f32[16,4096]{1,0:T(8,128)} custom-call(f32[128,4096]{1,0:T(8,128)} %get-tuple-element.36.step_ref, f32[128,4096]{1,0:T(8,128)} %get-tuple-element.26.drive_ref, f32[16,4096]{1,0:T(8,128)} %copy-done.1, f32[128,16,128]{2,1,0:T(8,128)} %broadcast_in_dim.18.in_ref, f32[128,16,128]{2,1,0:T(8,128)} %broadcast_in_dim.19.out_ref, ...), custom_call_target="tpu_custom_call" | custom-call | tf_op jit(solution)/shard_map/pallas_call | solution.py:159
  54.0 1.0 copy_bitcast_fusion.2
  54.9 0.8 pad_maximum_fusion.2
  55.8 50.4 %all-to-all-done = bf16[32,128,1,384]{3,1,2,0:T(8,128)(2,1)} async-done(((bf16[32,128,1,384]{3,1,2,0:T(8,128)(2,1)}), bf16[32,128,1,384]{3,1,2,0:T(8,128)(2,1)}, u32[]{:S(2)}, u32[]{:S(2)}) %all-to-all-start) | async-done | bytes 3145760 | tf_op jit(solution)/shard_map/all_to_all | solution.py:40
  106.2 4.1 %all-to-all-start.1 = ((f32[17,32,128]{2,0,1:T(8,128)}), f32[17,32,128]{2,0,1:T(8,128)S(1)}, u32[]{:S(2)}, u32[]{:S(2)}) async-start(f32[17,32,128]{2,0,1:T(8,128)} %pad_maximum_fusion.2), calls=%async_computation.1 | async-start | bytes 786432 | tf_op jit(solution)/shard_map/all_to_all | solution.py:174
  110.3 3.6 %slice_bitcast_fusion = (bf16[1,4096,128]{2,1,0:T(8,128)(2,1)}, bf16[1,4096,128]{2,1,0:T(8,128)(2,1)}, bf16[1,4096,128]{2,1,0:T(8,128)(2,1)}) fusion(bf16[4096,1,384]{2,0,1:T(8,128)(2,1)} %bitcast.12), kind=kLoop, calls=%fused_computation.19 | loop fusion | bytes 6291456 | tf_op jit(solution)/shard_map/transpose | solution.py:106
  113.9 11.1 %shard_map.150 = bf16[1,2048,128]{2,1,0:T(8,128)(2,1)} custom-call(bf16[1,4096,128]{2,1,0:T(8,128)(2,1)} %get-tuple-element.23.q_ref, bf16[1,4096,128]{2,1,0:T(8,128)(2,1)} %get-tuple-element.24.k_ref, bf16[1,4096,128]{2,1,0:T(8,128)(2,1)} %get-tuple-element.25.v_ref), custom_call_target="tpu_custom_call" | custom-call | tf_op jit(solution)/shard_map/pallas_call | solution.py:93
  125.1 0.0 all-to-all-done.1
  125.1 0.1 copy.48
  125.1 0.3 fusion.7
  125.5 3.0 %multiply_reduce_fusion = f32[32,16,128]{2,1,0:T(8,128)} fusion(f32[32,16,128]{2,1,0:T(8,128)S(1)} %slice_bitcast_fusion.3, f32[32,32,128]{2,1,0:T(8,128)S(1)} %fusion.7, f32[16,128]{1,0:T(8,128)S(1)} %constant_dynamic-slice_fusion, pred[32,32]{1,0:T(8,128)(4,1)S(1)} %get-tuple-element.38), kind=kLoop, calls=%fused_computation | loop fusion | flops 8323072 | bytes 1057792 | tf_op jit(solution)/shard_map/reduce_sum | solution.py:196
  128.5 9.9 %all-to-all-start.2 = ((f32[16,32,128]{2,0,1:T(8,128)}), f32[16,32,128]{2,0,1:T(8,128)S(1)}, u32[]{:S(2)}, u32[]{:S(2)}) async-start(f32[16,32,128]{2,0,1:T(8,128)} %bitcast.19), calls=%async_computation.2 | async-start | bytes 524288 | tf_op jit(solution)/shard_map/all_to_all | solution.py:201
  138.4 25.7 %shard_map.152 = bf16[1,2048,128]{2,1,0:T(8,128)(2,1)} custom-call(bf16[1,4096,128]{2,1,0:T(8,128)(2,1)} %get-tuple-element.23.q_ref, bf16[1,4096,128]{2,1,0:T(8,128)(2,1)} %get-tuple-element.24.k_ref, bf16[1,4096,128]{2,1,0:T(8,128)(2,1)} %get-tuple-element.25.v_ref), custom_call_target="tpu_custom_call" | custom-call | tf_op jit(solution)/shard_map/pallas_call | solution.py:93
  164.2 2.1 %pad_maximum_fusion.1 = bf16[1,4096,128]{2,1,0:T(8,128)(2,1)} fusion(bf16[1,2048,128]{2,1,0:T(8,128)(2,1)} %shard_map.152, bf16[1,2048,128]{2,1,0:T(8,128)(2,1)S(1)} %copy-done.2), kind=kLoop, calls=%fused_computation.18 | loop fusion | flops 2097152 | bytes 2097152 | tf_op jit(solution)/shard_map/concatenate | solution.py:111
  166.2 0.0 all-to-all-done.2
  166.2 9.8 %all-to-all-start.3 = ((bf16[32,128,128]{2,1,0:T(8,128)(2,1)}), bf16[32,128,128]{2,1,0:T(8,128)(2,1)S(1)}, u32[]{:S(2)}, u32[]{:S(2)}) async-start(bf16[32,128,128]{2,1,0:T(8,128)(2,1)} %bitcast.20), calls=%async_computation.3 | async-start | bytes 2097152 | tf_op jit(solution)/shard_map/all_to_all | solution.py:114
  176.0 0.7 copy_bitcast_fusion.1.init_ref
  176.8 16.3 %shard_map.151 = f32[128,4096]{1,0:T(8,128)} custom-call(f32[128,4096]{1,0:T(8,128)} %get-tuple-element.36.step_ref, f32[128,4096]{1,0:T(8,128)} %get-tuple-element.26.drive_ref, f32[16,4096]{1,0:T(8,128)} %copy-done.1, f32[128,16,128]{2,1,0:T(8,128)} %broadcast_in_dim.18.in_ref, f32[128,16,128]{2,1,0:T(8,128)} %broadcast_in_dim.19.out_ref, ...), custom_call_target="tpu_custom_call" | custom-call | tf_op jit(solution)/shard_map/pallas_call | solution.py:159
  193.1 4.2 %fusion.4 = bf16[128,4096]{1,0:T(8,128)(2,1)} fusion(bf16[128,4096]{1,0:T(8,128)(2,1)} %param.15, f32[128,4096]{1,0:T(8,128)} %shard_map.151, f32[128,4096]{1,0:T(8,128)} %get-tuple-element.27, f32[4096]{0:T(1024)S(1)} %copy-done.5), kind=kLoop, calls=%fused_computation.11 | loop fusion | flops 4718592 | bytes 6307840 | tf_op jit(solution)/shard_map/convert_element_type | solution.py:256
  197.3 5.8 %all-to-all-done.3 = bf16[32,128,128]{2,1,0:T(8,128)(2,1)S(1)} async-done(((bf16[32,128,128]{2,1,0:T(8,128)(2,1)}), bf16[32,128,128]{2,1,0:T(8,128)(2,1)S(1)}, u32[]{:S(2)}, u32[]{:S(2)}) %all-to-all-start.3) | async-done | bytes 1048608 | tf_op jit(solution)/shard_map/all_to_all | solution.py:114
  203.1 1.1 copy_bitcast_fusion
  (17 shorter events, 0.2 us)
Async XLA Ops:
  0.6 32.5 %copy-start = (bf16[256,4096]{1,0:T(8,128)(2,1)S(1)}, bf16[256,4096]{1,0:T(8,128)(2,1)}, u32[]{:S(2)}) copy-start(bf16[256,4096]{1,0:T(8,128)(2,1)} %param.19) | copy-start | bytes 6291460
  1.7 5.4 %collective-permute-start = (bf16[3,4096]{1,0:T(4,128)(2,1)S(1)}, bf16[3,4096]{1,0:T(4,128)(2,1)S(1)}, u32[]{:S(2)}, u32[]{:S(2)}) collective-permute-start(bf16[3,4096]{1,0:T(4,128)(2,1)S(1)} %slice.40), channel_id=1, source_target_pairs={{0,1},{1,2},{2,3},{3,4},{4,5},{5,6},{6,7},{7,8},{8,9},{9,10},{10,1... | collective-permute-start | bytes 73736 | tf_op jit(solution)/shard_map/ppermute | solution.py:19
  19.5 13.2 %copy-start.6 = (f32[128,16]{0,1:T(8,128)S(1)}, f32[128,16]{0,1:T(8,128)}, u32[]{:S(2)}) copy-start(f32[128,16]{0,1:T(8,128)} %param.22) | copy-start | bytes 24580
  19.5 13.4 %copy-start.7 = (f32[128,16]{0,1:T(8,128)S(1)}, f32[128,16]{0,1:T(8,128)}, u32[]{:S(2)}) copy-start(f32[128,16]{0,1:T(8,128)} %param.23) | copy-start | bytes 24580
  19.5 13.5 %copy-start.3 = (f32[16,4096]{1,0:T(8,128)S(1)}, f32[16,4096]{1,0:T(8,128)}, u32[]{:S(2)}) copy-start(f32[16,4096]{1,0:T(8,128)} %param.21) | copy-start | bytes 786436
  19.5 13.6 %copy-start.4 = (f32[4,4096]{1,0:T(4,128)S(1)}, f32[4,4096]{1,0:T(4,128)}, u32[]{:S(2)}) copy-start(f32[4,4096]{1,0:T(4,128)} %param.16) | copy-start | bytes 196612
  19.5 13.6 %copy-start.8 = (bf16[128,256]{1,0:T(8,128)(2,1)S(1)}, bf16[128,256]{1,0:T(8,128)(2,1)}, u32[]{:S(2)}) copy-start(bf16[128,256]{1,0:T(8,128)(2,1)} %param.18) | copy-start | bytes 196612
  19.5 13.6 %copy-start.9 = (f32[4096]{0:T(1024)S(1)}, f32[4096]{0:T(1024)}, u32[]{:S(2)}) copy-start(f32[4096]{0:T(1024)} %param.17) | copy-start | bytes 49156
  19.5 13.6 %copy-start.10 = (f32[4096]{0:T(1024)S(1)}, f32[4096]{0:T(1024)}, u32[]{:S(2)}) copy-start(f32[4096]{0:T(1024)} %param.20) | copy-start | bytes 49156
  19.5 86.6 %all-to-all-start = ((bf16[32,128,1,384]{3,1,2,0:T(8,128)(2,1)}), bf16[32,128,1,384]{3,1,2,0:T(8,128)(2,1)}, u32[]{:S(2)}, u32[]{:S(2)}) async-start(bf16[32,128,1,384]{3,1,2,0:T(8,128)(2,1)} %copy.47), calls=%async_computation | async-start | bytes 6291456 | tf_op jit(solution)/shard_map/all_to_all | solution.py:40
  33.0 7.2 %copy-start.1 = (f32[16,4096]{1,0:T(8,128)}, f32[16,4096]{1,0:T(8,128)S(1)}, u32[]{:S(2)}) copy-start(f32[16,4096]{1,0:T(8,128)S(1)} %exponential_negate_fusion.rate_ref) | copy-start | bytes 786436
  106.2 18.9 %all-to-all-start.1 = ((f32[17,32,128]{2,0,1:T(8,128)}), f32[17,32,128]{2,0,1:T(8,128)S(1)}, u32[]{:S(2)}, u32[]{:S(2)}) async-start(f32[17,32,128]{2,0,1:T(8,128)} %pad_maximum_fusion.2), calls=%async_computation.1 | async-start | bytes 786432 | tf_op jit(solution)/shard_map/all_to_all | solution.py:174
  128.5 35.7 %copy-start.2 = (bf16[1,2048,128]{2,1,0:T(8,128)(2,1)S(1)}, bf16[1,2048,128]{2,1,0:T(8,128)(2,1)}, u32[]{:S(2)}) copy-start(bf16[1,2048,128]{2,1,0:T(8,128)(2,1)} %shard_map.150) | copy-start | bytes 1572868
  128.5 37.7 %all-to-all-start.2 = ((f32[16,32,128]{2,0,1:T(8,128)}), f32[16,32,128]{2,0,1:T(8,128)S(1)}, u32[]{:S(2)}, u32[]{:S(2)}) async-start(f32[16,32,128]{2,0,1:T(8,128)} %bitcast.19), calls=%async_computation.2 | async-start | bytes 524288 | tf_op jit(solution)/shard_map/all_to_all | solution.py:201
  166.2 36.8 %all-to-all-start.3 = ((bf16[32,128,128]{2,1,0:T(8,128)(2,1)}), bf16[32,128,128]{2,1,0:T(8,128)(2,1)S(1)}, u32[]{:S(2)}, u32[]{:S(2)}) async-start(bf16[32,128,128]{2,1,0:T(8,128)(2,1)} %bitcast.20), calls=%async_computation.3 | async-start | bytes 2097152 | tf_op jit(solution)/shard_map/all_to_all | solution.py:114
  176.8 16.3 %copy-start.5 = (f32[4096]{0:T(1024)S(1)}, f32[4096]{0:T(1024)}, u32[]{:S(2)}) copy-start(f32[4096]{0:T(1024)} %param.24) | copy-start | bytes 49156

commit v8 on v7

--- a/solution.py
+++ b/solution.py
@@ -57,30 +57,28 @@
         )
         return product * scale
 
-    def peak_step(j, peak):
-        return jnp.maximum(peak, jnp.max(scores(j), axis=1, keepdims=True))
-
-    peak = jnp.full((tile, 1), -jnp.inf, jnp.float32)
-    peak = lax.fori_loop(0, index, peak_step, peak)
-    last = jnp.where(diagonal, scores(index), -1e30)
-    peak = jnp.maximum(peak, jnp.max(last, axis=1, keepdims=True))
-
-    def add_block(j, expo, carry):
-        total, summed = carry
+    def add_block(j, masked, carry):
+        peak, total, summed = carry
+        fresh = jnp.maximum(peak, jnp.max(masked, axis=1, keepdims=True))
+        shrink = jnp.exp(peak - fresh)
+        expo = jnp.exp(masked - fresh)
         values = v_ref[0, pl.ds(pl.multiple_of(j * tile, tile), tile), :]
-        summed = summed + lax.dot_general(
+        summed = shrink * summed + lax.dot_general(
             expo.astype(jnp.bfloat16), values, (((1,), (0,)), ((), ())),
             preferred_element_type=jnp.float32,
         )
-        return total + jnp.sum(expo, axis=1, keepdims=True), summed
+        return fresh, shrink * total + jnp.sum(expo, axis=1, keepdims=True), summed
 
     def sum_step(j, carry):
-        return add_block(j, jnp.exp(scores(j) - peak), carry)
-
-    carry = (jnp.zeros((tile, 1), jnp.float32), jnp.zeros((tile, HEAD_DIM), jnp.float32))
+        return add_block(j, scores(j), carry)
+
+    carry = (
+        jnp.full((tile, 1), -1e30, jnp.float32),
+        jnp.zeros((tile, 1), jnp.float32),
+        jnp.zeros((tile, HEAD_DIM), jnp.float32),
+    )
     carry = lax.fori_loop(0, index, sum_step, carry)
-    expo = jnp.where(diagonal, jnp.exp(last - peak), 0.0)
-    total, summed = add_block(index, expo, carry)
+    peak, total, summed = add_block(index, jnp.where(diagonal, scores(index), -jnp.inf), carry)
     o_ref[0] = (summed / total).astype(o_ref.dtype)
 
 

time: 205 us -> 199 us (0.971)
  Pallas kernels: 63.6 us -> 57 us
    pallas_call x2, Pallas kernels: 36.9 us -> 30.3 us  [attend_heads(): pl.pallas_call(functools.partial(attention_kernel, tile=tile, scale=HEAD_...]
  transfers between devices with their start and end apart: 5 -> 5, of which waited for: 3 -> 4; matrix products, arithmetic and copies ran while one was open for 11% -> 12% of each run, Pallas kernels for 31% -> 29%
where the time goes in v8:
time: 199 us; the launch traced here: 198 us
  waiting for transfers between devices  58.8 us (30%)
  Pallas kernels  57 us (29%)
  starting transfers between devices  39.9 us (20%)
  local copies, waits for them, and re-layouts  21.8 us (11%)
  other arithmetic  11.9 us (6%)
  matrix products  7.39 us (4%)
    all_to_all x1, waiting for transfers between devices, send_heads(): lax.all_to_all(jnp.transpose(joined, (1, 0, 2, 3)), 'seq', split_axis=0,...  50.4 us
    pallas_call x2, Pallas kernels, attend_heads(): pl.pallas_call(functools.partial(attention_kernel, tile=tile, scale=HEAD_...  30.3 us
    pallas_call x2, Pallas kernels, run_scan(): pl.pallas_call(functools.partial(scan_kernel, with_read=with_read), grid=...  26.7 us
    all_to_all x1, starting transfers between devices, send_heads(): lax.all_to_all(jnp.transpose(joined, (1, 0, 2, 3)), 'seq', split_axis=0,...  13.2 us
    all_to_all x1, starting transfers between devices, attend_by_heads(): lax.all_to_all(merged.reshape(count, tokens, -1), 'seq', split_axis=0, co...  9.78 us
    all_to_all x1, starting transfers between devices, exchange_return(): lax.all_to_all(jnp.transpose(incoming, (1, 0, 2)), 'seq', 1, 1, tiled=True)  8.99 us
    dot_general x1, matrix products, per_device(): jnp.dot(step_low, step_proj, preferred_element_type=jnp.float32)  7.04 us
    all_to_all x1, waiting for transfers between devices, attend_by_heads(): lax.all_to_all(merged.reshape(count, tokens, -1), 'seq', split_axis=0, co...  5.8 us
  transfers between devices with their start and end apart: 5, of which 4 were waited for; matrix products, arithmetic and copies ran while one was open for 12% of the time, Pallas kernels for 29%

profile of v8, /device:TPU:16, one launch (start us, length us, event | category | flops | bytes accessed | tf_op | source)
XLA Modules:
  0.0 197.6 jit_solution(2319568616620478889)
XLA Ops:
  0.6 0.0 copy-start
  0.6 1.0 slice.40
  1.7 3.8 %collective-permute-start = (bf16[3,4096]{1,0:T(4,128)(2,1)S(1)}, bf16[3,4096]{1,0:T(4,128)(2,1)S(1)}, u32[]{:S(2)}, u32[]{:S(2)}) collective-permute-start(bf16[3,4096]{1,0:T(4,128)(2,1)S(1)} %slice.40), channel_id=1, source_target_pairs={{0,1},{1,2},{2,3},{3,4},{4,5},{5,6},{6,7},{7,8},{8,9},{9,10},{10,1... | collective-permute-start | bytes 73736 | tf_op jit(solution)/shard_map/ppermute | solution.py:19
  5.5 1.6 collective-permute-done
  7.1 1.8 copy.51
  8.9 1.1 copy.52
  10.0 1.6 copy.44
  11.6 1.2 broadcast_in_dim.22
  12.8 0.2 broadcast_in_dim.23
  13.0 1.8 maximum_bitcast_fusion
  14.8 4.7 %copy.47 = bf16[32,128,1,384]{3,1,2,0:T(8,128)(2,1)} copy(bf16[32,128,1,384]{1,3,0,2:T(8,128)(2,1)} %maximum_bitcast_fusion) | data formatting | bytes 6291456 | tf_op jit(solution)/shard_map/transpose | solution.py:41
  19.5 0.0 copy-start.8
  19.5 0.0 copy-start.9
  19.5 0.0 copy-start.10
  19.5 13.2 %all-to-all-start = ((bf16[32,128,1,384]{3,1,2,0:T(8,128)(2,1)}), bf16[32,128,1,384]{3,1,2,0:T(8,128)(2,1)}, u32[]{:S(2)}, u32[]{:S(2)}) async-start(bf16[32,128,1,384]{3,1,2,0:T(8,128)(2,1)} %copy.47), calls=%async_computation | async-start | bytes 6291456 | tf_op jit(solution)/shard_map/all_to_all | solution.py:40
  32.7 0.0 copy-done.6
  32.7 0.1 copy.41
  32.8 0.0 copy-done.7
  32.9 0.1 copy.42
  33.0 0.0 copy-done.3
  33.0 0.0 copy-start.1
  33.1 0.0 copy-done.4
  33.2 7.0 %fusion.11 = (f32[128,4096]{1,0:T(8,128)}, f32[128,4096]{1,0:T(8,128)}, f32[4096]{0:T(1024)S(1)}, f32[128,4096]{1,0:T(8,128)}) fusion(f32[4096]{0:T(1024)S(1)} %copy-done.9, bf16[128,4096]{1,0:T(8,128)(2,1)} %param.14, f32[4096]{0:T(1024)S(1)} %bitcast.54, bf16[3,4096]{1,0:T(4,128)(2,1)S(1)} %collective-permute-done, f32[4096]{0:T(1024)S(1)} %bitcast.55, ...), kind=kOutput, calls=%fused_computation.35 | convolution fusion | flops 286257152 | bytes 9641984 | tf_op jit(solution)/shard_map/dot_general | solution.py:226
  40.2 0.0 copy-done.1
  40.2 1.3 broadcast_in_dim.18.in_ref
  41.5 1.3 broadcast_in_dim.19.out_ref
  42.8 0.7 broadcast_in_dim.21.init_ref
  43.6 10.4 %shard_map.149 = f32[16,4096]{1,0:T(8,128)} custom-call(f32[128,4096]{1,0:T(8,128)} %get-tuple-element.36.step_ref, f32[128,4096]{1,0:T(8,128)} %get-tuple-element.26.drive_ref, f32[16,4096]{1,0:T(8,128)} %copy-done.1, f32[128,16,128]{2,1,0:T(8,128)} %broadcast_in_dim.18.in_ref, f32[128,16,128]{2,1,0:T(8,128)} %broadcast_in_dim.19.out_ref, ...), custom_call_target="tpu_custom_call" | custom-call | tf_op jit(solution)/shard_map/pallas_call | solution.py:157
  54.0 1.0 copy_bitcast_fusion.2
  54.9 0.8 pad_maximum_fusion.2
  55.8 50.4 %all-to-all-done = bf16[32,128,1,384]{3,1,2,0:T(8,128)(2,1)} async-done(((bf16[32,128,1,384]{3,1,2,0:T(8,128)(2,1)}), bf16[32,128,1,384]{3,1,2,0:T(8,128)(2,1)}, u32[]{:S(2)}, u32[]{:S(2)}) %all-to-all-start) | async-done | bytes 3145760 | tf_op jit(solution)/shard_map/all_to_all | solution.py:40
  106.2 4.1 %all-to-all-start.1 = ((f32[17,32,128]{2,0,1:T(8,128)}), f32[17,32,128]{2,0,1:T(8,128)S(1)}, u32[]{:S(2)}, u32[]{:S(2)}) async-start(f32[17,32,128]{2,0,1:T(8,128)} %pad_maximum_fusion.2), calls=%async_computation.1 | async-start | bytes 786432 | tf_op jit(solution)/shard_map/all_to_all | solution.py:172
  110.3 3.6 %slice_bitcast_fusion = (bf16[1,4096,128]{2,1,0:T(8,128)(2,1)}, bf16[1,4096,128]{2,1,0:T(8,128)(2,1)}, bf16[1,4096,128]{2,1,0:T(8,128)(2,1)}) fusion(bf16[4096,1,384]{2,0,1:T(8,128)(2,1)} %bitcast.12), kind=kLoop, calls=%fused_computation.19 | loop fusion | bytes 6291456 | tf_op jit(solution)/shard_map/transpose | solution.py:104
  113.9 9.6 %shard_map.150 = bf16[1,2048,128]{2,1,0:T(8,128)(2,1)} custom-call(bf16[1,4096,128]{2,1,0:T(8,128)(2,1)} %get-tuple-element.23.q_ref, bf16[1,4096,128]{2,1,0:T(8,128)(2,1)} %get-tuple-element.24.k_ref, bf16[1,4096,128]{2,1,0:T(8,128)(2,1)} %get-tuple-element.25.v_ref), custom_call_target="tpu_custom_call" | custom-call | tf_op jit(solution)/shard_map/pallas_call | solution.py:91
  123.5 0.9 all-to-all-done.1
  124.4 0.1 copy.48
  124.5 0.3 fusion.7
  124.9 3.0 %multiply_reduce_fusion = f32[32,16,128]{2,1,0:T(8,128)} fusion(f32[32,16,128]{2,1,0:T(8,128)S(1)} %slice_bitcast_fusion.3, f32[32,32,128]{2,1,0:T(8,128)S(1)} %fusion.7, f32[16,128]{1,0:T(8,128)S(1)} %constant_dynamic-slice_fusion, pred[32,32]{1,0:T(8,128)(4,1)S(1)} %get-tuple-element.38), kind=kLoop, calls=%fused_computation | loop fusion | flops 8323072 | bytes 1057792 | tf_op jit(solution)/shard_map/reduce_sum | solution.py:194
  127.9 9.0 %all-to-all-start.2 = ((f32[16,32,128]{2,0,1:T(8,128)}), f32[16,32,128]{2,0,1:T(8,128)S(1)}, u32[]{:S(2)}, u32[]{:S(2)}) async-start(f32[16,32,128]{2,0,1:T(8,128)} %bitcast.19), calls=%async_computation.2 | async-start | bytes 524288 | tf_op jit(solution)/shard_map/all_to_all | solution.py:199
  136.9 20.7 %shard_map.152 = bf16[1,2048,128]{2,1,0:T(8,128)(2,1)} custom-call(bf16[1,4096,128]{2,1,0:T(8,128)(2,1)} %get-tuple-element.23.q_ref, bf16[1,4096,128]{2,1,0:T(8,128)(2,1)} %get-tuple-element.24.k_ref, bf16[1,4096,128]{2,1,0:T(8,128)(2,1)} %get-tuple-element.25.v_ref), custom_call_target="tpu_custom_call" | custom-call | tf_op jit(solution)/shard_map/pallas_call | solution.py:91
  157.6 2.1 %pad_maximum_fusion.1 = bf16[1,4096,128]{2,1,0:T(8,128)(2,1)} fusion(bf16[1,2048,128]{2,1,0:T(8,128)(2,1)} %shard_map.152, bf16[1,2048,128]{2,1,0:T(8,128)(2,1)S(1)} %copy-done.2), kind=kLoop, calls=%fused_computation.18 | loop fusion | flops 2097152 | bytes 2097152 | tf_op jit(solution)/shard_map/concatenate | solution.py:109
  159.6 0.0 all-to-all-done.2
  159.6 9.8 %all-to-all-start.3 = ((bf16[32,128,128]{2,1,0:T(8,128)(2,1)}), bf16[32,128,128]{2,1,0:T(8,128)(2,1)S(1)}, u32[]{:S(2)}, u32[]{:S(2)}) async-start(bf16[32,128,128]{2,1,0:T(8,128)(2,1)} %bitcast.20), calls=%async_computation.3 | async-start | bytes 2097152 | tf_op jit(solution)/shard_map/all_to_all | solution.py:112
  169.4 0.7 copy_bitcast_fusion.1.init_ref
  170.2 16.3 %shard_map.151 = f32[128,4096]{1,0:T(8,128)} custom-call(f32[128,4096]{1,0:T(8,128)} %get-tuple-element.36.step_ref, f32[128,4096]{1,0:T(8,128)} %get-tuple-element.26.drive_ref, f32[16,4096]{1,0:T(8,128)} %copy-done.1, f32[128,16,128]{2,1,0:T(8,128)} %broadcast_in_dim.18.in_ref, f32[128,16,128]{2,1,0:T(8,128)} %broadcast_in_dim.19.out_ref, ...), custom_call_target="tpu_custom_call" | custom-call | tf_op jit(solution)/shard_map/pallas_call | solution.py:157
  186.5 4.2 %fusion.4 = bf16[128,4096]{1,0:T(8,128)(2,1)} fusion(bf16[128,4096]{1,0:T(8,128)(2,1)} %param.15, f32[128,4096]{1,0:T(8,128)} %shard_map.151, f32[128,4096]{1,0:T(8,128)} %get-tuple-element.27, f32[4096]{0:T(1024)S(1)} %copy-done.5), kind=kLoop, calls=%fused_computation.11 | loop fusion | flops 4718592 | bytes 6307840 | tf_op jit(solution)/shard_map/convert_element_type | solution.py:254
  190.7 5.8 %all-to-all-done.3 = bf16[32,128,128]{2,1,0:T(8,128)(2,1)S(1)} async-done(((bf16[32,128,128]{2,1,0:T(8,128)(2,1)}), bf16[32,128,128]{2,1,0:T(8,128)(2,1)S(1)}, u32[]{:S(2)}, u32[]{:S(2)}) %all-to-all-start.3) | async-done | bytes 1048608 | tf_op jit(solution)/shard_map/all_to_all | solution.py:112
  196.5 1.1 copy_bitcast_fusion
  (17 shorter events, 0.2 us)
Async XLA Ops:
  0.6 32.5 %copy-start = (bf16[256,4096]{1,0:T(8,128)(2,1)S(1)}, bf16[256,4096]{1,0:T(8,128)(2,1)}, u32[]{:S(2)}) copy-start(bf16[256,4096]{1,0:T(8,128)(2,1)} %param.19) | copy-start | bytes 6291460
  1.7 5.4 %collective-permute-start = (bf16[3,4096]{1,0:T(4,128)(2,1)S(1)}, bf16[3,4096]{1,0:T(4,128)(2,1)S(1)}, u32[]{:S(2)}, u32[]{:S(2)}) collective-permute-start(bf16[3,4096]{1,0:T(4,128)(2,1)S(1)} %slice.40), channel_id=1, source_target_pairs={{0,1},{1,2},{2,3},{3,4},{4,5},{5,6},{6,7},{7,8},{8,9},{9,10},{10,1... | collective-permute-start | bytes 73736 | tf_op jit(solution)/shard_map/ppermute | solution.py:19
  19.5 13.2 %copy-start.6 = (f32[128,16]{0,1:T(8,128)S(1)}, f32[128,16]{0,1:T(8,128)}, u32[]{:S(2)}) copy-start(f32[128,16]{0,1:T(8,128)} %param.22) | copy-start | bytes 24580
  19.5 13.4 %copy-start.7 = (f32[128,16]{0,1:T(8,128)S(1)}, f32[128,16]{0,1:T(8,128)}, u32[]{:S(2)}) copy-start(f32[128,16]{0,1:T(8,128)} %param.23) | copy-start | bytes 24580
  19.5 13.5 %copy-start.3 = (f32[16,4096]{1,0:T(8,128)S(1)}, f32[16,4096]{1,0:T(8,128)}, u32[]{:S(2)}) copy-start(f32[16,4096]{1,0:T(8,128)} %param.21) | copy-start | bytes 786436
  19.5 13.6 %copy-start.4 = (f32[4,4096]{1,0:T(4,128)S(1)}, f32[4,4096]{1,0:T(4,128)}, u32[]{:S(2)}) copy-start(f32[4,4096]{1,0:T(4,128)} %param.16) | copy-start | bytes 196612
  19.5 13.6 %copy-start.8 = (bf16[128,256]{1,0:T(8,128)(2,1)S(1)}, bf16[128,256]{1,0:T(8,128)(2,1)}, u32[]{:S(2)}) copy-start(bf16[128,256]{1,0:T(8,128)(2,1)} %param.18) | copy-start | bytes 196612
  19.5 13.6 %copy-start.9 = (f32[4096]{0:T(1024)S(1)}, f32[4096]{0:T(1024)}, u32[]{:S(2)}) copy-start(f32[4096]{0:T(1024)} %param.17) | copy-start | bytes 49156
  19.5 13.6 %copy-start.10 = (f32[4096]{0:T(1024)S(1)}, f32[4096]{0:T(1024)}, u32[]{:S(2)}) copy-start(f32[4096]{0:T(1024)} %param.20) | copy-start | bytes 49156
  19.5 86.6 %all-to-all-start = ((bf16[32,128,1,384]{3,1,2,0:T(8,128)(2,1)}), bf16[32,128,1,384]{3,1,2,0:T(8,128)(2,1)}, u32[]{:S(2)}, u32[]{:S(2)}) async-start(bf16[32,128,1,384]{3,1,2,0:T(8,128)(2,1)} %copy.47), calls=%async_computation | async-start | bytes 6291456 | tf_op jit(solution)/shard_map/all_to_all | solution.py:40
  33.0 7.2 %copy-start.1 = (f32[16,4096]{1,0:T(8,128)}, f32[16,4096]{1,0:T(8,128)S(1)}, u32[]{:S(2)}) copy-start(f32[16,4096]{1,0:T(8,128)S(1)} %exponential_negate_fusion.rate_ref) | copy-start | bytes 786436
  106.2 18.2 %all-to-all-start.1 = ((f32[17,32,128]{2,0,1:T(8,128)}), f32[17,32,128]{2,0,1:T(8,128)S(1)}, u32[]{:S(2)}, u32[]{:S(2)}) async-start(f32[17,32,128]{2,0,1:T(8,128)} %pad_maximum_fusion.2), calls=%async_computation.1 | async-start | bytes 786432 | tf_op jit(solution)/shard_map/all_to_all | solution.py:172
  127.9 29.7 %copy-start.2 = (bf16[1,2048,128]{2,1,0:T(8,128)(2,1)S(1)}, bf16[1,2048,128]{2,1,0:T(8,128)(2,1)}, u32[]{:S(2)}) copy-start(bf16[1,2048,128]{2,1,0:T(8,128)(2,1)} %shard_map.150) | copy-start | bytes 1572868
  127.9 31.8 %all-to-all-start.2 = ((f32[16,32,128]{2,0,1:T(8,128)}), f32[16,32,128]{2,0,1:T(8,128)S(1)}, u32[]{:S(2)}, u32[]{:S(2)}) async-start(f32[16,32,128]{2,0,1:T(8,128)} %bitcast.19), calls=%async_computation.2 | async-start | bytes 524288 | tf_op jit(solution)/shard_map/all_to_all | solution.py:199
  159.6 36.8 %all-to-all-start.3 = ((bf16[32,128,128]{2,1,0:T(8,128)(2,1)}), bf16[32,128,128]{2,1,0:T(8,128)(2,1)S(1)}, u32[]{:S(2)}, u32[]{:S(2)}) async-start(bf16[32,128,128]{2,1,0:T(8,128)(2,1)} %bitcast.20), calls=%async_computation.3 | async-start | bytes 2097152 | tf_op jit(solution)/shard_map/all_to_all | solution.py:112
  170.2 16.3 %copy-start.5 = (f32[4096]{0:T(1024)S(1)}, f32[4096]{0:T(1024)}, u32[]{:S(2)}) copy-start(f32[4096]{0:T(1024)} %param.24) | copy-start | bytes 49156

commit v9 on v8

--- a/solution.py
+++ b/solution.py
@@ -30,17 +30,32 @@
     return jax.nn.silu(total + conv_bias[None, :])
 
 
-def send_heads(q_three, k_three, v_three):
-    tokens, heads = q_three.shape[:2]
+def pack_kernel(q_ref, k_ref, v_ref, o_ref):
+    for i in range(o_ref.shape[1]):
+        head = pl.ds(i * HEAD_DIM, HEAD_DIM)
+        o_ref[0, i, :, pl.ds(0, HEAD_DIM)] = q_ref[:, head]
+        o_ref[0, i, :, pl.ds(HEAD_DIM, HEAD_DIM)] = k_ref[...]
+        o_ref[0, i, :, pl.ds(2 * HEAD_DIM, HEAD_DIM)] = v_ref[...]
+
+
+def send_heads(query_heads, key_heads, value_heads):
+    tokens = query_heads.shape[0]
+    heads = query_heads.shape[1] // HEAD_DIM
     count = lax.axis_size("seq")
-    group = heads // k_three.shape[1]
-    k_wide = jnp.repeat(k_three, group, axis=1)
-    v_wide = jnp.repeat(v_three, group, axis=1)
-    joined = jnp.concatenate([q_three, k_wide, v_wide], 2).reshape(tokens, count, heads // count, -1)
-    arrived = lax.all_to_all(
-        jnp.transpose(joined, (1, 0, 2, 3)), "seq", split_axis=0, concat_axis=0, tiled=True
-    )
-    return arrived.reshape(count * tokens, heads // count, -1)
+    local = heads // count
+    group = heads // (key_heads.shape[1] // HEAD_DIM)
+    assert group % local == 0
+    kv_spec = pl.BlockSpec((tokens, HEAD_DIM), lambda j: (0, j * local // group))
+    joined = pl.pallas_call(
+        pack_kernel,
+        grid=(count,),
+        in_specs=[pl.BlockSpec((tokens, local * HEAD_DIM), lambda j: (0, j)), kv_spec, kv_spec],
+        out_specs=pl.BlockSpec((1, local, tokens, 3 * HEAD_DIM), lambda j: (j, 0, 0, 0)),
+        out_shape=jax.ShapeDtypeStruct((count, local, tokens, 3 * HEAD_DIM), query_heads.dtype),
+        interpret=INTERPRET,
+    )(query_heads, key_heads, value_heads)
+    arrived = lax.all_to_all(joined, "seq", split_axis=0, concat_axis=0, tiled=True)
+    return jnp.transpose(arrived, (1, 0, 2, 3)).reshape(local, count * tokens, -1)
 
 
 def attention_kernel(q_ref, k_ref, v_ref, o_ref, *, tile, scale, first):
@@ -82,32 +97,29 @@
     o_ref[0] = (summed / total).astype(o_ref.dtype)
 
 
-def attend_heads(q_all, k_all, v_all, first, blocks):
-    heads, length, _ = q_all.shape
+def attend_heads(joined, first, blocks):
+    heads, length, _ = joined.shape
     tile = length // blocks
-    head_spec = pl.BlockSpec((1, length, HEAD_DIM), lambda h, i: (h, 0, 0))
+    key_spec = pl.BlockSpec((1, length, HEAD_DIM), lambda h, i: (h, 0, 1))
+    value_spec = pl.BlockSpec((1, length, HEAD_DIM), lambda h, i: (h, 0, 2))
     tile_spec = pl.BlockSpec((1, tile, HEAD_DIM), lambda h, i: (h, i + first, 0))
     out_spec = pl.BlockSpec((1, tile, HEAD_DIM), lambda h, i: (h, i, 0))
     return pl.pallas_call(
         functools.partial(attention_kernel, tile=tile, scale=HEAD_DIM ** (-0.5), first=first),
         grid=(heads, blocks // 2),
-        in_specs=[tile_spec, head_spec, head_spec],
+        in_specs=[tile_spec, key_spec, value_spec],
         out_specs=out_spec,
         out_shape=jax.ShapeDtypeStruct((heads, length // 2, HEAD_DIM), jnp.bfloat16),
         interpret=INTERPRET,
-    )(q_all, k_all, v_all)
+    )(joined, joined, joined)
 
 
 def attend_by_heads(joined, tokens, midway):
-    length = joined.shape[0]
+    length = joined.shape[1]
     blocks = length // math.gcd(length, 512)
-    heads_first = [jnp.transpose(x, (1, 0, 2)) for x in (
-        joined[:, :, :HEAD_DIM], joined[:, :, HEAD_DIM : 2 * HEAD_DIM], joined[:, :, 2 * HEAD_DIM :]
-    )]
-    early, heads_first = midway(attend_heads(*heads_first, 0, blocks), heads_first)
-    late = attend_heads(*heads_first, blocks // 2, blocks)
+    early, joined = midway(attend_heads(joined, 0, blocks), joined)
+    late = attend_heads(joined, blocks // 2, blocks)
     merged = jnp.transpose(jnp.concatenate([early, late], 1), (1, 0, 2))
-    length = merged.shape[0]
     count = length // tokens
     back = lax.all_to_all(
         merged.reshape(count, tokens, -1), "seq", split_axis=0, concat_axis=0, tiled=True
@@ -233,11 +245,7 @@
     zero_state = jnp.zeros(rate.shape, jnp.float32)
     local_end = run_scan(step, drive, rate, in_wide, out_wide, zero_state, False)
     tokens = query_heads.shape[0]
-    joined = send_heads(
-        query_heads.reshape(tokens, -1, HEAD_DIM),
-        key_heads.reshape(tokens, -1, HEAD_DIM),
-        value_heads.reshape(tokens, -1, HEAD_DIM),
-    )
+    joined = send_heads(query_heads, key_heads, value_heads)
     gathered, joined = exchange_send(jnp.sum(step, axis=0), local_end, joined)
     prefix = []
 

time: 199 us -> 201 us (1.010)
  Pallas kernels: 57 us -> 73 us
  local copies, waits for them, and re-layouts: 21.8 us -> 8.26 us
  starting transfers between devices: 39.9 us -> 36.9 us
  waiting for transfers between devices: 58.8 us -> 61 us
    pallas_call x0 -> x1, Pallas kernels: none -> 16 us  [send_heads(): pl.pallas_call(pack_kernel, grid=(count,), in_specs=[pl.BlockSpec((tokens...]
    transpose x2 -> x0, local copies, waits for them, and re-layouts: 8.27 us -> none  [the longest x1 4.67 us: send_heads(): jnp.transpose(joined, (1, 0, 2, 3))]
    all_to_all x1, starting transfers between devices: 8.99 us -> 5.99 us  [exchange_return(): lax.all_to_all(jnp.transpose(incoming, (1, 0, 2)), 'seq', 1, 1, tiled=True)]
    reshape x2 -> x0, local copies, waits for them, and re-layouts: 2.91 us -> none  [the longest x1 1.79 us: per_device(): key_heads.reshape(tokens, -1, HEAD_DIM)]
    all_to_all x1, waiting for transfers between devices: 0.94 us -> 3.8 us  [exchange_send(): return (lax.all_to_all(packed, 'seq', 1, 1, tiled=True), joined)]
  transfers between devices with their start and end apart: 5 -> 5, of which waited for: 4 -> 4; matrix products, arithmetic and copies ran while one was open for 12% -> 11% of each run, Pallas kernels for 29% -> 29%
where the time goes in v9:
time: 201 us; the launch traced here: 198 us
  Pallas kernels  73 us (36%)
  waiting for transfers between devices  61 us (30%)
  starting transfers between devices  36.9 us (18%)
  other arithmetic  10.8 us (5%)
  local copies, waits for them, and re-layouts  8.26 us (4%)
  matrix products  7.42 us (4%)
    all_to_all x1, waiting for transfers between devices, send_heads(): lax.all_to_all(joined, 'seq', split_axis=0, concat_axis=0, tiled=True)  49.8 us
    pallas_call x2, Pallas kernels, attend_heads(): pl.pallas_call(functools.partial(attention_kernel, tile=tile, scale=HEAD_...  30.3 us
    pallas_call x2, Pallas kernels, run_scan(): pl.pallas_call(functools.partial(scan_kernel, with_read=with_read), grid=...  26.7 us
    pallas_call x1, Pallas kernels, send_heads(): pl.pallas_call(pack_kernel, grid=(count,), in_specs=[pl.BlockSpec((tokens...  16 us
    all_to_all x1, starting transfers between devices, send_heads(): lax.all_to_all(joined, 'seq', split_axis=0, concat_axis=0, tiled=True)  13.2 us
    all_to_all x1, starting transfers between devices, attend_by_heads(): lax.all_to_all(merged.reshape(count, tokens, -1), 'seq', split_axis=0, co...  9.79 us
    dot_general x1, matrix products, per_device(): jnp.dot(step_low, step_proj, preferred_element_type=jnp.float32)  7.07 us
    all_to_all x1, starting transfers between devices, exchange_return(): lax.all_to_all(jnp.transpose(incoming, (1, 0, 2)), 'seq', 1, 1, tiled=True)  5.99 us
  transfers between devices with their start and end apart: 5, of which 4 were waited for; matrix products, arithmetic and copies ran while one was open for 11% of the time, Pallas kernels for 29%

profile of v9, /device:TPU:16, one launch (start us, length us, event | category | flops | bytes accessed | tf_op | source)
XLA Modules:
  0.0 198.3 jit_solution(17726741649039388624)
XLA Ops:
  0.6 0.0 copy-start
  0.6 1.0 slice.31
  1.7 3.8 %collective-permute-start = (bf16[3,4096]{1,0:T(4,128)(2,1)S(1)}, bf16[3,4096]{1,0:T(4,128)(2,1)S(1)}, u32[]{:S(2)}, u32[]{:S(2)}) collective-permute-start(bf16[3,4096]{1,0:T(4,128)(2,1)S(1)} %slice.31), channel_id=1, source_target_pairs={{0,1},{1,2},{2,3},{3,4},{4,5},{5,6},{6,7},{7,8},{8,9},{9,10},{10,1... | collective-permute-start | bytes 73736 | tf_op jit(solution)/shard_map/ppermute | solution.py:19
  5.5 1.6 collective-permute-done
  7.1 16.0 %shard_map.150 = bf16[32,1,128,384]{3,2,1,0:T(8,128)(2,1)} custom-call(bf16[128,4096]{1,0:T(8,128)(2,1)} %q_ref, bf16[128,1024]{1,0:T(8,128)(2,1)} %k_ref, bf16[128,1024]{1,0:T(8,128)(2,1)} %v_ref), custom_call_target="tpu_custom_call" | custom-call | tf_op jit(solution)/shard_map/pallas_call | solution.py:49
  23.1 0.0 copy-start.2
  23.1 0.0 copy-start.7
  23.1 0.0 copy-start.8
  23.1 0.0 copy-start.9
  23.1 13.2 %all-to-all-start = ((bf16[32,1,128,384]{3,2,1,0:T(8,128)(2,1)}), bf16[32,1,128,384]{3,2,1,0:T(8,128)(2,1)}, u32[]{:S(2)}, u32[]{:S(2)}) async-start(bf16[32,1,128,384]{3,2,1,0:T(8,128)(2,1)} %shard_map.150), calls=%async_computation | async-start | bytes 6291456 | tf_op jit(solution)/shard_map/all_to_all | solution.py:57
  36.3 0.0 copy-done.5
  36.3 0.1 copy.26
  36.4 0.0 copy-done.6
  36.4 0.1 copy.27
  36.5 0.0 copy-done.3
  36.6 0.0 copy-done.2
  36.6 0.7 exponential_negate_fusion.rate_ref
  37.4 0.0 copy-done
  37.4 0.0 copy-done.7
  37.4 0.0 copy-done.8
  37.4 0.0 copy-done.9
  37.4 7.1 %fusion.11 = (f32[128,4096]{1,0:T(8,128)}, f32[128,4096]{1,0:T(8,128)}, f32[4096]{0:T(1024)S(1)}, f32[128,4096]{1,0:T(8,128)}) fusion(f32[4096]{0:T(1024)S(1)} %copy-done.8, bf16[128,4096]{1,0:T(8,128)(2,1)} %param.14, f32[4096]{0:T(1024)S(1)} %bitcast.34, bf16[3,4096]{1,0:T(4,128)(2,1)S(1)} %collective-permute-done, f32[4096]{0:T(1024)S(1)} %bitcast.35, ...), kind=kOutput, calls=%fused_computation.31 | convolution fusion | flops 286257152 | bytes 9641984 | tf_op jit(solution)/shard_map/dot_general | solution.py:238
  44.4 1.3 broadcast_in_dim.15.out_ref
  45.7 1.3 broadcast_in_dim.14.in_ref
  47.1 0.7 broadcast_in_dim.17.init_ref
  47.8 10.4 %shard_map.149 = f32[16,4096]{1,0:T(8,128)} custom-call(f32[128,4096]{1,0:T(8,128)} %get-tuple-element.29.step_ref, f32[128,4096]{1,0:T(8,128)} %get-tuple-element.22.drive_ref, f32[16,4096]{1,0:T(8,128)} %exponential_negate_fusion.rate_ref, f32[128,16,128]{2,1,0:T(8,128)} %broadcast_in_dim.14.in_ref, f32[128,16,128]{2,1,0:T(8,128)} %broadcast_in_dim.15.out_ref, ...), custom_call_target="tpu_custom_call" | custom-call | tf_op jit(solution)/shard_map/pallas_call | solution.py:169
  58.2 1.0 copy_bitcast_fusion.2
  59.1 0.8 pad_maximum_fusion.2
  60.0 49.8 %all-to-all-done = bf16[32,1,128,384]{3,2,1,0:T(8,128)(2,1)} async-done(((bf16[32,1,128,384]{3,2,1,0:T(8,128)(2,1)}), bf16[32,1,128,384]{3,2,1,0:T(8,128)(2,1)}, u32[]{:S(2)}, u32[]{:S(2)}) %all-to-all-start) | async-done | bytes 3145760 | tf_op jit(solution)/shard_map/all_to_all | solution.py:57
  109.8 4.1 %all-to-all-start.1 = ((f32[17,32,128]{2,0,1:T(8,128)}), f32[17,32,128]{2,0,1:T(8,128)S(1)}, u32[]{:S(2)}, u32[]{:S(2)}) async-start(f32[17,32,128]{2,0,1:T(8,128)} %pad_maximum_fusion.2), calls=%async_computation.1 | async-start | bytes 786432 | tf_op jit(solution)/shard_map/all_to_all | solution.py:184
  113.9 0.7 constant_dynamic-slice_fusion
  114.6 9.6 %shard_map.151 = bf16[1,2048,128]{2,1,0:T(8,128)(2,1)} custom-call(bf16[1,4096,384]{2,1,0:T(8,128)(2,1)} %bitcast.5.q_ref.k_ref.v_ref, bf16[1,4096,384]{2,1,0:T(8,128)(2,1)} %bitcast.5.q_ref.k_ref.v_ref, bf16[1,4096,384]{2,1,0:T(8,128)(2,1)} %bitcast.5.q_ref.k_ref.v_ref), custom_call_target="tpu_custom_call" | custom-call | tf_op jit(solution)/shard_map/pallas_call | solution.py:107
  124.2 3.8 %all-to-all-done.1 = f32[17,32,128]{2,0,1:T(8,128)S(1)} async-done(((f32[17,32,128]{2,0,1:T(8,128)}), f32[17,32,128]{2,0,1:T(8,128)S(1)}, u32[]{:S(2)}, u32[]{:S(2)}) %all-to-all-start.1) | async-done | bytes 278560 | tf_op jit(solution)/shard_map/all_to_all | solution.py:184
  128.0 0.1 copy.29
  128.1 0.3 fusion.7
  128.5 3.0 %multiply_reduce_fusion = f32[32,16,128]{2,1,0:T(8,128)} fusion(f32[32,16,128]{2,1,0:T(8,128)S(1)} %slice_bitcast_fusion, f32[32,32,128]{2,1,0:T(8,128)S(1)} %fusion.7, f32[16,128]{1,0:T(8,128)S(1)} %constant_dynamic-slice_fusion, pred[32,32]{1,0:T(8,128)(4,1)S(1)} %get-tuple-element.31), kind=kLoop, calls=%fused_computation | loop fusion | flops 8323072 | bytes 1057792 | tf_op jit(solution)/shard_map/reduce_sum | solution.py:206
  131.5 6.0 %all-to-all-start.2 = ((f32[16,32,128]{2,0,1:T(8,128)}), f32[16,32,128]{2,0,1:T(8,128)S(1)}, u32[]{:S(2)}, u32[]{:S(2)}) async-start(f32[16,32,128]{2,0,1:T(8,128)} %bitcast.9), calls=%async_computation.2 | async-start | bytes 524288 | tf_op jit(solution)/shard_map/all_to_all | solution.py:211
  137.5 0.0 copy-start.1
  137.5 20.8 %shard_map.153 = bf16[1,2048,128]{2,1,0:T(8,128)(2,1)} custom-call(bf16[1,4096,384]{2,1,0:T(8,128)(2,1)} %bitcast.5.q_ref.k_ref.v_ref, bf16[1,4096,384]{2,1,0:T(8,128)(2,1)} %bitcast.5.q_ref.k_ref.v_ref, bf16[1,4096,384]{2,1,0:T(8,128)(2,1)} %bitcast.5.q_ref.k_ref.v_ref), custom_call_target="tpu_custom_call" | custom-call | tf_op jit(solution)/shard_map/pallas_call | solution.py:107
  158.2 2.1 %pad_maximum_fusion.1 = bf16[1,4096,128]{2,1,0:T(8,128)(2,1)} fusion(bf16[1,2048,128]{2,1,0:T(8,128)(2,1)} %shard_map.153, bf16[1,2048,128]{2,1,0:T(8,128)(2,1)S(1)} %copy-done.1), kind=kLoop, calls=%fused_computation.17 | loop fusion | flops 2097152 | bytes 2097152 | tf_op jit(solution)/shard_map/concatenate | solution.py:122
  160.3 0.0 all-to-all-done.2
  160.3 9.8 %all-to-all-start.3 = ((bf16[32,128,128]{2,1,0:T(8,128)(2,1)}), bf16[32,128,128]{2,1,0:T(8,128)(2,1)S(1)}, u32[]{:S(2)}, u32[]{:S(2)}) async-start(bf16[32,128,128]{2,1,0:T(8,128)(2,1)} %bitcast.10), calls=%async_computation.3 | async-start | bytes 2097152 | tf_op jit(solution)/shard_map/all_to_all | solution.py:124
  170.1 0.7 copy_bitcast_fusion.1.init_ref
  170.8 16.3 %shard_map.152 = f32[128,4096]{1,0:T(8,128)} custom-call(f32[128,4096]{1,0:T(8,128)} %get-tuple-element.29.step_ref, f32[128,4096]{1,0:T(8,128)} %get-tuple-element.22.drive_ref, f32[16,4096]{1,0:T(8,128)} %exponential_negate_fusion.rate_ref, f32[128,16,128]{2,1,0:T(8,128)} %broadcast_in_dim.14.in_ref, f32[128,16,128]{2,1,0:T(8,128)} %broadcast_in_dim.15.out_ref, ...), custom_call_target="tpu_custom_call" | custom-call | tf_op jit(solution)/shard_map/pallas_call | solution.py:169
  187.2 0.0 copy-done.4
  187.2 4.2 %fusion.4 = bf16[128,4096]{1,0:T(8,128)(2,1)} fusion(bf16[128,4096]{1,0:T(8,128)(2,1)} %param.15, f32[128,4096]{1,0:T(8,128)} %shard_map.152, f32[128,4096]{1,0:T(8,128)} %get-tuple-element.23, f32[4096]{0:T(1024)S(1)} %copy-done.4), kind=kLoop, calls=%fused_computation.10 | loop fusion | flops 4718592 | bytes 6307840 | tf_op jit(solution)/shard_map/convert_element_type | solution.py:262
  191.4 5.8 %all-to-all-done.3 = bf16[32,128,128]{2,1,0:T(8,128)(2,1)S(1)} async-done(((bf16[32,128,128]{2,1,0:T(8,128)(2,1)}), bf16[32,128,128]{2,1,0:T(8,128)(2,1)S(1)}, u32[]{:S(2)}, u32[]{:S(2)}) %all-to-all-start.3) | async-done | bytes 1048608 | tf_op jit(solution)/shard_map/all_to_all | solution.py:124
  197.2 1.1 copy_bitcast_fusion
  (8 shorter events, 0.1 us)
Async XLA Ops:
  0.6 36.7 %copy-start = (bf16[256,4096]{1,0:T(8,128)(2,1)S(1)}, bf16[256,4096]{1,0:T(8,128)(2,1)}, u32[]{:S(2)}) copy-start(bf16[256,4096]{1,0:T(8,128)(2,1)} %param.19) | copy-start | bytes 6291460
  1.7 5.4 %collective-permute-start = (bf16[3,4096]{1,0:T(4,128)(2,1)S(1)}, bf16[3,4096]{1,0:T(4,128)(2,1)S(1)}, u32[]{:S(2)}, u32[]{:S(2)}) collective-permute-start(bf16[3,4096]{1,0:T(4,128)(2,1)S(1)} %slice.31), channel_id=1, source_target_pairs={{0,1},{1,2},{2,3},{3,4},{4,5},{5,6},{6,7},{7,8},{8,9},{9,10},{10,1... | collective-permute-start | bytes 73736 | tf_op jit(solution)/shard_map/ppermute | solution.py:19
  23.1 13.2 %copy-start.5 = (f32[128,16]{0,1:T(8,128)S(1)}, f32[128,16]{0,1:T(8,128)}, u32[]{:S(2)}) copy-start(f32[128,16]{0,1:T(8,128)} %param.22) | copy-start | bytes 24580
  23.1 13.4 %copy-start.6 = (f32[128,16]{0,1:T(8,128)S(1)}, f32[128,16]{0,1:T(8,128)}, u32[]{:S(2)}) copy-start(f32[128,16]{0,1:T(8,128)} %param.23) | copy-start | bytes 24580
  23.1 13.5 %copy-start.3 = (f32[4,4096]{1,0:T(4,128)S(1)}, f32[4,4096]{1,0:T(4,128)}, u32[]{:S(2)}) copy-start(f32[4,4096]{1,0:T(4,128)} %param.16) | copy-start | bytes 196612
  23.1 13.5 %copy-start.2 = (f32[16,4096]{1,0:T(8,128)S(1)}, f32[16,4096]{1,0:T(8,128)}, u32[]{:S(2)}) copy-start(f32[16,4096]{1,0:T(8,128)} %param.21) | copy-start | bytes 786436
  23.1 14.3 %copy-start.7 = (bf16[128,256]{1,0:T(8,128)(2,1)S(1)}, bf16[128,256]{1,0:T(8,128)(2,1)}, u32[]{:S(2)}) copy-start(bf16[128,256]{1,0:T(8,128)(2,1)} %param.18) | copy-start | bytes 196612
  23.1 14.3 %copy-start.8 = (f32[4096]{0:T(1024)S(1)}, f32[4096]{0:T(1024)}, u32[]{:S(2)}) copy-start(f32[4096]{0:T(1024)} %param.17) | copy-start | bytes 49156
  23.1 14.2 %copy-start.9 = (f32[4096]{0:T(1024)S(1)}, f32[4096]{0:T(1024)}, u32[]{:S(2)}) copy-start(f32[4096]{0:T(1024)} %param.20) | copy-start | bytes 49156
  23.1 86.6 %all-to-all-start = ((bf16[32,1,128,384]{3,2,1,0:T(8,128)(2,1)}), bf16[32,1,128,384]{3,2,1,0:T(8,128)(2,1)}, u32[]{:S(2)}, u32[]{:S(2)}) async-start(bf16[32,1,128,384]{3,2,1,0:T(8,128)(2,1)} %shard_map.150), calls=%async_computation | async-start | bytes 6291456 | tf_op jit(solution)/shard_map/all_to_all | solution.py:57
  109.8 18.2 %all-to-all-start.1 = ((f32[17,32,128]{2,0,1:T(8,128)}), f32[17,32,128]{2,0,1:T(8,128)S(1)}, u32[]{:S(2)}, u32[]{:S(2)}) async-start(f32[17,32,128]{2,0,1:T(8,128)} %pad_maximum_fusion.2), calls=%async_computation.1 | async-start | bytes 786432 | tf_op jit(solution)/shard_map/all_to_all | solution.py:184
  131.5 28.8 %all-to-all-start.2 = ((f32[16,32,128]{2,0,1:T(8,128)}), f32[16,32,128]{2,0,1:T(8,128)S(1)}, u32[]{:S(2)}, u32[]{:S(2)}) async-start(f32[16,32,128]{2,0,1:T(8,128)} %bitcast.9), calls=%async_computation.2 | async-start | bytes 524288 | tf_op jit(solution)/shard_map/all_to_all | solution.py:211
  137.5 20.8 %copy-start.1 = (bf16[1,2048,128]{2,1,0:T(8,128)(2,1)S(1)}, bf16[1,2048,128]{2,1,0:T(8,128)(2,1)}, u32[]{:S(2)}) copy-start(bf16[1,2048,128]{2,1,0:T(8,128)(2,1)} %shard_map.151) | copy-start | bytes 1572868
  160.3 36.8 %all-to-all-start.3 = ((bf16[32,128,128]{2,1,0:T(8,128)(2,1)}), bf16[32,128,128]{2,1,0:T(8,128)(2,1)S(1)}, u32[]{:S(2)}, u32[]{:S(2)}) async-start(bf16[32,128,128]{2,1,0:T(8,128)(2,1)} %bitcast.10), calls=%async_computation.3 | async-start | bytes 2097152 | tf_op jit(solution)/shard_map/all_to_all | solution.py:124
  170.8 16.3 %copy-start.4 = (f32[4096]{0:T(1024)S(1)}, f32[4096]{0:T(1024)}, u32[]{:S(2)}) copy-start(f32[4096]{0:T(1024)} %param.24) | copy-start | bytes 49156

commit v10 on v9

--- a/solution.py
+++ b/solution.py
@@ -30,12 +30,15 @@
     return jax.nn.silu(total + conv_bias[None, :])
 
 
-def pack_kernel(q_ref, k_ref, v_ref, o_ref):
-    for i in range(o_ref.shape[1]):
-        head = pl.ds(i * HEAD_DIM, HEAD_DIM)
-        o_ref[0, i, :, pl.ds(0, HEAD_DIM)] = q_ref[:, head]
-        o_ref[0, i, :, pl.ds(HEAD_DIM, HEAD_DIM)] = k_ref[...]
-        o_ref[0, i, :, pl.ds(2 * HEAD_DIM, HEAD_DIM)] = v_ref[...]
+def pack_kernel(q_ref, k_ref, v_ref, o_ref, *, group):
+    count, local = o_ref.shape[:2]
+    for j in range(count):
+        for i in range(local):
+            head = j * local + i
+            kv = pl.ds(head // group * HEAD_DIM, HEAD_DIM)
+            o_ref[j, i, :, pl.ds(0, HEAD_DIM)] = q_ref[:, pl.ds(head * HEAD_DIM, HEAD_DIM)]
+            o_ref[j, i, :, pl.ds(HEAD_DIM, HEAD_DIM)] = k_ref[:, kv]
+            o_ref[j, i, :, pl.ds(2 * HEAD_DIM, HEAD_DIM)] = v_ref[:, kv]
 
 
 def send_heads(query_heads, key_heads, value_heads):
@@ -44,13 +47,8 @@
     count = lax.axis_size("seq")
     local = heads // count
     group = heads // (key_heads.shape[1] // HEAD_DIM)
-    assert group % local == 0
-    kv_spec = pl.BlockSpec((tokens, HEAD_DIM), lambda j: (0, j * local // group))
     joined = pl.pallas_call(
-        pack_kernel,
-        grid=(count,),
-        in_specs=[pl.BlockSpec((tokens, local * HEAD_DIM), lambda j: (0, j)), kv_spec, kv_spec],
-        out_specs=pl.BlockSpec((1, local, tokens, 3 * HEAD_DIM), lambda j: (j, 0, 0, 0)),
+        functools.partial(pack_kernel, group=group),
         out_shape=jax.ShapeDtypeStruct((count, local, tokens, 3 * HEAD_DIM), query_heads.dtype),
         interpret=INTERPRET,
     )(query_heads, key_heads, value_heads)

time: 201 us -> 187 us (0.930)
  Pallas kernels: 73 us -> 60.5 us
    pallas_call x1, Pallas kernels: 16 us -> 3.44 us  [send_heads(): pl.pallas_call(functools.partial(pack_kernel, group=group), out_shape=jax...]
  transfers between devices with their start and end apart: 5 -> 5, of which waited for: 4 -> 4; matrix products, arithmetic and copies ran while one was open for 11% -> 11% of each run, Pallas kernels for 29% -> 31%
where the time goes in v10:
time: 187 us; the launch traced here: 186 us
  waiting for transfers between devices  61 us (33%)
  Pallas kernels  60.5 us (32%)
  starting transfers between devices  36.9 us (20%)
  other arithmetic  10.8 us (6%)
  local copies, waits for them, and re-layouts  8.26 us (4%)
  matrix products  7.42 us (4%)
    all_to_all x1, waiting for transfers between devices, send_heads(): lax.all_to_all(joined, 'seq', split_axis=0, concat_axis=0, tiled=True)  49.8 us
    pallas_call x2, Pallas kernels, attend_heads(): pl.pallas_call(functools.partial(attention_kernel, tile=tile, scale=HEAD_...  30.3 us
    pallas_call x2, Pallas kernels, run_scan(): pl.pallas_call(functools.partial(scan_kernel, with_read=with_read), grid=...  26.7 us
    all_to_all x1, starting transfers between devices, send_heads(): lax.all_to_all(joined, 'seq', split_axis=0, concat_axis=0, tiled=True)  13.2 us
    all_to_all x1, starting transfers between devices, attend_by_heads(): lax.all_to_all(merged.reshape(count, tokens, -1), 'seq', split_axis=0, co...  9.79 us
    dot_general x1, matrix products, per_device(): jnp.dot(step_low, step_proj, preferred_element_type=jnp.float32)  7.07 us
    all_to_all x1, starting transfers between devices, exchange_return(): lax.all_to_all(jnp.transpose(incoming, (1, 0, 2)), 'seq', 1, 1, tiled=True)  5.99 us
    all_to_all x1, waiting for transfers between devices, attend_by_heads(): lax.all_to_all(merged.reshape(count, tokens, -1), 'seq', split_axis=0, co...  5.8 us
  transfers between devices with their start and end apart: 5, of which 4 were waited for; matrix products, arithmetic and copies ran while one was open for 11% of the time, Pallas kernels for 31%

profile of v10, /device:TPU:16, one launch (start us, length us, event | category | flops | bytes accessed | tf_op | source)
XLA Modules:
  0.0 185.7 jit_solution(1819093481209143399)
XLA Ops:
  0.6 0.0 copy-start
  0.6 1.0 slice.31
  1.7 3.8 %collective-permute-start = (bf16[3,4096]{1,0:T(4,128)(2,1)S(1)}, bf16[3,4096]{1,0:T(4,128)(2,1)S(1)}, u32[]{:S(2)}, u32[]{:S(2)}) collective-permute-start(bf16[3,4096]{1,0:T(4,128)(2,1)S(1)} %slice.31), channel_id=1, source_target_pairs={{0,1},{1,2},{2,3},{3,4},{4,5},{5,6},{6,7},{7,8},{8,9},{9,10},{10,1... | collective-permute-start | bytes 73736 | tf_op jit(solution)/shard_map/ppermute | solution.py:19
  5.5 1.6 collective-permute-done
  7.1 3.4 %shard_map.150 = bf16[32,1,128,384]{3,2,1,0:T(8,128)(2,1)} custom-call(bf16[128,4096]{1,0:T(8,128)(2,1)} %q_ref, bf16[128,1024]{1,0:T(8,128)(2,1)} %k_ref, bf16[128,1024]{1,0:T(8,128)(2,1)} %v_ref), custom_call_target="tpu_custom_call" | custom-call | tf_op jit(solution)/shard_map/pallas_call | solution.py:50
  10.5 0.0 copy-start.7
  10.5 0.0 copy-start.8
  10.5 0.0 copy-start.9
  10.6 13.2 %all-to-all-start = ((bf16[32,1,128,384]{3,2,1,0:T(8,128)(2,1)}), bf16[32,1,128,384]{3,2,1,0:T(8,128)(2,1)}, u32[]{:S(2)}, u32[]{:S(2)}) async-start(bf16[32,1,128,384]{3,2,1,0:T(8,128)(2,1)} %shard_map.150), calls=%async_computation | async-start | bytes 6291456 | tf_op jit(solution)/shard_map/all_to_all | solution.py:55
  23.8 0.0 copy-done.5
  23.8 0.1 copy.26
  23.9 0.0 copy-done.6
  23.9 0.1 copy.27
  24.0 0.0 copy-done.3
  24.0 0.0 copy-done.2
  24.0 0.7 exponential_negate_fusion.rate_ref
  24.8 0.0 copy-done
  24.8 0.0 copy-done.7
  24.8 0.0 copy-done.8
  24.8 0.0 copy-done.9
  24.8 7.1 %fusion.11 = (f32[128,4096]{1,0:T(8,128)}, f32[128,4096]{1,0:T(8,128)}, f32[4096]{0:T(1024)S(1)}, f32[128,4096]{1,0:T(8,128)}) fusion(f32[4096]{0:T(1024)S(1)} %copy-done.8, bf16[128,4096]{1,0:T(8,128)(2,1)} %param.14, f32[4096]{0:T(1024)S(1)} %bitcast.34, bf16[3,4096]{1,0:T(4,128)(2,1)S(1)} %collective-permute-done, f32[4096]{0:T(1024)S(1)} %bitcast.35, ...), kind=kOutput, calls=%fused_computation.31 | convolution fusion | flops 286257152 | bytes 9641984 | tf_op jit(solution)/shard_map/dot_general | solution.py:236
  31.9 1.3 broadcast_in_dim.15.out_ref
  33.2 1.3 broadcast_in_dim.14.in_ref
  34.5 0.7 broadcast_in_dim.17.init_ref
  35.2 10.4 %shard_map.149 = f32[16,4096]{1,0:T(8,128)} custom-call(f32[128,4096]{1,0:T(8,128)} %get-tuple-element.29.step_ref, f32[128,4096]{1,0:T(8,128)} %get-tuple-element.22.drive_ref, f32[16,4096]{1,0:T(8,128)} %exponential_negate_fusion.rate_ref, f32[128,16,128]{2,1,0:T(8,128)} %broadcast_in_dim.14.in_ref, f32[128,16,128]{2,1,0:T(8,128)} %broadcast_in_dim.15.out_ref, ...), custom_call_target="tpu_custom_call" | custom-call | tf_op jit(solution)/shard_map/pallas_call | solution.py:167
  45.6 1.0 copy_bitcast_fusion.2
  46.6 0.8 pad_maximum_fusion.2
  47.4 49.8 %all-to-all-done = bf16[32,1,128,384]{3,2,1,0:T(8,128)(2,1)} async-done(((bf16[32,1,128,384]{3,2,1,0:T(8,128)(2,1)}), bf16[32,1,128,384]{3,2,1,0:T(8,128)(2,1)}, u32[]{:S(2)}, u32[]{:S(2)}) %all-to-all-start) | async-done | bytes 3145760 | tf_op jit(solution)/shard_map/all_to_all | solution.py:55
  97.2 4.1 %all-to-all-start.1 = ((f32[17,32,128]{2,0,1:T(8,128)}), f32[17,32,128]{2,0,1:T(8,128)S(1)}, u32[]{:S(2)}, u32[]{:S(2)}) async-start(f32[17,32,128]{2,0,1:T(8,128)} %pad_maximum_fusion.2), calls=%async_computation.1 | async-start | bytes 786432 | tf_op jit(solution)/shard_map/all_to_all | solution.py:182
  101.4 0.7 constant_dynamic-slice_fusion
  102.1 9.6 %shard_map.151 = bf16[1,2048,128]{2,1,0:T(8,128)(2,1)} custom-call(bf16[1,4096,384]{2,1,0:T(8,128)(2,1)} %bitcast.5.q_ref.k_ref.v_ref, bf16[1,4096,384]{2,1,0:T(8,128)(2,1)} %bitcast.5.q_ref.k_ref.v_ref, bf16[1,4096,384]{2,1,0:T(8,128)(2,1)} %bitcast.5.q_ref.k_ref.v_ref), custom_call_target="tpu_custom_call" | custom-call | tf_op jit(solution)/shard_map/pallas_call | solution.py:105
  111.6 3.8 %all-to-all-done.1 = f32[17,32,128]{2,0,1:T(8,128)S(1)} async-done(((f32[17,32,128]{2,0,1:T(8,128)}), f32[17,32,128]{2,0,1:T(8,128)S(1)}, u32[]{:S(2)}, u32[]{:S(2)}) %all-to-all-start.1) | async-done | bytes 278560 | tf_op jit(solution)/shard_map/all_to_all | solution.py:182
  115.5 0.1 copy.29
  115.5 0.3 fusion.7
  115.9 3.0 %multiply_reduce_fusion = f32[32,16,128]{2,1,0:T(8,128)} fusion(f32[32,16,128]{2,1,0:T(8,128)S(1)} %slice_bitcast_fusion, f32[32,32,128]{2,1,0:T(8,128)S(1)} %fusion.7, f32[16,128]{1,0:T(8,128)S(1)} %constant_dynamic-slice_fusion, pred[32,32]{1,0:T(8,128)(4,1)S(1)} %get-tuple-element.31), kind=kLoop, calls=%fused_computation | loop fusion | flops 8323072 | bytes 1057792 | tf_op jit(solution)/shard_map/reduce_sum | solution.py:204
  118.9 6.0 %all-to-all-start.2 = ((f32[16,32,128]{2,0,1:T(8,128)}), f32[16,32,128]{2,0,1:T(8,128)S(1)}, u32[]{:S(2)}, u32[]{:S(2)}) async-start(f32[16,32,128]{2,0,1:T(8,128)} %bitcast.9), calls=%async_computation.2 | async-start | bytes 524288 | tf_op jit(solution)/shard_map/all_to_all | solution.py:209
  124.9 0.0 copy-start.1
  124.9 20.8 %shard_map.153 = bf16[1,2048,128]{2,1,0:T(8,128)(2,1)} custom-call(bf16[1,4096,384]{2,1,0:T(8,128)(2,1)} %bitcast.5.q_ref.k_ref.v_ref, bf16[1,4096,384]{2,1,0:T(8,128)(2,1)} %bitcast.5.q_ref.k_ref.v_ref, bf16[1,4096,384]{2,1,0:T(8,128)(2,1)} %bitcast.5.q_ref.k_ref.v_ref), custom_call_target="tpu_custom_call" | custom-call | tf_op jit(solution)/shard_map/pallas_call | solution.py:105
  145.7 0.0 copy-done.1
  145.7 2.1 %pad_maximum_fusion.1 = bf16[1,4096,128]{2,1,0:T(8,128)(2,1)} fusion(bf16[1,2048,128]{2,1,0:T(8,128)(2,1)} %shard_map.153, bf16[1,2048,128]{2,1,0:T(8,128)(2,1)S(1)} %copy-done.1), kind=kLoop, calls=%fused_computation.17 | loop fusion | flops 2097152 | bytes 2097152 | tf_op jit(solution)/shard_map/concatenate | solution.py:120
  147.7 0.0 all-to-all-done.2
  147.7 9.8 %all-to-all-start.3 = ((bf16[32,128,128]{2,1,0:T(8,128)(2,1)}), bf16[32,128,128]{2,1,0:T(8,128)(2,1)S(1)}, u32[]{:S(2)}, u32[]{:S(2)}) async-start(bf16[32,128,128]{2,1,0:T(8,128)(2,1)} %bitcast.10), calls=%async_computation.3 | async-start | bytes 2097152 | tf_op jit(solution)/shard_map/all_to_all | solution.py:122
  157.5 0.7 copy_bitcast_fusion.1.init_ref
  158.3 16.3 %shard_map.152 = f32[128,4096]{1,0:T(8,128)} custom-call(f32[128,4096]{1,0:T(8,128)} %get-tuple-element.29.step_ref, f32[128,4096]{1,0:T(8,128)} %get-tuple-element.22.drive_ref, f32[16,4096]{1,0:T(8,128)} %exponential_negate_fusion.rate_ref, f32[128,16,128]{2,1,0:T(8,128)} %broadcast_in_dim.14.in_ref, f32[128,16,128]{2,1,0:T(8,128)} %broadcast_in_dim.15.out_ref, ...), custom_call_target="tpu_custom_call" | custom-call | tf_op jit(solution)/shard_map/pallas_call | solution.py:167
  174.6 0.0 copy-done.4
  174.6 4.2 %fusion.4 = bf16[128,4096]{1,0:T(8,128)(2,1)} fusion(bf16[128,4096]{1,0:T(8,128)(2,1)} %param.15, f32[128,4096]{1,0:T(8,128)} %shard_map.152, f32[128,4096]{1,0:T(8,128)} %get-tuple-element.23, f32[4096]{0:T(1024)S(1)} %copy-done.4), kind=kLoop, calls=%fused_computation.10 | loop fusion | flops 4718592 | bytes 6307840 | tf_op jit(solution)/shard_map/convert_element_type | solution.py:260
  178.8 5.8 %all-to-all-done.3 = bf16[32,128,128]{2,1,0:T(8,128)(2,1)S(1)} async-done(((bf16[32,128,128]{2,1,0:T(8,128)(2,1)}), bf16[32,128,128]{2,1,0:T(8,128)(2,1)S(1)}, u32[]{:S(2)}, u32[]{:S(2)}) %all-to-all-start.3) | async-done | bytes 1048608 | tf_op jit(solution)/shard_map/all_to_all | solution.py:122
  184.6 1.1 copy_bitcast_fusion
  (8 shorter events, 0.1 us)
Async XLA Ops:
  0.6 24.2 %copy-start = (bf16[256,4096]{1,0:T(8,128)(2,1)S(1)}, bf16[256,4096]{1,0:T(8,128)(2,1)}, u32[]{:S(2)}) copy-start(bf16[256,4096]{1,0:T(8,128)(2,1)} %param.19) | copy-start | bytes 6291460
  1.7 5.4 %collective-permute-start = (bf16[3,4096]{1,0:T(4,128)(2,1)S(1)}, bf16[3,4096]{1,0:T(4,128)(2,1)S(1)}, u32[]{:S(2)}, u32[]{:S(2)}) collective-permute-start(bf16[3,4096]{1,0:T(4,128)(2,1)S(1)} %slice.31), channel_id=1, source_target_pairs={{0,1},{1,2},{2,3},{3,4},{4,5},{5,6},{6,7},{7,8},{8,9},{9,10},{10,1... | collective-permute-start | bytes 73736 | tf_op jit(solution)/shard_map/ppermute | solution.py:19
  10.5 13.2 %copy-start.5 = (f32[128,16]{0,1:T(8,128)S(1)}, f32[128,16]{0,1:T(8,128)}, u32[]{:S(2)}) copy-start(f32[128,16]{0,1:T(8,128)} %param.22) | copy-start | bytes 24580
  10.5 13.3 %copy-start.6 = (f32[128,16]{0,1:T(8,128)S(1)}, f32[128,16]{0,1:T(8,128)}, u32[]{:S(2)}) copy-start(f32[128,16]{0,1:T(8,128)} %param.23) | copy-start | bytes 24580
  10.5 13.5 %copy-start.3 = (f32[4,4096]{1,0:T(4,128)S(1)}, f32[4,4096]{1,0:T(4,128)}, u32[]{:S(2)}) copy-start(f32[4,4096]{1,0:T(4,128)} %param.16) | copy-start | bytes 196612
  10.5 13.5 %copy-start.2 = (f32[16,4096]{1,0:T(8,128)S(1)}, f32[16,4096]{1,0:T(8,128)}, u32[]{:S(2)}) copy-start(f32[16,4096]{1,0:T(8,128)} %param.21) | copy-start | bytes 786436
  10.5 14.3 %copy-start.7 = (bf16[128,256]{1,0:T(8,128)(2,1)S(1)}, bf16[128,256]{1,0:T(8,128)(2,1)}, u32[]{:S(2)}) copy-start(bf16[128,256]{1,0:T(8,128)(2,1)} %param.18) | copy-start | bytes 196612
  10.5 14.3 %copy-start.8 = (f32[4096]{0:T(1024)S(1)}, f32[4096]{0:T(1024)}, u32[]{:S(2)}) copy-start(f32[4096]{0:T(1024)} %param.17) | copy-start | bytes 49156
  10.5 14.2 %copy-start.9 = (f32[4096]{0:T(1024)S(1)}, f32[4096]{0:T(1024)}, u32[]{:S(2)}) copy-start(f32[4096]{0:T(1024)} %param.20) | copy-start | bytes 49156
  10.6 86.6 %all-to-all-start = ((bf16[32,1,128,384]{3,2,1,0:T(8,128)(2,1)}), bf16[32,1,128,384]{3,2,1,0:T(8,128)(2,1)}, u32[]{:S(2)}, u32[]{:S(2)}) async-start(bf16[32,1,128,384]{3,2,1,0:T(8,128)(2,1)} %shard_map.150), calls=%async_computation | async-start | bytes 6291456 | tf_op jit(solution)/shard_map/all_to_all | solution.py:55
  97.2 18.2 %all-to-all-start.1 = ((f32[17,32,128]{2,0,1:T(8,128)}), f32[17,32,128]{2,0,1:T(8,128)S(1)}, u32[]{:S(2)}, u32[]{:S(2)}) async-start(f32[17,32,128]{2,0,1:T(8,128)} %pad_maximum_fusion.2), calls=%async_computation.1 | async-start | bytes 786432 | tf_op jit(solution)/shard_map/all_to_all | solution.py:182
  118.9 28.8 %all-to-all-start.2 = ((f32[16,32,128]{2,0,1:T(8,128)}), f32[16,32,128]{2,0,1:T(8,128)S(1)}, u32[]{:S(2)}, u32[]{:S(2)}) async-start(f32[16,32,128]{2,0,1:T(8,128)} %bitcast.9), calls=%async_computation.2 | async-start | bytes 524288 | tf_op jit(solution)/shard_map/all_to_all | solution.py:209
  124.9 20.8 %copy-start.1 = (bf16[1,2048,128]{2,1,0:T(8,128)(2,1)S(1)}, bf16[1,2048,128]{2,1,0:T(8,128)(2,1)}, u32[]{:S(2)}) copy-start(bf16[1,2048,128]{2,1,0:T(8,128)(2,1)} %shard_map.151) | copy-start | bytes 1572868
  147.7 36.8 %all-to-all-start.3 = ((bf16[32,128,128]{2,1,0:T(8,128)(2,1)}), bf16[32,128,128]{2,1,0:T(8,128)(2,1)S(1)}, u32[]{:S(2)}, u32[]{:S(2)}) async-start(bf16[32,128,128]{2,1,0:T(8,128)(2,1)} %bitcast.10), calls=%async_computation.3 | async-start | bytes 2097152 | tf_op jit(solution)/shard_map/all_to_all | solution.py:122
  158.3 16.3 %copy-start.4 = (f32[4096]{0:T(1024)S(1)}, f32[4096]{0:T(1024)}, u32[]{:S(2)}) copy-start(f32[4096]{0:T(1024)} %param.24) | copy-start | bytes 49156

commit v11 on v10

--- a/solution.py
+++ b/solution.py
@@ -114,7 +114,7 @@
 
 def attend_by_heads(joined, tokens, midway):
     length = joined.shape[1]
-    blocks = length // math.gcd(length, 512)
+    blocks = length // math.gcd(length, 1024)
     early, joined = midway(attend_heads(joined, 0, blocks), joined)
     late = attend_heads(joined, blocks // 2, blocks)
     merged = jnp.transpose(jnp.concatenate([early, late], 1), (1, 0, 2))

time: 187 us -> 183 us (0.979)
  Pallas kernels: 60.5 us -> 56.3 us
    pallas_call x2, Pallas kernels: 30.3 us -> 26.2 us  [attend_heads(): pl.pallas_call(functools.partial(attention_kernel, tile=tile, scale=HEAD_...]
  transfers between devices with their start and end apart: 5 -> 5, of which waited for: 4 -> 4; matrix products, arithmetic and copies ran while one was open for 11% -> 11% of each run, Pallas kernels for 31% -> 29%
where the time goes in v11:
time: 183 us; the launch traced here: 182 us
  waiting for transfers between devices  62 us (34%)
  Pallas kernels  56.3 us (31%)
  starting transfers between devices  36.1 us (20%)
  other arithmetic  10.8 us (6%)
  local copies, waits for them, and re-layouts  8.26 us (5%)
  matrix products  7.42 us (4%)
    all_to_all x1, waiting for transfers between devices, send_heads(): lax.all_to_all(joined, 'seq', split_axis=0, concat_axis=0, tiled=True)  49.8 us
    pallas_call x2, Pallas kernels, run_scan(): pl.pallas_call(functools.partial(scan_kernel, with_read=with_read), grid=...  26.7 us
    pallas_call x2, Pallas kernels, attend_heads(): pl.pallas_call(functools.partial(attention_kernel, tile=tile, scale=HEAD_...  26.2 us
    all_to_all x1, starting transfers between devices, send_heads(): lax.all_to_all(joined, 'seq', split_axis=0, concat_axis=0, tiled=True)  13.2 us
    all_to_all x1, starting transfers between devices, attend_by_heads(): lax.all_to_all(merged.reshape(count, tokens, -1), 'seq', split_axis=0, co...  9.63 us
    dot_general x1, matrix products, per_device(): jnp.dot(step_low, step_proj, preferred_element_type=jnp.float32)  7.07 us
    all_to_all x1, waiting for transfers between devices, attend_by_heads(): lax.all_to_all(merged.reshape(count, tokens, -1), 'seq', split_axis=0, co...  5.79 us
    all_to_all x1, starting transfers between devices, exchange_return(): lax.all_to_all(jnp.transpose(incoming, (1, 0, 2)), 'seq', 1, 1, tiled=True)  5.38 us
  transfers between devices with their start and end apart: 5, of which 4 were waited for; matrix products, arithmetic and copies ran while one was open for 11% of the time, Pallas kernels for 29%

profile of v11, /device:TPU:16, one launch (start us, length us, event | category | flops | bytes accessed | tf_op | source)
XLA Modules:
  0.0 181.8 jit_solution(2683127291091846397)
XLA Ops:
  0.6 0.0 copy-start
  0.6 1.0 slice.31
  1.7 3.8 %collective-permute-start = (bf16[3,4096]{1,0:T(4,128)(2,1)S(1)}, bf16[3,4096]{1,0:T(4,128)(2,1)S(1)}, u32[]{:S(2)}, u32[]{:S(2)}) collective-permute-start(bf16[3,4096]{1,0:T(4,128)(2,1)S(1)} %slice.31), channel_id=1, source_target_pairs={{0,1},{1,2},{2,3},{3,4},{4,5},{5,6},{6,7},{7,8},{8,9},{9,10},{10,1... | collective-permute-start | bytes 73736 | tf_op jit(solution)/shard_map/ppermute | solution.py:19
  5.5 1.6 collective-permute-done
  7.1 3.4 %shard_map.150 = bf16[32,1,128,384]{3,2,1,0:T(8,128)(2,1)} custom-call(bf16[128,4096]{1,0:T(8,128)(2,1)} %q_ref, bf16[128,1024]{1,0:T(8,128)(2,1)} %k_ref, bf16[128,1024]{1,0:T(8,128)(2,1)} %v_ref), custom_call_target="tpu_custom_call" | custom-call | tf_op jit(solution)/shard_map/pallas_call | solution.py:50
  10.5 0.0 copy-start.7
  10.5 0.0 copy-start.8
  10.5 0.0 copy-start.9
  10.6 13.2 %all-to-all-start = ((bf16[32,1,128,384]{3,2,1,0:T(8,128)(2,1)}), bf16[32,1,128,384]{3,2,1,0:T(8,128)(2,1)}, u32[]{:S(2)}, u32[]{:S(2)}) async-start(bf16[32,1,128,384]{3,2,1,0:T(8,128)(2,1)} %shard_map.150), calls=%async_computation | async-start | bytes 6291456 | tf_op jit(solution)/shard_map/all_to_all | solution.py:55
  23.8 0.0 copy-done.5
  23.8 0.1 copy.26
  23.9 0.0 copy-done.6
  23.9 0.1 copy.27
  24.0 0.0 copy-done.3
  24.0 0.0 copy-done.2
  24.0 0.7 exponential_negate_fusion.rate_ref
  24.8 0.0 copy-done
  24.8 0.0 copy-done.7
  24.8 0.0 copy-done.8
  24.8 0.0 copy-done.9
  24.8 7.1 %fusion.11 = (f32[128,4096]{1,0:T(8,128)}, f32[128,4096]{1,0:T(8,128)}, f32[4096]{0:T(1024)S(1)}, f32[128,4096]{1,0:T(8,128)}) fusion(f32[4096]{0:T(1024)S(1)} %copy-done.8, bf16[128,4096]{1,0:T(8,128)(2,1)} %param.14, f32[4096]{0:T(1024)S(1)} %bitcast.34, bf16[3,4096]{1,0:T(4,128)(2,1)S(1)} %collective-permute-done, f32[4096]{0:T(1024)S(1)} %bitcast.35, ...), kind=kOutput, calls=%fused_computation.31 | convolution fusion | flops 286257152 | bytes 9641984 | tf_op jit(solution)/shard_map/dot_general | solution.py:236
  31.9 1.3 broadcast_in_dim.15.out_ref
  33.2 1.3 broadcast_in_dim.14.in_ref
  34.5 0.7 broadcast_in_dim.17.init_ref
  35.2 10.4 %shard_map.149 = f32[16,4096]{1,0:T(8,128)} custom-call(f32[128,4096]{1,0:T(8,128)} %get-tuple-element.29.step_ref, f32[128,4096]{1,0:T(8,128)} %get-tuple-element.22.drive_ref, f32[16,4096]{1,0:T(8,128)} %exponential_negate_fusion.rate_ref, f32[128,16,128]{2,1,0:T(8,128)} %broadcast_in_dim.14.in_ref, f32[128,16,128]{2,1,0:T(8,128)} %broadcast_in_dim.15.out_ref, ...), custom_call_target="tpu_custom_call" | custom-call | tf_op jit(solution)/shard_map/pallas_call | solution.py:167
  45.6 1.0 copy_bitcast_fusion.2
  46.6 0.8 pad_maximum_fusion.2
  47.4 49.8 %all-to-all-done = bf16[32,1,128,384]{3,2,1,0:T(8,128)(2,1)} async-done(((bf16[32,1,128,384]{3,2,1,0:T(8,128)(2,1)}), bf16[32,1,128,384]{3,2,1,0:T(8,128)(2,1)}, u32[]{:S(2)}, u32[]{:S(2)}) %all-to-all-start) | async-done | bytes 3145760 | tf_op jit(solution)/shard_map/all_to_all | solution.py:55
  97.2 4.1 %all-to-all-start.1 = ((f32[17,32,128]{2,0,1:T(8,128)}), f32[17,32,128]{2,0,1:T(8,128)S(1)}, u32[]{:S(2)}, u32[]{:S(2)}) async-start(f32[17,32,128]{2,0,1:T(8,128)} %pad_maximum_fusion.2), calls=%async_computation.1 | async-start | bytes 786432 | tf_op jit(solution)/shard_map/all_to_all | solution.py:182
  101.4 0.7 constant_dynamic-slice_fusion
  102.1 8.5 %shard_map.151 = bf16[1,2048,128]{2,1,0:T(8,128)(2,1)} custom-call(bf16[1,4096,384]{2,1,0:T(8,128)(2,1)} %bitcast.5.q_ref.k_ref.v_ref, bf16[1,4096,384]{2,1,0:T(8,128)(2,1)} %bitcast.5.q_ref.k_ref.v_ref, bf16[1,4096,384]{2,1,0:T(8,128)(2,1)} %bitcast.5.q_ref.k_ref.v_ref), custom_call_target="tpu_custom_call" | custom-call | tf_op jit(solution)/shard_map/pallas_call | solution.py:105
  110.6 4.8 %all-to-all-done.1 = f32[17,32,128]{2,0,1:T(8,128)S(1)} async-done(((f32[17,32,128]{2,0,1:T(8,128)}), f32[17,32,128]{2,0,1:T(8,128)S(1)}, u32[]{:S(2)}, u32[]{:S(2)}) %all-to-all-start.1) | async-done | bytes 278560 | tf_op jit(solution)/shard_map/all_to_all | solution.py:182
  115.5 0.1 copy.29
  115.5 0.3 fusion.7
  115.9 3.0 %multiply_reduce_fusion = f32[32,16,128]{2,1,0:T(8,128)} fusion(f32[32,16,128]{2,1,0:T(8,128)S(1)} %slice_bitcast_fusion, f32[32,32,128]{2,1,0:T(8,128)S(1)} %fusion.7, f32[16,128]{1,0:T(8,128)S(1)} %constant_dynamic-slice_fusion, pred[32,32]{1,0:T(8,128)(4,1)S(1)} %get-tuple-element.31), kind=kLoop, calls=%fused_computation | loop fusion | flops 8323072 | bytes 1057792 | tf_op jit(solution)/shard_map/reduce_sum | solution.py:204
  118.9 5.4 %all-to-all-start.2 = ((f32[16,32,128]{2,0,1:T(8,128)}), f32[16,32,128]{2,0,1:T(8,128)S(1)}, u32[]{:S(2)}, u32[]{:S(2)}) async-start(f32[16,32,128]{2,0,1:T(8,128)} %bitcast.9), calls=%async_computation.2 | async-start | bytes 524288 | tf_op jit(solution)/shard_map/all_to_all | solution.py:209
  124.3 0.0 copy-start.1
  124.3 17.6 %shard_map.153 = bf16[1,2048,128]{2,1,0:T(8,128)(2,1)} custom-call(bf16[1,4096,384]{2,1,0:T(8,128)(2,1)} %bitcast.5.q_ref.k_ref.v_ref, bf16[1,4096,384]{2,1,0:T(8,128)(2,1)} %bitcast.5.q_ref.k_ref.v_ref, bf16[1,4096,384]{2,1,0:T(8,128)(2,1)} %bitcast.5.q_ref.k_ref.v_ref), custom_call_target="tpu_custom_call" | custom-call | tf_op jit(solution)/shard_map/pallas_call | solution.py:105
  141.9 0.0 copy-done.1
  141.9 2.1 %pad_maximum_fusion.1 = bf16[1,4096,128]{2,1,0:T(8,128)(2,1)} fusion(bf16[1,2048,128]{2,1,0:T(8,128)(2,1)} %shard_map.153, bf16[1,2048,128]{2,1,0:T(8,128)(2,1)S(1)} %copy-done.1), kind=kLoop, calls=%fused_computation.17 | loop fusion | flops 2097152 | bytes 2097152 | tf_op jit(solution)/shard_map/concatenate | solution.py:120
  144.0 0.0 all-to-all-done.2
  144.0 9.6 %all-to-all-start.3 = ((bf16[32,128,128]{2,1,0:T(8,128)(2,1)}), bf16[32,128,128]{2,1,0:T(8,128)(2,1)S(1)}, u32[]{:S(2)}, u32[]{:S(2)}) async-start(bf16[32,128,128]{2,1,0:T(8,128)(2,1)} %bitcast.10), calls=%async_computation.3 | async-start | bytes 2097152 | tf_op jit(solution)/shard_map/all_to_all | solution.py:122
  153.7 0.7 copy_bitcast_fusion.1.init_ref
  154.4 16.3 %shard_map.152 = f32[128,4096]{1,0:T(8,128)} custom-call(f32[128,4096]{1,0:T(8,128)} %get-tuple-element.29.step_ref, f32[128,4096]{1,0:T(8,128)} %get-tuple-element.22.drive_ref, f32[16,4096]{1,0:T(8,128)} %exponential_negate_fusion.rate_ref, f32[128,16,128]{2,1,0:T(8,128)} %broadcast_in_dim.14.in_ref, f32[128,16,128]{2,1,0:T(8,128)} %broadcast_in_dim.15.out_ref, ...), custom_call_target="tpu_custom_call" | custom-call | tf_op jit(solution)/shard_map/pallas_call | solution.py:167
  170.7 0.0 copy-done.4
  170.7 4.2 %fusion.4 = bf16[128,4096]{1,0:T(8,128)(2,1)} fusion(bf16[128,4096]{1,0:T(8,128)(2,1)} %param.15, f32[128,4096]{1,0:T(8,128)} %shard_map.152, f32[128,4096]{1,0:T(8,128)} %get-tuple-element.23, f32[4096]{0:T(1024)S(1)} %copy-done.4), kind=kLoop, calls=%fused_computation.10 | loop fusion | flops 4718592 | bytes 6307840 | tf_op jit(solution)/shard_map/convert_element_type | solution.py:260
  174.9 5.8 %all-to-all-done.3 = bf16[32,128,128]{2,1,0:T(8,128)(2,1)S(1)} async-done(((bf16[32,128,128]{2,1,0:T(8,128)(2,1)}), bf16[32,128,128]{2,1,0:T(8,128)(2,1)S(1)}, u32[]{:S(2)}, u32[]{:S(2)}) %all-to-all-start.3) | async-done | bytes 1048608 | tf_op jit(solution)/shard_map/all_to_all | solution.py:122
  180.7 1.1 copy_bitcast_fusion
  (8 shorter events, 0.1 us)
Async XLA Ops:
  0.6 24.2 %copy-start = (bf16[256,4096]{1,0:T(8,128)(2,1)S(1)}, bf16[256,4096]{1,0:T(8,128)(2,1)}, u32[]{:S(2)}) copy-start(bf16[256,4096]{1,0:T(8,128)(2,1)} %param.19) | copy-start | bytes 6291460
  1.7 5.4 %collective-permute-start = (bf16[3,4096]{1,0:T(4,128)(2,1)S(1)}, bf16[3,4096]{1,0:T(4,128)(2,1)S(1)}, u32[]{:S(2)}, u32[]{:S(2)}) collective-permute-start(bf16[3,4096]{1,0:T(4,128)(2,1)S(1)} %slice.31), channel_id=1, source_target_pairs={{0,1},{1,2},{2,3},{3,4},{4,5},{5,6},{6,7},{7,8},{8,9},{9,10},{10,1... | collective-permute-start | bytes 73736 | tf_op jit(solution)/shard_map/ppermute | solution.py:19
  10.5 13.2 %copy-start.5 = (f32[128,16]{0,1:T(8,128)S(1)}, f32[128,16]{0,1:T(8,128)}, u32[]{:S(2)}) copy-start(f32[128,16]{0,1:T(8,128)} %param.22) | copy-start | bytes 24580
  10.5 13.3 %copy-start.6 = (f32[128,16]{0,1:T(8,128)S(1)}, f32[128,16]{0,1:T(8,128)}, u32[]{:S(2)}) copy-start(f32[128,16]{0,1:T(8,128)} %param.23) | copy-start | bytes 24580
  10.5 13.5 %copy-start.3 = (f32[4,4096]{1,0:T(4,128)S(1)}, f32[4,4096]{1,0:T(4,128)}, u32[]{:S(2)}) copy-start(f32[4,4096]{1,0:T(4,128)} %param.16) | copy-start | bytes 196612
  10.5 13.5 %copy-start.2 = (f32[16,4096]{1,0:T(8,128)S(1)}, f32[16,4096]{1,0:T(8,128)}, u32[]{:S(2)}) copy-start(f32[16,4096]{1,0:T(8,128)} %param.21) | copy-start | bytes 786436
  10.5 14.3 %copy-start.7 = (bf16[128,256]{1,0:T(8,128)(2,1)S(1)}, bf16[128,256]{1,0:T(8,128)(2,1)}, u32[]{:S(2)}) copy-start(bf16[128,256]{1,0:T(8,128)(2,1)} %param.18) | copy-start | bytes 196612
  10.5 14.3 %copy-start.8 = (f32[4096]{0:T(1024)S(1)}, f32[4096]{0:T(1024)}, u32[]{:S(2)}) copy-start(f32[4096]{0:T(1024)} %param.17) | copy-start | bytes 49156
  10.5 14.2 %copy-start.9 = (f32[4096]{0:T(1024)S(1)}, f32[4096]{0:T(1024)}, u32[]{:S(2)}) copy-start(f32[4096]{0:T(1024)} %param.20) | copy-start | bytes 49156
  10.6 86.6 %all-to-all-start = ((bf16[32,1,128,384]{3,2,1,0:T(8,128)(2,1)}), bf16[32,1,128,384]{3,2,1,0:T(8,128)(2,1)}, u32[]{:S(2)}, u32[]{:S(2)}) async-start(bf16[32,1,128,384]{3,2,1,0:T(8,128)(2,1)} %shard_map.150), calls=%async_computation | async-start | bytes 6291456 | tf_op jit(solution)/shard_map/all_to_all | solution.py:55
  97.2 18.2 %all-to-all-start.1 = ((f32[17,32,128]{2,0,1:T(8,128)}), f32[17,32,128]{2,0,1:T(8,128)S(1)}, u32[]{:S(2)}, u32[]{:S(2)}) async-start(f32[17,32,128]{2,0,1:T(8,128)} %pad_maximum_fusion.2), calls=%async_computation.1 | async-start | bytes 786432 | tf_op jit(solution)/shard_map/all_to_all | solution.py:182
  118.9 25.1 %all-to-all-start.2 = ((f32[16,32,128]{2,0,1:T(8,128)}), f32[16,32,128]{2,0,1:T(8,128)S(1)}, u32[]{:S(2)}, u32[]{:S(2)}) async-start(f32[16,32,128]{2,0,1:T(8,128)} %bitcast.9), calls=%async_computation.2 | async-start | bytes 524288 | tf_op jit(solution)/shard_map/all_to_all | solution.py:209
  124.3 17.7 %copy-start.1 = (bf16[1,2048,128]{2,1,0:T(8,128)(2,1)S(1)}, bf16[1,2048,128]{2,1,0:T(8,128)(2,1)}, u32[]{:S(2)}) copy-start(bf16[1,2048,128]{2,1,0:T(8,128)(2,1)} %shard_map.151) | copy-start | bytes 1572868
  144.0 36.7 %all-to-all-start.3 = ((bf16[32,128,128]{2,1,0:T(8,128)(2,1)}), bf16[32,128,128]{2,1,0:T(8,128)(2,1)S(1)}, u32[]{:S(2)}, u32[]{:S(2)}) async-start(bf16[32,128,128]{2,1,0:T(8,128)(2,1)} %bitcast.10), calls=%async_computation.3 | async-start | bytes 2097152 | tf_op jit(solution)/shard_map/all_to_all | solution.py:122
  154.4 16.3 %copy-start.4 = (f32[4096]{0:T(1024)S(1)}, f32[4096]{0:T(1024)}, u32[]{:S(2)}) copy-start(f32[4096]{0:T(1024)} %param.24) | copy-start | bytes 49156
